TPU v7x, 512 devices: a whole 4x4x16 slice. The times are simulated.
512 devices in a mesh: ctx: 64 (over z, y), tp: 8 (over x, core).
Axes of the slice: x: 4, y: 4, z: 16, core: 2. Of those that a mesh axis runs over, the one named last changes fastest.
Arguments:
- features: bfloat16 [3, 4096, 8192], P(None, 'ctx', 'tp'), may hold values from -6 to 6
- short_weight: float32 [3, 3, 8192], P(None, None, 'tp'), may hold values from -3 to 3
- decay_rate: float32 [512, 16], P('tp'), may hold values from 0.00012207031 to 0.03
- residue: float32 [512, 16], P('tp'), may hold values from -3 to 3
- skip_gain: float32 [8192], P('tp'), may hold values from -1 to 1
- out_weight: bfloat16 [8192, 4096], P('tp', 'ctx'), may hold values from -0.1875 to 0.1875
Outputs:
- mixed_out: bfloat16 [4096, 4096], P('ctx', 'tp')
All inputs are finite; a program needn't handle non-finite values.
Results may differ from a plain program's by a relative error of at most 0.006.
Values may be sent and summed in bfloat16 or wider, within the bound.
No kernel may reach another device: no remote copies, remote signals or barrier semaphores. Data moves between devices by JAX's collectives and lax.ppermute only.
A program may use at most 128 MiB of HBM per device.

v0:
```python
import math

import jax
import jax.numpy as jnp
from jax import lax
from jax.sharding import PartitionSpec as P


def passed_along(shard, axis, by):
    length = lax.axis_size(axis)
    pairs = [(i, i + by) for i in range(length) if 0 <= i + by < length]
    return lax.ppermute(shard, axis, pairs)


def entering(value, axis, join, neutral):
    count, mine = (lax.axis_size(axis), lax.axis_index(axis))
    pieces = jax.tree.map(lambda part: lax.all_gather(part, axis), value)
    running = jax.tree.map(
        lambda part, zero: jnp.full_like(part, 0) + jnp.asarray(zero, part.dtype), value, neutral
    )

    def hop(position, running):
        longer = join(running, jax.tree.map(lambda part: part[position], pieces))
        return jax.tree.map(lambda new, old: jnp.where(position < mine, new, old), longer, running)

    return lax.fori_loop(0, count - 1, hop, running)


def combine_states(earlier, later):
    return (earlier[0] * later[0], later[1] + later[0][:, None, :] * earlier[1])


def per_device(features, short_weight, decay_rate, residue, skip_gain, out_weight):
    hi = lax.Precision.HIGHEST
    rows = features.shape[1]
    chans = features.shape[2]
    groups = decay_rate.shape[0]
    modes = decay_rate.shape[1]
    width = chans // groups
    taps = short_weight.shape[1]
    rim = passed_along(features[:, rows - (taps - 1) :, :], "ctx", 1)
    extended = jnp.concatenate([rim, features], axis=1)
    conv = jnp.zeros(features.shape, jnp.float32)
    for j in range(taps):
        conv = conv + short_weight[:, j][:, None, :] * extended[
            :, taps - 1 - j : taps - 1 - j + rows, :
        ].astype(jnp.float32)
    q_lane = conv[0]
    gated = (conv[1] * conv[2]).astype(jnp.bfloat16)
    coef = residue * jnp.sqrt(-jnp.expm1(-2.0 * decay_rate))
    lags = jnp.arange(rows, dtype=jnp.float32)
    near_filter = jnp.sum(
        coef[:, :, None] * jnp.exp(-decay_rate[:, :, None] * lags[None, None, :]), axis=1
    ).astype(jnp.bfloat16)
    index = jnp.arange(rows, dtype=jnp.int32)
    offset = index[:, None] - index[None, :]
    lower = offset >= 0
    clipped = jnp.clip(offset, 0, rows - 1)
    gstep = math.gcd(groups, 8)
    nblock = groups // gstep
    filter_blocks = near_filter.reshape(nblock, gstep, rows)
    input_blocks = gated.reshape(rows, nblock, gstep, width).transpose(1, 0, 2, 3)

    def near_block(pair):
        taps_here, inputs_here = pair
        toeplitz = jnp.where(lower[None], taps_here[:, clipped], jnp.zeros((), jnp.bfloat16))
        return jnp.einsum("gts,sgw->tgw", toeplitz, inputs_here, preferred_element_type=jnp.float32)

    near = (
        lax.map(near_block, (filter_blocks, input_blocks))
        .transpose(1, 0, 2, 3)
        .reshape(rows, chans)
    )
    gated_wide = gated.astype(jnp.float32)
    grouped = gated_wide.reshape(rows, groups, width)
    end_basis = jnp.exp(-decay_rate[None] * (rows - 1.0 - lags)[:, None, None])
    own_state = jnp.einsum("tgs,tgw->gws", end_basis, grouped, precision=hi)
    block_decay = jnp.exp(-decay_rate * rows)
    identity = (
        jnp.ones((groups, modes), jnp.float32),
        jnp.zeros((groups, width, modes), jnp.float32),
    )
    incoming = entering((block_decay, own_state), "ctx", combine_states, identity)[1]
    far_basis = coef[None] * jnp.exp(-decay_rate[None] * (lags + 1.0)[:, None, None])
    far = jnp.einsum("tgs,gws->tgw", far_basis, incoming, precision=hi).reshape(rows, chans)
    mixed = (q_lane * (near + far + skip_gain[None, :] * gated_wide)).astype(jnp.bfloat16)
    partial_out = jnp.dot(
        mixed,
        lax.all_gather(out_weight, "ctx", axis=1, tiled=True),
        preferred_element_type=jnp.float32,
    )
    return lax.psum_scatter(partial_out, "tp", scatter_dimension=1, tiled=True).astype(jnp.bfloat16)


def solution(mesh):
    placed = (
        P(None, "ctx", "tp"),
        P(None, None, "tp"),
        P("tp", None),
        P("tp", None),
        P("tp"),
        P("tp", "ctx"),
    )
    return jax.shard_map(
        per_device, mesh=mesh, in_specs=placed, out_specs=P("ctx", "tp"), check_vma=False
    )
```

profile of v0, /device:TPU:16, one launch (start us, length us, event | category | flops | bytes accessed | tf_op | source)
XLA Modules:
  0.0 521.4 jit_solution(11579085921228791961)
XLA Ops:
  7.4 3.2 collective-permute-start
  12.3 1.4 copy.41
  14.2 2.2 multiply_add_fusion
  16.4 1.4 fusion.23
  18.7 114.5 %all-gather.2 = f32[64,64,16]{1,2,0:T(8,128)} all-gather(f32[1,64,16]{1,2,0:T(8,128)S(1)} %get-tuple-element.216), channel_id=3, replica_groups=mesh['ctx'=64,'tp'=8] {'ctx'}, dimensions={0}, use_global_device_ids=true | all-gather | bytes 266240 | tf_op jit(solution)/shard_map/all_gather | solution.py:17
  133.7 108.6 %while.25 = (s32[]{:T(128)}, f32[8,64,8,16]{1,3,2,0:T(8,128)}, bf16[8,64,8,16]{1,3,2,0:T(8,128)(2,1)S(1)}, bf16[8,8,64]{2,1,0:T(8,128)(2,1)S(1)}, s32[]{:T(128)}) while((s32[]{:T(128)}, f32[8,64,8,16]{1,3,2,0:T(8,128)}, bf16[8,64,8,16]{1,3,2,0:T(8,128)(2,1)S(1)}, bf16[8,8,64]{2,1,0:T(8,128)(2,1)S(1)}, s32[]{:T(128)}) %tuple.73), condition=%wide.region_2.3_spmd.clone, body=%wide.region_1.2_spmd.clone.sunk | while | flops 1114114 | bytes 607297 | solution.py:70
  133.9 12.1 %gather_fusion = bf16[4096,8]{1,0:T(8,128)(2,1)S(1)} fusion(bf16[8,64]{0,1:T(8,128)(2,1)S(1)} %bitcast.80, s32[4096]{0:T(1024)S(1)} %broadcast_clamp_fusion.2), kind=kCustom, calls=%fused_computation.clone.clone.1 | custom fusion | bytes 147456 | tf_op jit(solution)/shard_map/while/body/eval_jaxpr/gather | solution.py:66
  147.5 12.1 %gather_fusion = bf16[4096,8]{1,0:T(8,128)(2,1)S(1)} fusion(bf16[8,64]{0,1:T(8,128)(2,1)S(1)} %bitcast.80, s32[4096]{0:T(1024)S(1)} %broadcast_clamp_fusion.2), kind=kCustom, calls=%fused_computation.clone.clone.1 | custom fusion | bytes 147456 | tf_op jit(solution)/shard_map/while/body/eval_jaxpr/gather | solution.py:66
  161.0 12.1 %gather_fusion = bf16[4096,8]{1,0:T(8,128)(2,1)S(1)} fusion(bf16[8,64]{0,1:T(8,128)(2,1)S(1)} %bitcast.80, s32[4096]{0:T(1024)S(1)} %broadcast_clamp_fusion.2), kind=kCustom, calls=%fused_computation.clone.clone.1 | custom fusion | bytes 147456 | tf_op jit(solution)/shard_map/while/body/eval_jaxpr/gather | solution.py:66
  174.6 12.1 %gather_fusion = bf16[4096,8]{1,0:T(8,128)(2,1)S(1)} fusion(bf16[8,64]{0,1:T(8,128)(2,1)S(1)} %bitcast.80, s32[4096]{0:T(1024)S(1)} %broadcast_clamp_fusion.2), kind=kCustom, calls=%fused_computation.clone.clone.1 | custom fusion | bytes 147456 | tf_op jit(solution)/shard_map/while/body/eval_jaxpr/gather | solution.py:66
  188.2 12.1 %gather_fusion = bf16[4096,8]{1,0:T(8,128)(2,1)S(1)} fusion(bf16[8,64]{0,1:T(8,128)(2,1)S(1)} %bitcast.80, s32[4096]{0:T(1024)S(1)} %broadcast_clamp_fusion.2), kind=kCustom, calls=%fused_computation.clone.clone.1 | custom fusion | bytes 147456 | tf_op jit(solution)/shard_map/while/body/eval_jaxpr/gather | solution.py:66
  201.7 12.1 %gather_fusion = bf16[4096,8]{1,0:T(8,128)(2,1)S(1)} fusion(bf16[8,64]{0,1:T(8,128)(2,1)S(1)} %bitcast.80, s32[4096]{0:T(1024)S(1)} %broadcast_clamp_fusion.2), kind=kCustom, calls=%fused_computation.clone.clone.1 | custom fusion | bytes 147456 | tf_op jit(solution)/shard_map/while/body/eval_jaxpr/gather | solution.py:66
  215.3 12.1 %gather_fusion = bf16[4096,8]{1,0:T(8,128)(2,1)S(1)} fusion(bf16[8,64]{0,1:T(8,128)(2,1)S(1)} %bitcast.80, s32[4096]{0:T(1024)S(1)} %broadcast_clamp_fusion.2), kind=kCustom, calls=%fused_computation.clone.clone.1 | custom fusion | bytes 147456 | tf_op jit(solution)/shard_map/while/body/eval_jaxpr/gather | solution.py:66
  228.9 12.1 %gather_fusion = bf16[4096,8]{1,0:T(8,128)(2,1)S(1)} fusion(bf16[8,64]{0,1:T(8,128)(2,1)S(1)} %bitcast.80, s32[4096]{0:T(1024)S(1)} %broadcast_clamp_fusion.2), kind=kCustom, calls=%fused_computation.clone.clone.1 | custom fusion | bytes 147456 | tf_op jit(solution)/shard_map/while/body/eval_jaxpr/gather | solution.py:66
  242.3 71.9 %all-gather.8.cloned.1.call-done = f32[4096,16,16]{2,1,0:T(8,128)} async-done(((f32[64,16,16]{2,1,0:T(8,128)}), f32[4096,16,16]{2,1,0:T(8,128)}) %all-gather.8.cloned.1.call-update) | async-done | bytes 4194320 | tf_op jit(solution)/shard_map/all_gather | solution.py:17
  314.2 22.6 %copy.48 = f32[64,64,16,16]{1,3,2,0:T(8,128)} copy(f32[64,64,16,16]{3,2,1,0:T(8,128)} %bitcast.81) | data formatting | bytes 8388608
  336.8 106.0 %while.26 = (s32[]{:T(128)}, f32[64,16,16]{0,2,1:T(8,128)S(1)}, s32[]{:T(128)}, f32[64,64,16,16]{1,3,2,0:T(8,128)}, f32[64,64,16]{1,2,0:T(8,128)}, /*index=5*/s32[]{:T(128)}, s32[]{:T(128)}) while((s32[]{:T(128)}, f32[64,16,16]{0,2,1:T(8,128)S(1)}, s32[]{:T(128)}, f32[64,64,16,16]{1,3,2,0:T(8,128)}, f32[64,64,16]{1,2,0:T(8,128)}, ...), condition=%wide.region_4.5_spmd.clone, body=%wide.region_3.4_spmd.clone.sunk | while | flops 65540 | bytes 209001 | solution.py:26
  337.6 1.0 fusion.46
  401.4 1.0 fusion.46
  408.2 1.0 fusion.46
  409.8 1.0 fusion.46
  421.6 1.0 fusion.46
  426.7 1.0 fusion.46
  430.0 1.0 fusion.46
  431.7 1.0 fusion.46
  433.4 1.0 fusion.46
  438.4 1.0 fusion.46
  441.8 1.0 fusion.46
  444.1 25.6 %all-gather.6.cloned.1.call-done = bf16[1024,4096]{0,1:T(8,128)(2,1)} async-done(((bf16[1024,64]{0,1:T(8,128)(2,1)}), bf16[1024,4096]{0,1:T(8,128)(2,1)}) %all-gather.6.cloned.1.call-update) | async-done | bytes 8388624 | tf_op jit(solution)/shard_map/all_gather | solution.py:89
  469.7 7.0 %fusion.32 = f32[64,4096]{1,0:T(8,128)} fusion(bf16[64,1024]{0,1:T(8,128)(2,1)S(1)} %fusion.17, bf16[1024,4096]{0,1:T(8,128)(2,1)} %all-gather.6.cloned.1.call-done), kind=kOutput, calls=%fused_computation.53 | convolution fusion | flops 536870912 | bytes 9568256 | tf_op jit(solution)/shard_map/dot_general | solution.py:87
  476.8 36.6 %reduce-scatter.2.cloned.1.call-done = f32[64,512]{1,0:T(8,128)} async-done(((f32[64,4096]{1,0:T(8,128)}), f32[64,512]{1,0:T(8,128)}) %reduce-scatter.2.cloned.1.call-update) | async-done | bytes 131088 | tf_op jit(solution)/shard_map/reduce_scatter | solution.py:92
  513.4 1.5 convert_element_type.51
  (207 shorter events, 111.3 us)
Async XLA Ops:
  6.5 307.7 %all-gather.8.cloned.1.call-start = ((), (), s32[]{:S(2)}) async-start(), calls=%async_computation.3 | async-start | bytes 34078720 | tf_op jit(solution)/shard_map/all_gather | solution.py:17
  7.4 6.4 %collective-permute-start = (bf16[3,2,1024]{2,1,0:T(2,128)(2,1)S(1)}, bf16[3,2,1024]{2,1,0:T(2,128)(2,1)S(1)}, u32[]{:S(2)}, u32[]{:S(2)}) collective-permute-start(bf16[3,2,1024]{2,1,0:T(2,128)(2,1)S(1)} %slice.29), channel_id=1, source_target_pairs={{0,8},{8,16},{16,24},{24,32},{32,40},{40,48},{48,56},{56,64},{64,7... | collective-permute-start | bytes 36872 | tf_op jit(solution)/shard_map/ppermute | solution.py:12
  17.9 451.8 %all-gather.6.cloned.1.call-start = ((), (), s32[]{:S(2)}) async-start(), calls=%async_computation.1 | async-start | bytes 8519680 | tf_op jit(solution)/shard_map/all_gather | solution.py:89
  18.6 494.7 %reduce-scatter.2.cloned.1.call-start = ((), (), s32[]{:S(2)}) async-start(), calls=%async_computation.2 | async-start | bytes 1179648 | tf_op jit(solution)/shard_map/reduce_scatter | solution.py:92
  336.8 107.1 %copy-start = (f32[8,64,8,16]{1,3,2,0:T(8,128)S(1)}, f32[8,64,8,16]{1,3,2,0:T(8,128)}, u32[]{:S(2)}) copy-start(f32[8,64,8,16]{1,3,2,0:T(8,128)} %get-tuple-element.131) | copy-start | bytes 786436
  336.8 107.1 %copy-start.1 = (f32[1024]{0:T(1024)S(1)}, f32[1024]{0:T(1024)}, u32[]{:S(2)}) copy-start(f32[1024]{0:T(1024)} %param.14) | copy-start | bytes 12292
Sparse Core Ops, SparseCore 0:
  18.0 296.1 all-gather.7
  317.1 152.5 all-gather.5
  476.9 36.4 reduce-scatter.1
where the time goes:
time: 526 us; the launch traced here: 521 us
  local copies, waits for them, and re-layouts  173 us (33%)
  waiting for transfers between devices  135 us (26%)
  blocking collectives  114 us (22%)
  other arithmetic  65.9 us (13%)
  matrix products  15.8 us (3%)
  between operations  13.2 us (3%)
    all_gather x1, blocking collectives, entering(): pieces = jax.tree.map(lambda part: lax.all_gather(part, axis), value)  114 us
    gather x16, local copies, waits for them, and re-layouts, near_block(): taps_here[:, clipped]  100 us
    all_gather x1, waiting for transfers between devices, entering(): pieces = jax.tree.map(lambda part: lax.all_gather(part, axis), value)  71.9 us
    select_n x63, other arithmetic, hop(): jnp.where(position < mine, new, old)  60.5 us
    mul x63, local copies, waits for them, and re-layouts, combine_states(): return (earlier[0] * later[0], later[1] + later[0][:, None, :] * earlier[1])  44.3 us
    reduce_scatter x1, waiting for transfers between devices, per_device(): lax.psum_scatter(partial_out, 'tp', scatter_dimension=1, tiled=True)  36.6 us
    all_gather x1, waiting for transfers between devices, per_device(): lax.all_gather(out_weight, 'ctx', axis=1, tiled=True)  25.6 us
    unnamed x8, local copies, waits for them, and re-layouts  24 us
  transfers between devices with their start and end apart: 4, of which 3 were waited for; matrix products, arithmetic and copies ran while one was open for 46% of the time, Pallas kernels for 0%

commit v1 on v0

v1 whole, which is shorter than its diff:
```python
import jax
import jax.numpy as jnp
import numpy as np
from jax import lax
from jax.sharding import Mesh
from jax.sharding import PartitionSpec as P

CTX = ("chi", "clo")


def shifted(value, axis, count, by):
    pairs = [(i, i + by) for i in range(count) if i + by < count]
    return lax.ppermute(value, axis, pairs)


def make_per_device(n_ctx, n_tp):
    n_lo = n_ctx // n_tp

    def per_device(features, short_weight, decay_rate, residue, skip_gain, out_weight):
        rows = features.shape[1]
        chans = features.shape[2]
        groups = decay_rate.shape[0]
        modes = decay_rate.shape[1]
        width = chans // groups
        taps = short_weight.shape[1]

        rim = shifted(features[:, rows - (taps - 1) :, :], CTX, n_ctx, 1)
        extended = jnp.concatenate([rim, features], axis=1)
        conv = jnp.zeros(features.shape, jnp.float32)
        for j in range(taps):
            conv = conv + short_weight[:, j][:, None, :] * extended[
                :, taps - 1 - j : taps - 1 - j + rows, :
            ].astype(jnp.float32)
        q_lane = conv[0]
        gated = (conv[1] * conv[2]).astype(jnp.bfloat16)
        gated_wide = gated.astype(jnp.float32)

        coef = residue * jnp.sqrt(-jnp.expm1(-2.0 * decay_rate))
        lags = jnp.arange(rows, dtype=jnp.float32)
        near_filter = jnp.sum(
            coef[:, :, None] * jnp.exp(-decay_rate[:, :, None] * lags[None, None, :]), axis=1
        ).astype(jnp.bfloat16)

        index = np.arange(rows)
        onehot = (
            (index[None, :, None] - index[None, None, :]) == index[:, None, None]
        ).astype(np.float32)
        onehot = jnp.asarray(onehot.reshape(rows, rows * rows), jnp.bfloat16)
        toeplitz = jnp.dot(near_filter, onehot, preferred_element_type=jnp.float32)
        toeplitz = toeplitz.astype(jnp.bfloat16).reshape(groups, rows, rows)
        near = jnp.einsum(
            "gts,sgw->tgw",
            toeplitz,
            gated.reshape(rows, groups, width),
            preferred_element_type=jnp.float32,
        ).reshape(rows, chans)

        rate_c = jnp.repeat(decay_rate.T, width, axis=1)
        coef_c = jnp.repeat(coef.T, width, axis=1)
        end_basis = jnp.exp(-rate_c[None] * (rows - 1.0 - lags)[:, None, None])
        own_state = jnp.sum(end_basis * gated_wide[:, None, :], axis=0)
        state = shifted(own_state, CTX, n_ctx, 1)
        by = 1
        while by < n_ctx:
            decay = jnp.exp(-rate_c * float(rows * by))
            state = state + decay * shifted(state, CTX, n_ctx, by)
            by *= 2
        far_basis = coef_c[None] * jnp.exp(-rate_c[None] * (lags + 1.0)[:, None, None])
        far = jnp.sum(far_basis * state[None], axis=1)

        mixed = (q_lane * (near + far + skip_gain[None, :] * gated_wide)).astype(jnp.bfloat16)

        tokens = lax.all_gather(mixed, "chi", axis=0)
        weight = lax.all_gather(out_weight, "clo", axis=1, tiled=True)
        partial = jnp.einsum(
            "ktc,co->kto", tokens, weight, preferred_element_type=jnp.float32
        )
        block = lax.psum_scatter(partial, "tp", scatter_dimension=0, tiled=False)
        block = block.astype(jnp.bfloat16)
        swap = [(a * n_tp + b, b * n_tp + a) for a in range(n_tp) for b in range(n_tp)]
        return lax.ppermute(block, ("chi", "tp"), swap)

    return per_device


def solution(mesh):
    n_ctx = mesh.shape["ctx"]
    n_tp = mesh.shape["tp"]
    devices = np.asarray(mesh.devices).reshape(n_tp, n_ctx // n_tp, n_tp)
    split = Mesh(devices, ("chi", "clo", "tp"))
    placed = (
        P(None, CTX, "tp"),
        P(None, None, "tp"),
        P("tp", None),
        P("tp", None),
        P("tp"),
        P("tp", CTX),
    )
    return jax.shard_map(
        make_per_device(n_ctx, n_tp),
        mesh=split,
        in_specs=placed,
        out_specs=P(CTX, "tp"),
        check_vma=False,
    )
```

time: 526 us -> 211 us (0.40)
  the two profiles are of different devices: /device:TPU:16 before, /device:TPU:4 now
where the time goes in v1:
time: 211 us; the launch traced here: 210 us
  waiting for transfers between devices  97.7 us (46%)
  starting transfers between devices  84.4 us (40%)
  between operations  13.4 us (6%)
  other arithmetic  5.36 us (3%)
  local copies, waits for them, and re-layouts  5.05 us (2%)
  matrix products  4.19 us (2%)
    ppermute x8, starting transfers between devices, shifted(): return lax.ppermute(value, axis, pairs)  66.7 us
    all_gather x1, waiting for transfers between devices, per_device(): tokens = lax.all_gather(mixed, 'chi', axis=0)  54 us
    reduce_scatter x1, waiting for transfers between devices, per_device(): block = lax.psum_scatter(partial, 'tp', scatter_dimension=0, tiled=False)  31.5 us
    ppermute x1, starting transfers between devices, per_device(): return lax.ppermute(block, ('chi', 'tp'), swap)  17.6 us
    ppermute x8, waiting for transfers between devices, shifted(): return lax.ppermute(value, axis, pairs)  9.8 us
  transfers between devices with their start and end apart: 12, of which 9 were waited for; matrix products, arithmetic and copies ran while one was open for 4% of the time, Pallas kernels for 0%

profile of v1, /device:TPU:4, one launch (start us, length us, event | category | flops | bytes accessed | tf_op | source)
XLA Modules:
  0.0 210.1 jit_solution(5089914782824719049)
XLA Ops:
  6.5 0.9 slice.29
  7.4 3.5 %collective-permute-start = (bf16[3,2,1024]{2,1,0:T(2,128)(2,1)S(1)}, bf16[3,2,1024]{2,1,0:T(2,128)(2,1)S(1)}, u32[]{:S(2)}, u32[]{:S(2)}) collective-permute-start(bf16[3,2,1024]{2,1,0:T(2,128)(2,1)S(1)} %slice.29), channel_id=1, source_target_pairs={{0,8},{8,16},{16,24},{24,32},{32,40},{40,48},{48,56},{56,64},{64,7... | collective-permute-start | bytes 36872 | tf_op jit(solution)/shard_map/ppermute | solution.py:13
  10.9 0.9 fusion.9
  11.9 0.7 negate_bitcast_fusion
  13.1 0.3 multiply_add_fusion
  13.5 0.7 multiply_reduce_fusion.1
  14.2 3.6 %collective-permute-start.1 = (f32[16,1024]{1,0:T(8,128)S(1)}, f32[16,1024]{1,0:T(8,128)S(1)}, u32[]{:S(2)}, u32[]{:S(2)}) collective-permute-start(f32[16,1024]{1,0:T(8,128)S(1)} %multiply_reduce_fusion.1), channel_id=1, source_target_pairs={{0,8},{8,16},{16,24},{24,32},{32,40},{40,48},{48,56},{56,64},{64,7... | collective-permute-start | bytes 196616 | tf_op jit(solution)/shard_map/ppermute | solution.py:13
  17.9 1.9 collective-permute-done.1
  19.7 4.3 %collective-permute-start.2 = (f32[16,1024]{1,0:T(8,128)S(1)}, f32[16,1024]{1,0:T(8,128)S(1)}, u32[]{:S(2)}, u32[]{:S(2)}) collective-permute-start(f32[16,1024]{1,0:T(8,128)S(1)} %collective-permute-done.1), channel_id=1, source_target_pairs={{0,8},{8,16},{16,24},{24,32},{32,40},{40,48},{48,56},{56,64},{64,7... | collective-permute-start | bytes 196616 | tf_op jit(solution)/shard_map/ppermute | solution.py:13
  24.0 1.9 collective-permute-done.2
  25.9 6.0 %collective-permute-start.3 = (f32[16,1024]{1,0:T(8,128)S(1)}, f32[16,1024]{1,0:T(8,128)S(1)}, u32[]{:S(2)}, u32[]{:S(2)}) collective-permute-start(f32[16,1024]{1,0:T(8,128)S(1)} %multiply_add_fusion.6), channel_id=1, source_target_pairs={{0,16},{8,24},{16,32},{24,40},{32,48},{40,56},{48,64},{56,72},{64,... | collective-permute-start | bytes 196616 | tf_op jit(solution)/shard_map/ppermute | solution.py:13
  32.2 1.6 collective-permute-done.3
  33.8 11.9 %collective-permute-start.4 = (f32[16,1024]{1,0:T(8,128)S(1)}, f32[16,1024]{1,0:T(8,128)S(1)}, u32[]{:S(2)}, u32[]{:S(2)}) collective-permute-start(f32[16,1024]{1,0:T(8,128)S(1)} %multiply_add_fusion.5), channel_id=1, source_target_pairs={{0,32},{8,40},{16,48},{24,56},{32,64},{40,72},{48,80},{56,88},{64,... | collective-permute-start | bytes 196616 | tf_op jit(solution)/shard_map/ppermute | solution.py:13
  45.7 0.4 multiply_reduce_fusion.2
  46.1 1.6 collective-permute-done.4
  47.7 6.2 %collective-permute-start.5 = (f32[16,1024]{1,0:T(8,128)S(1)}, f32[16,1024]{1,0:T(8,128)S(1)}, u32[]{:S(2)}, u32[]{:S(2)}) collective-permute-start(f32[16,1024]{1,0:T(8,128)S(1)} %multiply_add_fusion.4), channel_id=1, source_target_pairs={{0,64},{8,72},{16,80},{24,88},{32,96},{40,104},{48,112},{56,120},{... | collective-permute-start | bytes 196616 | tf_op jit(solution)/shard_map/ppermute | solution.py:13
  54.0 0.3 convolution_convert_fusion
  54.7 1.1 reshape.70
  55.9 15.2 %collective-permute-start.6 = (f32[16,1024]{1,0:T(8,128)S(1)}, f32[16,1024]{1,0:T(8,128)S(1)}, u32[]{:S(2)}, u32[]{:S(2)}) collective-permute-start(f32[16,1024]{1,0:T(8,128)S(1)} %multiply_add_fusion.3), channel_id=1, source_target_pairs={{0,128},{8,136},{16,144},{24,152},{32,160},{40,168},{48,176},{56,1... | collective-permute-start | bytes 196616 | tf_op jit(solution)/shard_map/ppermute | solution.py:13
  71.3 1.7 collective-permute-done.6
  73.1 16.0 %collective-permute-start.7 = (f32[16,1024]{1,0:T(8,128)S(1)}, f32[16,1024]{1,0:T(8,128)S(1)}, u32[]{:S(2)}, u32[]{:S(2)}) collective-permute-start(f32[16,1024]{1,0:T(8,128)S(1)} %multiply_add_fusion.2), channel_id=1, source_target_pairs={{0,256},{8,264},{16,272},{24,280},{32,288},{40,296},{48,304},{56,3... | collective-permute-start | bytes 196616 | tf_op jit(solution)/shard_map/ppermute | solution.py:13
  89.1 0.7 fusion.10
  89.9 1.0 collective-permute-done.7
  91.0 1.4 multiply_reduce_fusion
  92.4 0.7 fusion.5
  93.3 54.0 %all-gather.3.cloned.1.call-done = bf16[8,64,1024]{2,1,0:T(8,128)(2,1)} async-done(((bf16[1,64,1024]{2,1,0:T(8,128)(2,1)}), bf16[8,64,1024]{2,1,0:T(8,128)(2,1)}) %all-gather.3.cloned.1.call-update) | async-done | bytes 1048592 | tf_op jit(solution)/shard_map/all_gather | solution.py:73
  147.3 3.3 %fusion = f32[8,64,512]{2,1,0:T(8,128)} fusion(bf16[8,64,1024]{2,1,0:T(8,128)(2,1)} %all-gather.3.cloned.1.call-done, bf16[1024,512]{0,1:T(8,128)(2,1)} %all-gather.5.cloned.1.call-done), kind=kOutput, calls=%fused_computation.3 | convolution fusion | flops 536870912 | bytes 3145728 | tf_op jit(solution)/shard_map/ktc,co->kto/dot_general | solution.py:75
  150.5 31.5 %reduce-scatter.2.cloned.1.call-done = f32[1,64,512]{2,1,0:T(8,128)} async-done(((f32[8,64,512]{2,1,0:T(8,128)}), f32[1,64,512]{2,1,0:T(8,128)}) %reduce-scatter.2.cloned.1.call-update) | async-done | bytes 131088 | tf_op jit(solution)/shard_map/reduce_scatter | solution.py:78
  182.1 0.9 convert_bitcast_fusion.1
  183.0 17.6 %collective-permute-start.8 = (bf16[64,512]{1,0:T(8,128)(2,1)S(1)}, bf16[64,512]{1,0:T(8,128)(2,1)S(1)}, u32[]{:S(2)}, u32[]{:S(2)}) collective-permute-start(bf16[64,512]{1,0:T(8,128)(2,1)S(1)} %convert_bitcast_fusion.1), channel_id=1, source_target_pairs={{0,0},{1,64},{2,128},{3,192},{4,256},{5,320},{6,384},{7,448},{64,1... | collective-permute-start | bytes 196616 | tf_op jit(solution)/shard_map/ppermute | solution.py:81
  200.6 2.3 %collective-permute-done.8 = bf16[64,512]{1,0:T(8,128)(2,1)S(1)} collective-permute-done((bf16[64,512]{1,0:T(8,128)(2,1)S(1)}, bf16[64,512]{1,0:T(8,128)(2,1)S(1)}, u32[]{:S(2)}, u32[]{:S(2)}) %collective-permute-start.8) | collective-permute-done | bytes 65568 | tf_op jit(solution)/shard_map/ppermute | solution.py:81
  202.9 0.6 copy.42
  (34 shorter events, 1.8 us)
Async XLA Ops:
  6.5 6.6 %copy-start.1 = (bf16[3,64,1024]{2,1,0:T(8,128)(2,1)S(1)}, bf16[3,64,1024]{2,1,0:T(8,128)(2,1)}, u32[]{:S(2)}) copy-start(bf16[3,64,1024]{2,1,0:T(8,128)(2,1)} %param.7) | copy-start | bytes 1179652
  6.5 86.7 %all-gather.5.cloned.1.call-start = ((), (), s32[]{:S(2)}) async-start(), calls=%async_computation.2 | async-start | bytes 1179648 | tf_op jit(solution)/shard_map/all_gather | solution.py:74
  7.4 5.7 %collective-permute-start = (bf16[3,2,1024]{2,1,0:T(2,128)(2,1)S(1)}, bf16[3,2,1024]{2,1,0:T(2,128)(2,1)S(1)}, u32[]{:S(2)}, u32[]{:S(2)}) collective-permute-start(bf16[3,2,1024]{2,1,0:T(2,128)(2,1)S(1)} %slice.29), channel_id=1, source_target_pairs={{0,8},{8,16},{16,24},{24,32},{32,40},{40,48},{48,56},{56,64},{64,7... | collective-permute-start | bytes 36872 | tf_op jit(solution)/shard_map/ppermute | solution.py:13
  14.2 39.7 %copy-start = (bf16[64,4096]{1,0:T(8,128)(2,1)S(1)}, bf16[64,4096]{1,0:T(8,128)(2,1)}, u32[]{:S(2)}) copy-start(bf16[64,4096]{1,0:T(8,128)(2,1)} %constant.22.clone) | copy-start | bytes 1572868
  14.2 5.5 %collective-permute-start.1 = (f32[16,1024]{1,0:T(8,128)S(1)}, f32[16,1024]{1,0:T(8,128)S(1)}, u32[]{:S(2)}, u32[]{:S(2)}) collective-permute-start(f32[16,1024]{1,0:T(8,128)S(1)} %multiply_reduce_fusion.1), channel_id=1, source_target_pairs={{0,8},{8,16},{16,24},{24,32},{32,40},{40,48},{48,56},{56,64},{64,7... | collective-permute-start | bytes 196616 | tf_op jit(solution)/shard_map/ppermute | solution.py:13
  19.7 6.1 %collective-permute-start.2 = (f32[16,1024]{1,0:T(8,128)S(1)}, f32[16,1024]{1,0:T(8,128)S(1)}, u32[]{:S(2)}, u32[]{:S(2)}) collective-permute-start(f32[16,1024]{1,0:T(8,128)S(1)} %collective-permute-done.1), channel_id=1, source_target_pairs={{0,8},{8,16},{16,24},{24,32},{32,40},{40,48},{48,56},{56,64},{64,7... | collective-permute-start | bytes 196616 | tf_op jit(solution)/shard_map/ppermute | solution.py:13
  25.9 7.9 %collective-permute-start.3 = (f32[16,1024]{1,0:T(8,128)S(1)}, f32[16,1024]{1,0:T(8,128)S(1)}, u32[]{:S(2)}, u32[]{:S(2)}) collective-permute-start(f32[16,1024]{1,0:T(8,128)S(1)} %multiply_add_fusion.6), channel_id=1, source_target_pairs={{0,16},{8,24},{16,32},{24,40},{32,48},{40,56},{48,64},{56,72},{64,... | collective-permute-start | bytes 196616 | tf_op jit(solution)/shard_map/ppermute | solution.py:13
  32.0 115.3 %all-gather.3.cloned.1.call-start = ((), (), s32[]{:S(2)}) async-start(), calls=%async_computation.1 | async-start | bytes 1179648 | tf_op jit(solution)/shard_map/all_gather | solution.py:73
  33.8 13.8 %collective-permute-start.4 = (f32[16,1024]{1,0:T(8,128)S(1)}, f32[16,1024]{1,0:T(8,128)S(1)}, u32[]{:S(2)}, u32[]{:S(2)}) collective-permute-start(f32[16,1024]{1,0:T(8,128)S(1)} %multiply_add_fusion.5), channel_id=1, source_target_pairs={{0,32},{8,40},{16,48},{24,56},{32,64},{40,72},{48,80},{56,88},{64,... | collective-permute-start | bytes 196616 | tf_op jit(solution)/shard_map/ppermute | solution.py:13
  47.7 8.1 %collective-permute-start.5 = (f32[16,1024]{1,0:T(8,128)S(1)}, f32[16,1024]{1,0:T(8,128)S(1)}, u32[]{:S(2)}, u32[]{:S(2)}) collective-permute-start(f32[16,1024]{1,0:T(8,128)S(1)} %multiply_add_fusion.4), channel_id=1, source_target_pairs={{0,64},{8,72},{16,80},{24,88},{32,96},{40,104},{48,112},{56,120},{... | collective-permute-start | bytes 196616 | tf_op jit(solution)/shard_map/ppermute | solution.py:13
  55.9 17.2 %collective-permute-start.6 = (f32[16,1024]{1,0:T(8,128)S(1)}, f32[16,1024]{1,0:T(8,128)S(1)}, u32[]{:S(2)}, u32[]{:S(2)}) collective-permute-start(f32[16,1024]{1,0:T(8,128)S(1)} %multiply_add_fusion.3), channel_id=1, source_target_pairs={{0,128},{8,136},{16,144},{24,152},{32,160},{40,168},{48,176},{56,1... | collective-permute-start | bytes 196616 | tf_op jit(solution)/shard_map/ppermute | solution.py:13
  73.1 17.9 %collective-permute-start.7 = (f32[16,1024]{1,0:T(8,128)S(1)}, f32[16,1024]{1,0:T(8,128)S(1)}, u32[]{:S(2)}, u32[]{:S(2)}) collective-permute-start(f32[16,1024]{1,0:T(8,128)S(1)} %multiply_add_fusion.2), channel_id=1, source_target_pairs={{0,256},{8,264},{16,272},{24,280},{32,288},{40,296},{48,304},{56,3... | collective-permute-start | bytes 196616 | tf_op jit(solution)/shard_map/ppermute | solution.py:13
  91.0 1.5 copy-start.2
  93.2 88.9 %reduce-scatter.2.cloned.1.call-start = ((), (), s32[]{:S(2)}) async-start(), calls=%async_computation.3 | async-start | bytes 1179648 | tf_op jit(solution)/shard_map/reduce_scatter | solution.py:78
  183.0 19.9 %collective-permute-start.8 = (bf16[64,512]{1,0:T(8,128)(2,1)S(1)}, bf16[64,512]{1,0:T(8,128)(2,1)S(1)}, u32[]{:S(2)}, u32[]{:S(2)}) collective-permute-start(bf16[64,512]{1,0:T(8,128)(2,1)S(1)} %convert_bitcast_fusion.1), channel_id=1, source_target_pairs={{0,0},{1,64},{2,128},{3,192},{4,256},{5,320},{6,384},{7,448},{64,1... | collective-permute-start | bytes 196616 | tf_op jit(solution)/shard_map/ppermute | solution.py:81
Sparse Core Ops, SparseCore 0:
  32.1 58.0 all-gather.4
  93.3 53.9 all-gather.2
  150.7 31.3 reduce-scatter.1

commit v2 on v1

--- a/solution.py
+++ b/solution.py
@@ -13,6 +13,27 @@
     return lax.ppermute(value, axis, pairs)
 
 
+def rotated(value, axis, count, by):
+    return lax.ppermute(value, axis, [(i, (i + by) % count) for i in range(count)])
+
+
+def digit_rotated(value, count, stride, size, by):
+    pairs = []
+    for i in range(count):
+        d = (i // stride) % size
+        pairs.append((i, i + (((d + by) % size) - d) * stride))
+    return lax.ppermute(value, CTX, pairs)
+
+
+def scan_levels(count):
+    levels = []
+    while count > 1:
+        size = 4 if count % 4 == 0 else count
+        levels.append(size)
+        count //= size
+    return levels
+
+
 def make_per_device(n_ctx, n_tp):
     n_lo = n_ctx // n_tp
 
@@ -20,9 +41,15 @@
         rows = features.shape[1]
         chans = features.shape[2]
         groups = decay_rate.shape[0]
-        modes = decay_rate.shape[1]
         width = chans // groups
         taps = short_weight.shape[1]
+        chi = lax.axis_index("chi")
+        clo = lax.axis_index("clo")
+        me = chi * n_lo + clo
+        tp = lax.axis_index("tp")
+
+        weight = lax.all_gather(out_weight, "chi", axis=1, tiled=True)
+        weight = weight.reshape(chans, n_tp, -1)
 
         rim = shifted(features[:, rows - (taps - 1) :, :], CTX, n_ctx, 1)
         extended = jnp.concatenate([rim, features], axis=1)
@@ -57,28 +84,49 @@
 
         rate_c = jnp.repeat(decay_rate.T, width, axis=1)
         coef_c = jnp.repeat(coef.T, width, axis=1)
+
+        def decay(blocks):
+            return jnp.exp(-rate_c * (rows * blocks.astype(jnp.float32)))
+
         end_basis = jnp.exp(-rate_c[None] * (rows - 1.0 - lags)[:, None, None])
         own_state = jnp.sum(end_basis * gated_wide[:, None, :], axis=0)
-        state = shifted(own_state, CTX, n_ctx, 1)
-        by = 1
-        while by < n_ctx:
-            decay = jnp.exp(-rate_c * float(rows * by))
-            state = state + decay * shifted(state, CTX, n_ctx, by)
-            by *= 2
+        before = jnp.zeros_like(own_state)
+        total = own_state
+        stride = 1
+        for size in scan_levels(n_ctx):
+            d = (me // stride) % size
+            r = me % stride
+            merged = decay((size - 1 - d) * stride) * total
+            for by in range(1, size):
+                got = digit_rotated(total, n_ctx, stride, size, by)
+                src = (d - by) % size
+                before = before + jnp.where(
+                    by <= d, decay((by - 1) * stride + r) * got, jnp.zeros_like(got)
+                )
+                merged = merged + decay((size - 1 - src) * stride) * got
+            total = merged
+            stride *= size
         far_basis = coef_c[None] * jnp.exp(-rate_c[None] * (lags + 1.0)[:, None, None])
-        far = jnp.sum(far_basis * state[None], axis=1)
+        far = jnp.sum(far_basis * before[None], axis=1)
 
         mixed = (q_lane * (near + far + skip_gain[None, :] * gated_wide)).astype(jnp.bfloat16)
 
-        tokens = lax.all_gather(mixed, "chi", axis=0)
-        weight = lax.all_gather(out_weight, "clo", axis=1, tiled=True)
+        tokens = [mixed] + [rotated(mixed, "clo", n_lo, by) for by in range(1, n_lo)]
+        tokens = jnp.stack(tokens)
         partial = jnp.einsum(
-            "ktc,co->kto", tokens, weight, preferred_element_type=jnp.float32
+            "ktc,cqo->qkto", tokens, weight, preferred_element_type=jnp.float32
         )
-        block = lax.psum_scatter(partial, "tp", scatter_dimension=0, tiled=False)
-        block = block.astype(jnp.bfloat16)
-        swap = [(a * n_tp + b, b * n_tp + a) for a in range(n_tp) for b in range(n_tp)]
-        return lax.ppermute(block, ("chi", "tp"), swap)
+        summed = lax.dynamic_index_in_dim(partial, tp, 0, keepdims=False)
+        for by in range(1, n_tp):
+            piece = lax.dynamic_index_in_dim(partial, (tp + by) % n_tp, 0, keepdims=False)
+            summed = summed + rotated(piece, "tp", n_tp, by)
+        summed = summed.astype(jnp.bfloat16)
+        back = [summed[0]] + [
+            rotated(summed[by], "clo", n_lo, n_lo - by) for by in range(1, n_lo)
+        ]
+        back = jnp.stack(back)
+        back = jnp.roll(back, clo, axis=0)
+        return back.transpose(1, 0, 2).reshape(rows, -1)
 
     return per_device
 

time: 211 us -> 189 us (0.90)
  the two profiles are of different devices: /device:TPU:4 before, /device:TPU:32 now
where the time goes in v2:
time: 189 us; the launch traced here: 188 us
  starting transfers between devices  116 us (61%)
  waiting for transfers between devices  34.7 us (18%)
  between operations  14.3 us (8%)
  local copies, waits for them, and re-layouts  11.3 us (6%)
  other arithmetic  7.29 us (4%)
  matrix products  3.72 us (2%)
    ppermute x21, starting transfers between devices, rotated(): lax.ppermute(value, axis, [(i, (i + by) % count) for i in range(count)])  67.3 us
    ppermute x9, starting transfers between devices, digit_rotated(): return lax.ppermute(value, CTX, pairs)  45.6 us
    ppermute x21, waiting for transfers between devices, rotated(): lax.ppermute(value, axis, [(i, (i + by) % count) for i in range(count)])  19.5 us
    ppermute x9, waiting for transfers between devices, digit_rotated(): return lax.ppermute(value, CTX, pairs)  13.7 us
    unnamed x26, local copies, waits for them, and re-layouts  4.12 us
  transfers between devices with their start and end apart: 32, of which 13 were waited for; matrix products, arithmetic and copies ran while one was open for 8% of the time, Pallas kernels for 0%

profile of v2, /device:TPU:32, one launch (start us, length us, event | category | flops | bytes accessed | tf_op | source)
XLA Modules:
  0.0 187.7 jit_solution(8896078289423122640)
XLA Ops:
  7.4 3.5 %collective-permute-start = (bf16[3,2,1024]{2,1,0:T(2,128)(2,1)S(1)}, bf16[3,2,1024]{2,1,0:T(2,128)(2,1)S(1)}, u32[]{:S(2)}, u32[]{:S(2)}) collective-permute-start(bf16[3,2,1024]{2,1,0:T(2,128)(2,1)S(1)} %slice.53), channel_id=1, source_target_pairs={{0,8},{8,16},{16,24},{24,32},{32,40},{40,48},{48,56},{56,64},{64,7... | collective-permute-start | bytes 36872 | tf_op jit(solution)/shard_map/ppermute | solution.py:13
  17.7 2.1 %collective-permute-start.1 = (f32[16,1024]{1,0:T(8,128)S(1)}, f32[16,1024]{1,0:T(8,128)S(1)}, u32[]{:S(2)}, u32[]{:S(2)}) collective-permute-start(f32[16,1024]{1,0:T(8,128)S(1)} %multiply_reduce_fusion.1), channel_id=1, source_target_pairs={{0,8},{8,16},{16,24},{24,0},{32,40},{40,48},{48,56},{56,32},{64,72... | collective-permute-start | bytes 196616 | tf_op jit(solution)/shard_map/ppermute | solution.py:25
  19.7 4.8 %collective-permute-start.2 = (f32[16,1024]{1,0:T(8,128)S(1)}, f32[16,1024]{1,0:T(8,128)S(1)}, u32[]{:S(2)}, u32[]{:S(2)}) collective-permute-start(f32[16,1024]{1,0:T(8,128)S(1)} %multiply_reduce_fusion.1), channel_id=1, source_target_pairs={{0,16},{8,24},{16,0},{24,8},{32,48},{40,56},{48,32},{56,40},{64,80... | collective-permute-start | bytes 196616 | tf_op jit(solution)/shard_map/ppermute | solution.py:25
  24.6 3.0 %collective-permute-start.3 = (f32[16,1024]{1,0:T(8,128)S(1)}, f32[16,1024]{1,0:T(8,128)S(1)}, u32[]{:S(2)}, u32[]{:S(2)}) collective-permute-start(f32[16,1024]{1,0:T(8,128)S(1)} %multiply_reduce_fusion.1), channel_id=1, source_target_pairs={{0,24},{8,0},{16,8},{24,16},{32,56},{40,32},{48,40},{56,48},{64,88... | collective-permute-start | bytes 196616 | tf_op jit(solution)/shard_map/ppermute | solution.py:25
  30.8 3.8 %collective-permute-start.4 = (f32[16,1024]{1,0:T(8,128)S(1)}, f32[16,1024]{1,0:T(8,128)S(1)}, u32[]{:S(2)}, u32[]{:S(2)}) collective-permute-start(f32[16,1024]{1,0:T(8,128)S(1)} %multiply_add_fusion.2), channel_id=1, source_target_pairs={{0,32},{8,40},{16,48},{24,56},{32,64},{40,72},{48,80},{56,88},{64,... | collective-permute-start | bytes 196616 | tf_op jit(solution)/shard_map/ppermute | solution.py:25
  34.6 4.5 %collective-permute-start.5 = (f32[16,1024]{1,0:T(8,128)S(1)}, f32[16,1024]{1,0:T(8,128)S(1)}, u32[]{:S(2)}, u32[]{:S(2)}) collective-permute-start(f32[16,1024]{1,0:T(8,128)S(1)} %multiply_add_fusion.2), channel_id=1, source_target_pairs={{0,64},{8,72},{16,80},{24,88},{32,96},{40,104},{48,112},{56,120},{... | collective-permute-start | bytes 196616 | tf_op jit(solution)/shard_map/ppermute | solution.py:25
  39.1 3.9 %collective-permute-start.6 = (f32[16,1024]{1,0:T(8,128)S(1)}, f32[16,1024]{1,0:T(8,128)S(1)}, u32[]{:S(2)}, u32[]{:S(2)}) collective-permute-start(f32[16,1024]{1,0:T(8,128)S(1)} %multiply_add_fusion.2), channel_id=1, source_target_pairs={{0,96},{8,104},{16,112},{24,120},{32,0},{40,8},{48,16},{56,24},{64... | collective-permute-start | bytes 196616 | tf_op jit(solution)/shard_map/ppermute | solution.py:25
  43.2 2.3 %collective-permute-done.5 = f32[16,1024]{1,0:T(8,128)S(1)} collective-permute-done((f32[16,1024]{1,0:T(8,128)S(1)}, f32[16,1024]{1,0:T(8,128)S(1)}, u32[]{:S(2)}, u32[]{:S(2)}) %collective-permute-start.5) | collective-permute-done | bytes 65568 | tf_op jit(solution)/shard_map/ppermute | solution.py:25
  45.5 3.0 %collective-permute-done.6 = f32[16,1024]{1,0:T(8,128)S(1)} collective-permute-done((f32[16,1024]{1,0:T(8,128)S(1)}, f32[16,1024]{1,0:T(8,128)S(1)}, u32[]{:S(2)}, u32[]{:S(2)}) %collective-permute-start.6) | collective-permute-done | bytes 65568 | tf_op jit(solution)/shard_map/ppermute | solution.py:25
  48.5 12.2 %collective-permute-start.7 = (f32[16,1024]{1,0:T(8,128)S(1)}, f32[16,1024]{1,0:T(8,128)S(1)}, u32[]{:S(2)}, u32[]{:S(2)}) collective-permute-start(f32[16,1024]{1,0:T(8,128)S(1)} %multiply_add_fusion.1), channel_id=1, source_target_pairs={{0,128},{8,136},{16,144},{24,152},{32,160},{40,168},{48,176},{56,1... | collective-permute-start | bytes 196616 | tf_op jit(solution)/shard_map/ppermute | solution.py:25
  60.7 5.3 %collective-permute-start.8 = (f32[16,1024]{1,0:T(8,128)S(1)}, f32[16,1024]{1,0:T(8,128)S(1)}, u32[]{:S(2)}, u32[]{:S(2)}) collective-permute-start(f32[16,1024]{1,0:T(8,128)S(1)} %multiply_add_fusion.1), channel_id=1, source_target_pairs={{0,256},{8,264},{16,272},{24,280},{32,288},{40,296},{48,304},{56,3... | collective-permute-start | bytes 196616 | tf_op jit(solution)/shard_map/ppermute | solution.py:25
  66.0 6.1 %collective-permute-start.9 = (f32[16,1024]{1,0:T(8,128)S(1)}, f32[16,1024]{1,0:T(8,128)S(1)}, u32[]{:S(2)}, u32[]{:S(2)}) collective-permute-start(f32[16,1024]{1,0:T(8,128)S(1)} %multiply_add_fusion.1), channel_id=1, source_target_pairs={{0,384},{8,392},{16,400},{24,408},{32,416},{40,424},{48,432},{56,4... | collective-permute-start | bytes 196616 | tf_op jit(solution)/shard_map/ppermute | solution.py:25
  73.1 7.5 %collective-permute-done.8 = f32[16,1024]{1,0:T(8,128)S(1)} collective-permute-done((f32[16,1024]{1,0:T(8,128)S(1)}, f32[16,1024]{1,0:T(8,128)S(1)}, u32[]{:S(2)}, u32[]{:S(2)}) %collective-permute-start.8) | collective-permute-done | bytes 65568 | tf_op jit(solution)/shard_map/ppermute | solution.py:25
  84.2 4.5 %collective-permute-start.11 = (bf16[64,1024]{1,0:T(8,128)(2,1)S(1)}, bf16[64,1024]{1,0:T(8,128)(2,1)S(1)}, u32[]{:S(2)}, u32[]{:S(2)}) collective-permute-start(bf16[64,1024]{1,0:T(8,128)(2,1)S(1)} %fusion.14), channel_id=1, source_target_pairs={{0,16},{8,24},{16,32},{24,40},{32,48},{40,56},{48,0},{56,8},{1,17}... | collective-permute-start | bytes 393224 | tf_op jit(solution)/shard_map/ppermute | solution.py:17
  88.7 3.8 %collective-permute-start.12 = (bf16[64,1024]{1,0:T(8,128)(2,1)S(1)}, bf16[64,1024]{1,0:T(8,128)(2,1)S(1)}, u32[]{:S(2)}, u32[]{:S(2)}) collective-permute-start(bf16[64,1024]{1,0:T(8,128)(2,1)S(1)} %fusion.14), channel_id=1, source_target_pairs={{0,24},{8,32},{16,40},{24,48},{32,56},{40,0},{48,8},{56,16},{1,25}... | collective-permute-start | bytes 393224 | tf_op jit(solution)/shard_map/ppermute | solution.py:17
  92.5 2.1 %collective-permute-start.13 = (bf16[64,1024]{1,0:T(8,128)(2,1)S(1)}, bf16[64,1024]{1,0:T(8,128)(2,1)S(1)}, u32[]{:S(2)}, u32[]{:S(2)}) collective-permute-start(bf16[64,1024]{1,0:T(8,128)(2,1)S(1)} %fusion.14), channel_id=1, source_target_pairs={{0,32},{8,40},{16,48},{24,56},{32,0},{40,8},{48,16},{56,24},{1,33}... | collective-permute-start | bytes 393224 | tf_op jit(solution)/shard_map/ppermute | solution.py:17
  94.6 4.1 %collective-permute-start.14 = (bf16[64,1024]{1,0:T(8,128)(2,1)S(1)}, bf16[64,1024]{1,0:T(8,128)(2,1)S(1)}, u32[]{:S(2)}, u32[]{:S(2)}) collective-permute-start(bf16[64,1024]{1,0:T(8,128)(2,1)S(1)} %fusion.14), channel_id=1, source_target_pairs={{0,40},{8,48},{16,56},{24,0},{32,8},{40,16},{48,24},{56,32},{1,41}... | collective-permute-start | bytes 393224 | tf_op jit(solution)/shard_map/ppermute | solution.py:17
  99.5 4.1 %collective-permute-start.15 = (bf16[64,1024]{1,0:T(8,128)(2,1)S(1)}, bf16[64,1024]{1,0:T(8,128)(2,1)S(1)}, u32[]{:S(2)}, u32[]{:S(2)}) collective-permute-start(bf16[64,1024]{1,0:T(8,128)(2,1)S(1)} %fusion.14), channel_id=1, source_target_pairs={{0,48},{8,56},{16,0},{24,8},{32,16},{40,24},{48,32},{56,40},{1,49}... | collective-permute-start | bytes 393224 | tf_op jit(solution)/shard_map/ppermute | solution.py:17
  104.2 3.4 %collective-permute-start.16 = (bf16[64,1024]{1,0:T(8,128)(2,1)S(1)}, bf16[64,1024]{1,0:T(8,128)(2,1)S(1)}, u32[]{:S(2)}, u32[]{:S(2)}) collective-permute-start(bf16[64,1024]{1,0:T(8,128)(2,1)S(1)} %fusion.14), channel_id=1, source_target_pairs={{0,56},{8,0},{16,8},{24,16},{32,24},{40,32},{48,40},{56,48},{1,57}... | collective-permute-start | bytes 393224 | tf_op jit(solution)/shard_map/ppermute | solution.py:17
  111.8 2.8 %fusion = f32[8,64,8,64]{3,1,2,0:T(8,128)S(1)} fusion(bf16[1024,8,64,1]{0,2,1,3:T(8,128)(2,1)} %bitcast.129, bf16[8,64,1024]{2,1,0:T(8,128)(2,1)} %bitcast_dynamic-update-slice_fusion), kind=kOutput, calls=%fused_computation.3 | convolution fusion | flops 536870912 | bytes 3145728 | tf_op jit(solution)/shard_map/ktc,cqo->qkto/dot_general | solution.py:116
  115.7 3.1 %collective-permute-start.18 = (f32[8,64,64]{2,1,0:T(8,128)S(1)}, f32[8,64,64]{2,1,0:T(8,128)S(1)}, u32[]{:S(2)}, u32[]{:S(2)}) collective-permute-start(f32[8,64,64]{2,1,0:T(8,128)S(1)} %get-tuple-element.13), channel_id=1, source_target_pairs={{0,2},{1,3},{2,4},{3,5},{4,6},{5,7},{6,0},{7,1},{8,10},{9,11},{10,... | collective-permute-start | bytes 393224 | tf_op jit(solution)/shard_map/ppermute | solution.py:17
  118.8 3.3 %collective-permute-start.19 = (f32[8,64,64]{2,1,0:T(8,128)}, f32[8,64,64]{2,1,0:T(8,128)S(1)}, u32[]{:S(2)}, u32[]{:S(2)}) collective-permute-start(f32[8,64,64]{2,1,0:T(8,128)} %get-tuple-element.12), channel_id=1, source_target_pairs={{0,3},{1,4},{2,5},{3,6},{4,7},{5,0},{6,1},{7,2},{8,11},{9,12},{10,... | collective-permute-start | bytes 393224 | tf_op jit(solution)/shard_map/ppermute | solution.py:17
  122.1 4.6 %collective-permute-start.20 = (f32[8,64,64]{2,1,0:T(8,128)}, f32[8,64,64]{2,1,0:T(8,128)S(1)}, u32[]{:S(2)}, u32[]{:S(2)}) collective-permute-start(f32[8,64,64]{2,1,0:T(8,128)} %get-tuple-element.11), channel_id=1, source_target_pairs={{0,4},{1,5},{2,6},{3,7},{4,0},{5,1},{6,2},{7,3},{8,12},{9,13},{10,... | collective-permute-start | bytes 393224 | tf_op jit(solution)/shard_map/ppermute | solution.py:17
  126.7 2.8 %collective-permute-start.21 = (f32[8,64,64]{2,1,0:T(8,128)}, f32[8,64,64]{2,1,0:T(8,128)S(1)}, u32[]{:S(2)}, u32[]{:S(2)}) collective-permute-start(f32[8,64,64]{2,1,0:T(8,128)} %get-tuple-element.10), channel_id=1, source_target_pairs={{0,5},{1,6},{2,7},{3,0},{4,1},{5,2},{6,3},{7,4},{8,13},{9,14},{10,... | collective-permute-start | bytes 393224 | tf_op jit(solution)/shard_map/ppermute | solution.py:17
  129.6 3.9 %collective-permute-start.22 = (f32[8,64,64]{2,1,0:T(8,128)}, f32[8,64,64]{2,1,0:T(8,128)}, u32[]{:S(2)}, u32[]{:S(2)}) collective-permute-start(f32[8,64,64]{2,1,0:T(8,128)} %get-tuple-element.9), channel_id=1, source_target_pairs={{0,6},{1,7},{2,0},{3,1},{4,2},{5,3},{6,4},{7,5},{8,14},{9,15},{10,... | collective-permute-start | bytes 393224 | tf_op jit(solution)/shard_map/ppermute | solution.py:17
  134.3 4.9 %collective-permute-done.20 = f32[8,64,64]{2,1,0:T(8,128)S(1)} collective-permute-done((f32[8,64,64]{2,1,0:T(8,128)}, f32[8,64,64]{2,1,0:T(8,128)S(1)}, u32[]{:S(2)}, u32[]{:S(2)}) %collective-permute-start.20) | collective-permute-done | bytes 131104 | tf_op jit(solution)/shard_map/ppermute | solution.py:17
  140.0 5.4 %collective-permute-done.22 = f32[8,64,64]{2,1,0:T(8,128)} collective-permute-done((f32[8,64,64]{2,1,0:T(8,128)}, f32[8,64,64]{2,1,0:T(8,128)}, u32[]{:S(2)}, u32[]{:S(2)}) %collective-permute-start.22) | collective-permute-done | bytes 131104 | tf_op jit(solution)/shard_map/ppermute | solution.py:17
  148.3 5.6 %collective-permute-start.24 = (bf16[64,64]{1,0:T(8,128)(2,1)S(1)}, bf16[64,64]{1,0:T(8,128)(2,1)S(1)}, u32[]{:S(2)}, u32[]{:S(2)}) collective-permute-start(bf16[64,64]{1,0:T(8,128)(2,1)S(1)} %get-tuple-element.21), channel_id=1, source_target_pairs={{0,56},{8,0},{16,8},{24,16},{32,24},{40,32},{48,40},{56,48},{1,57}... | collective-permute-start | bytes 24584 | tf_op jit(solution)/shard_map/ppermute | solution.py:17
  155.9 4.2 %collective-permute-start.26 = (bf16[64,64]{1,0:T(8,128)(2,1)S(1)}, bf16[64,64]{1,0:T(8,128)(2,1)S(1)}, u32[]{:S(2)}, u32[]{:S(2)}) collective-permute-start(bf16[64,64]{1,0:T(8,128)(2,1)S(1)} %get-tuple-element.19), channel_id=1, source_target_pairs={{0,40},{8,48},{16,56},{24,0},{32,8},{40,16},{48,24},{56,32},{1,41}... | collective-permute-start | bytes 24584 | tf_op jit(solution)/shard_map/ppermute | solution.py:17
  162.1 4.8 %collective-permute-start.28 = (bf16[64,64]{1,0:T(8,128)(2,1)S(1)}, bf16[64,64]{1,0:T(8,128)(2,1)S(1)}, u32[]{:S(2)}, u32[]{:S(2)}) collective-permute-start(bf16[64,64]{1,0:T(8,128)(2,1)S(1)} %get-tuple-element.17), channel_id=1, source_target_pairs={{0,24},{8,32},{16,40},{24,48},{32,56},{40,0},{48,8},{56,16},{1,25}... | collective-permute-start | bytes 24584 | tf_op jit(solution)/shard_map/ppermute | solution.py:17
  167.0 5.1 %collective-permute-start.29 = (bf16[64,64]{1,0:T(8,128)(2,1)S(1)}, bf16[64,64]{1,0:T(8,128)(2,1)S(1)}, u32[]{:S(2)}, u32[]{:S(2)}) collective-permute-start(bf16[64,64]{1,0:T(8,128)(2,1)S(1)} %get-tuple-element.16), channel_id=1, source_target_pairs={{0,16},{8,24},{16,32},{24,40},{32,48},{40,56},{48,0},{56,8},{1,17}... | collective-permute-start | bytes 24584 | tf_op jit(solution)/shard_map/ppermute | solution.py:17
  175.0 4.8 %collective-permute-done.30 = bf16[64,64]{1,0:T(8,128)(2,1)S(1)} collective-permute-done((bf16[64,64]{1,0:T(8,128)(2,1)S(1)}, bf16[64,64]{1,0:T(8,128)(2,1)S(1)}, u32[]{:S(2)}, u32[]{:S(2)}) %collective-permute-start.30) | collective-permute-done | bytes 8224 | tf_op jit(solution)/shard_map/ppermute | solution.py:17
  (95 shorter events, 34.0 us)
Async XLA Ops:
  6.5 105.2 %all-gather.2.cloned.1.call-start = ((), (), s32[]{:S(2)}) async-start(), calls=%async_computation | async-start | bytes 1179648 | tf_op jit(solution)/shard_map/all_gather | solution.py:51
  7.4 7.7 %collective-permute-start = (bf16[3,2,1024]{2,1,0:T(2,128)(2,1)S(1)}, bf16[3,2,1024]{2,1,0:T(2,128)(2,1)S(1)}, u32[]{:S(2)}, u32[]{:S(2)}) collective-permute-start(bf16[3,2,1024]{2,1,0:T(2,128)(2,1)S(1)} %slice.53), channel_id=1, source_target_pairs={{0,8},{8,16},{16,24},{24,32},{32,40},{40,48},{48,56},{56,64},{64,7... | collective-permute-start | bytes 36872 | tf_op jit(solution)/shard_map/ppermute | solution.py:13
  17.7 12.1 %collective-permute-start.1 = (f32[16,1024]{1,0:T(8,128)S(1)}, f32[16,1024]{1,0:T(8,128)S(1)}, u32[]{:S(2)}, u32[]{:S(2)}) collective-permute-start(f32[16,1024]{1,0:T(8,128)S(1)} %multiply_reduce_fusion.1), channel_id=1, source_target_pairs={{0,8},{8,16},{16,24},{24,0},{32,40},{40,48},{48,56},{56,32},{64,72... | collective-permute-start | bytes 196616 | tf_op jit(solution)/shard_map/ppermute | solution.py:25
  19.7 10.0 %collective-permute-start.2 = (f32[16,1024]{1,0:T(8,128)S(1)}, f32[16,1024]{1,0:T(8,128)S(1)}, u32[]{:S(2)}, u32[]{:S(2)}) collective-permute-start(f32[16,1024]{1,0:T(8,128)S(1)} %multiply_reduce_fusion.1), channel_id=1, source_target_pairs={{0,16},{8,24},{16,0},{24,8},{32,48},{40,56},{48,32},{56,40},{64,80... | collective-permute-start | bytes 196616 | tf_op jit(solution)/shard_map/ppermute | solution.py:25
  24.6 6.2 %collective-permute-start.3 = (f32[16,1024]{1,0:T(8,128)S(1)}, f32[16,1024]{1,0:T(8,128)S(1)}, u32[]{:S(2)}, u32[]{:S(2)}) collective-permute-start(f32[16,1024]{1,0:T(8,128)S(1)} %multiply_reduce_fusion.1), channel_id=1, source_target_pairs={{0,24},{8,0},{16,8},{24,16},{32,56},{40,32},{48,40},{56,48},{64,88... | collective-permute-start | bytes 196616 | tf_op jit(solution)/shard_map/ppermute | solution.py:25
  30.8 12.4 %collective-permute-start.4 = (f32[16,1024]{1,0:T(8,128)S(1)}, f32[16,1024]{1,0:T(8,128)S(1)}, u32[]{:S(2)}, u32[]{:S(2)}) collective-permute-start(f32[16,1024]{1,0:T(8,128)S(1)} %multiply_add_fusion.2), channel_id=1, source_target_pairs={{0,32},{8,40},{16,48},{24,56},{32,64},{40,72},{48,80},{56,88},{64,... | collective-permute-start | bytes 196616 | tf_op jit(solution)/shard_map/ppermute | solution.py:25
  34.6 10.9 %collective-permute-start.5 = (f32[16,1024]{1,0:T(8,128)S(1)}, f32[16,1024]{1,0:T(8,128)S(1)}, u32[]{:S(2)}, u32[]{:S(2)}) collective-permute-start(f32[16,1024]{1,0:T(8,128)S(1)} %multiply_add_fusion.2), channel_id=1, source_target_pairs={{0,64},{8,72},{16,80},{24,88},{32,96},{40,104},{48,112},{56,120},{... | collective-permute-start | bytes 196616 | tf_op jit(solution)/shard_map/ppermute | solution.py:25
  39.1 9.4 %collective-permute-start.6 = (f32[16,1024]{1,0:T(8,128)S(1)}, f32[16,1024]{1,0:T(8,128)S(1)}, u32[]{:S(2)}, u32[]{:S(2)}) collective-permute-start(f32[16,1024]{1,0:T(8,128)S(1)} %multiply_add_fusion.2), channel_id=1, source_target_pairs={{0,96},{8,104},{16,112},{24,120},{32,0},{40,8},{48,16},{56,24},{64... | collective-permute-start | bytes 196616 | tf_op jit(solution)/shard_map/ppermute | solution.py:25
  48.5 24.6 %collective-permute-start.7 = (f32[16,1024]{1,0:T(8,128)S(1)}, f32[16,1024]{1,0:T(8,128)S(1)}, u32[]{:S(2)}, u32[]{:S(2)}) collective-permute-start(f32[16,1024]{1,0:T(8,128)S(1)} %multiply_add_fusion.1), channel_id=1, source_target_pairs={{0,128},{8,136},{16,144},{24,152},{32,160},{40,168},{48,176},{56,1... | collective-permute-start | bytes 196616 | tf_op jit(solution)/shard_map/ppermute | solution.py:25
  60.7 19.9 %collective-permute-start.8 = (f32[16,1024]{1,0:T(8,128)S(1)}, f32[16,1024]{1,0:T(8,128)S(1)}, u32[]{:S(2)}, u32[]{:S(2)}) collective-permute-start(f32[16,1024]{1,0:T(8,128)S(1)} %multiply_add_fusion.1), channel_id=1, source_target_pairs={{0,256},{8,264},{16,272},{24,280},{32,288},{40,296},{48,304},{56,3... | collective-permute-start | bytes 196616 | tf_op jit(solution)/shard_map/ppermute | solution.py:25
  66.0 14.7 %collective-permute-start.9 = (f32[16,1024]{1,0:T(8,128)S(1)}, f32[16,1024]{1,0:T(8,128)S(1)}, u32[]{:S(2)}, u32[]{:S(2)}) collective-permute-start(f32[16,1024]{1,0:T(8,128)S(1)} %multiply_add_fusion.1), channel_id=1, source_target_pairs={{0,384},{8,392},{16,400},{24,408},{32,416},{40,424},{48,432},{56,4... | collective-permute-start | bytes 196616 | tf_op jit(solution)/shard_map/ppermute | solution.py:25
  82.3 17.2 %collective-permute-start.10 = (bf16[64,1024]{1,0:T(8,128)(2,1)S(1)}, bf16[64,1024]{1,0:T(8,128)(2,1)S(1)}, u32[]{:S(2)}, u32[]{:S(2)}) collective-permute-start(bf16[64,1024]{1,0:T(8,128)(2,1)S(1)} %fusion.14), channel_id=1, source_target_pairs={{0,8},{8,16},{16,24},{24,32},{32,40},{40,48},{48,56},{56,0},{1,9},... | collective-permute-start | bytes 393224 | tf_op jit(solution)/shard_map/ppermute | solution.py:17
  84.2 20.0 %collective-permute-start.11 = (bf16[64,1024]{1,0:T(8,128)(2,1)S(1)}, bf16[64,1024]{1,0:T(8,128)(2,1)S(1)}, u32[]{:S(2)}, u32[]{:S(2)}) collective-permute-start(bf16[64,1024]{1,0:T(8,128)(2,1)S(1)} %fusion.14), channel_id=1, source_target_pairs={{0,16},{8,24},{16,32},{24,40},{32,48},{40,56},{48,0},{56,8},{1,17}... | collective-permute-start | bytes 393224 | tf_op jit(solution)/shard_map/ppermute | solution.py:17
  88.7 19.6 %collective-permute-start.12 = (bf16[64,1024]{1,0:T(8,128)(2,1)S(1)}, bf16[64,1024]{1,0:T(8,128)(2,1)S(1)}, u32[]{:S(2)}, u32[]{:S(2)}) collective-permute-start(bf16[64,1024]{1,0:T(8,128)(2,1)S(1)} %fusion.14), channel_id=1, source_target_pairs={{0,24},{8,32},{16,40},{24,48},{32,56},{40,0},{48,8},{56,16},{1,25}... | collective-permute-start | bytes 393224 | tf_op jit(solution)/shard_map/ppermute | solution.py:17
  92.5 16.5 %collective-permute-start.13 = (bf16[64,1024]{1,0:T(8,128)(2,1)S(1)}, bf16[64,1024]{1,0:T(8,128)(2,1)S(1)}, u32[]{:S(2)}, u32[]{:S(2)}) collective-permute-start(bf16[64,1024]{1,0:T(8,128)(2,1)S(1)} %fusion.14), channel_id=1, source_target_pairs={{0,32},{8,40},{16,48},{24,56},{32,0},{40,8},{48,16},{56,24},{1,33}... | collective-permute-start | bytes 393224 | tf_op jit(solution)/shard_map/ppermute | solution.py:17
  94.6 15.0 %collective-permute-start.14 = (bf16[64,1024]{1,0:T(8,128)(2,1)S(1)}, bf16[64,1024]{1,0:T(8,128)(2,1)S(1)}, u32[]{:S(2)}, u32[]{:S(2)}) collective-permute-start(bf16[64,1024]{1,0:T(8,128)(2,1)S(1)} %fusion.14), channel_id=1, source_target_pairs={{0,40},{8,48},{16,56},{24,0},{32,8},{40,16},{48,24},{56,32},{1,41}... | collective-permute-start | bytes 393224 | tf_op jit(solution)/shard_map/ppermute | solution.py:17
  99.5 10.8 %collective-permute-start.15 = (bf16[64,1024]{1,0:T(8,128)(2,1)S(1)}, bf16[64,1024]{1,0:T(8,128)(2,1)S(1)}, u32[]{:S(2)}, u32[]{:S(2)}) collective-permute-start(bf16[64,1024]{1,0:T(8,128)(2,1)S(1)} %fusion.14), channel_id=1, source_target_pairs={{0,48},{8,56},{16,0},{24,8},{32,16},{40,24},{48,32},{56,40},{1,49}... | collective-permute-start | bytes 393224 | tf_op jit(solution)/shard_map/ppermute | solution.py:17
  104.2 6.9 %collective-permute-start.16 = (bf16[64,1024]{1,0:T(8,128)(2,1)S(1)}, bf16[64,1024]{1,0:T(8,128)(2,1)S(1)}, u32[]{:S(2)}, u32[]{:S(2)}) collective-permute-start(bf16[64,1024]{1,0:T(8,128)(2,1)S(1)} %fusion.14), channel_id=1, source_target_pairs={{0,56},{8,0},{16,8},{24,16},{32,24},{40,32},{48,40},{56,48},{1,57}... | collective-permute-start | bytes 393224 | tf_op jit(solution)/shard_map/ppermute | solution.py:17
  115.7 13.9 %collective-permute-start.17 = (f32[8,64,64]{2,1,0:T(8,128)S(1)}, f32[8,64,64]{2,1,0:T(8,128)S(1)}, u32[]{:S(2)}, u32[]{:S(2)}) collective-permute-start(f32[8,64,64]{2,1,0:T(8,128)S(1)} %get-tuple-element.7), channel_id=1, source_target_pairs={{0,1},{1,2},{2,3},{3,4},{4,5},{5,6},{6,7},{7,0},{8,9},{9,10},{10,1... | collective-permute-start | bytes 393224 | tf_op jit(solution)/shard_map/ppermute | solution.py:17
  115.7 17.8 %collective-permute-start.18 = (f32[8,64,64]{2,1,0:T(8,128)S(1)}, f32[8,64,64]{2,1,0:T(8,128)S(1)}, u32[]{:S(2)}, u32[]{:S(2)}) collective-permute-start(f32[8,64,64]{2,1,0:T(8,128)S(1)} %get-tuple-element.13), channel_id=1, source_target_pairs={{0,2},{1,3},{2,4},{3,5},{4,6},{5,7},{6,0},{7,1},{8,10},{9,11},{10,... | collective-permute-start | bytes 393224 | tf_op jit(solution)/shard_map/ppermute | solution.py:17
  118.8 15.5 %collective-permute-start.19 = (f32[8,64,64]{2,1,0:T(8,128)}, f32[8,64,64]{2,1,0:T(8,128)S(1)}, u32[]{:S(2)}, u32[]{:S(2)}) collective-permute-start(f32[8,64,64]{2,1,0:T(8,128)} %get-tuple-element.12), channel_id=1, source_target_pairs={{0,3},{1,4},{2,5},{3,6},{4,7},{5,0},{6,1},{7,2},{8,11},{9,12},{10,... | collective-permute-start | bytes 393224 | tf_op jit(solution)/shard_map/ppermute | solution.py:17
  122.1 17.1 %collective-permute-start.20 = (f32[8,64,64]{2,1,0:T(8,128)}, f32[8,64,64]{2,1,0:T(8,128)S(1)}, u32[]{:S(2)}, u32[]{:S(2)}) collective-permute-start(f32[8,64,64]{2,1,0:T(8,128)} %get-tuple-element.11), channel_id=1, source_target_pairs={{0,4},{1,5},{2,6},{3,7},{4,0},{5,1},{6,2},{7,3},{8,12},{9,13},{10,... | collective-permute-start | bytes 393224 | tf_op jit(solution)/shard_map/ppermute | solution.py:17
  126.7 13.2 %collective-permute-start.21 = (f32[8,64,64]{2,1,0:T(8,128)}, f32[8,64,64]{2,1,0:T(8,128)S(1)}, u32[]{:S(2)}, u32[]{:S(2)}) collective-permute-start(f32[8,64,64]{2,1,0:T(8,128)} %get-tuple-element.10), channel_id=1, source_target_pairs={{0,5},{1,6},{2,7},{3,0},{4,1},{5,2},{6,3},{7,4},{8,13},{9,14},{10,... | collective-permute-start | bytes 393224 | tf_op jit(solution)/shard_map/ppermute | solution.py:17
  129.6 15.8 %collective-permute-start.22 = (f32[8,64,64]{2,1,0:T(8,128)}, f32[8,64,64]{2,1,0:T(8,128)}, u32[]{:S(2)}, u32[]{:S(2)}) collective-permute-start(f32[8,64,64]{2,1,0:T(8,128)} %get-tuple-element.9), channel_id=1, source_target_pairs={{0,6},{1,7},{2,0},{3,1},{4,2},{5,3},{6,4},{7,5},{8,14},{9,15},{10,... | collective-permute-start | bytes 393224 | tf_op jit(solution)/shard_map/ppermute | solution.py:17
  133.5 13.7 %collective-permute-start.23 = (f32[8,64,64]{2,1,0:T(8,128)}, f32[8,64,64]{2,1,0:T(8,128)}, u32[]{:S(2)}, u32[]{:S(2)}) collective-permute-start(f32[8,64,64]{2,1,0:T(8,128)} %get-tuple-element.8), channel_id=1, source_target_pairs={{0,7},{1,0},{2,1},{3,2},{4,3},{5,4},{6,5},{7,6},{8,15},{9,8},{10,9... | collective-permute-start | bytes 393224 | tf_op jit(solution)/shard_map/ppermute | solution.py:17
  148.3 18.6 %collective-permute-start.24 = (bf16[64,64]{1,0:T(8,128)(2,1)S(1)}, bf16[64,64]{1,0:T(8,128)(2,1)S(1)}, u32[]{:S(2)}, u32[]{:S(2)}) collective-permute-start(bf16[64,64]{1,0:T(8,128)(2,1)S(1)} %get-tuple-element.21), channel_id=1, source_target_pairs={{0,56},{8,0},{16,8},{24,16},{32,24},{40,32},{48,40},{56,48},{1,57}... | collective-permute-start | bytes 24584 | tf_op jit(solution)/shard_map/ppermute | solution.py:17
  154.0 18.1 %collective-permute-start.25 = (bf16[64,64]{1,0:T(8,128)(2,1)S(1)}, bf16[64,64]{1,0:T(8,128)(2,1)S(1)}, u32[]{:S(2)}, u32[]{:S(2)}) collective-permute-start(bf16[64,64]{1,0:T(8,128)(2,1)S(1)} %get-tuple-element.20), channel_id=1, source_target_pairs={{0,48},{8,56},{16,0},{24,8},{32,16},{40,24},{48,32},{56,40},{1,49}... | collective-permute-start | bytes 24584 | tf_op jit(solution)/shard_map/ppermute | solution.py:17
  155.9 18.1 %collective-permute-start.26 = (bf16[64,64]{1,0:T(8,128)(2,1)S(1)}, bf16[64,64]{1,0:T(8,128)(2,1)S(1)}, u32[]{:S(2)}, u32[]{:S(2)}) collective-permute-start(bf16[64,64]{1,0:T(8,128)(2,1)S(1)} %get-tuple-element.19), channel_id=1, source_target_pairs={{0,40},{8,48},{16,56},{24,0},{32,8},{40,16},{48,24},{56,32},{1,41}... | collective-permute-start | bytes 24584 | tf_op jit(solution)/shard_map/ppermute | solution.py:17
  160.2 13.9 %collective-permute-start.27 = (bf16[64,64]{1,0:T(8,128)(2,1)S(1)}, bf16[64,64]{1,0:T(8,128)(2,1)S(1)}, u32[]{:S(2)}, u32[]{:S(2)}) collective-permute-start(bf16[64,64]{1,0:T(8,128)(2,1)S(1)} %get-tuple-element.18), channel_id=1, source_target_pairs={{0,32},{8,40},{16,48},{24,56},{32,0},{40,8},{48,16},{56,24},{1,33}... | collective-permute-start | bytes 24584 | tf_op jit(solution)/shard_map/ppermute | solution.py:17
  162.1 12.0 %collective-permute-start.28 = (bf16[64,64]{1,0:T(8,128)(2,1)S(1)}, bf16[64,64]{1,0:T(8,128)(2,1)S(1)}, u32[]{:S(2)}, u32[]{:S(2)}) collective-permute-start(bf16[64,64]{1,0:T(8,128)(2,1)S(1)} %get-tuple-element.17), channel_id=1, source_target_pairs={{0,24},{8,32},{16,40},{24,48},{32,56},{40,0},{48,8},{56,16},{1,25}... | collective-permute-start | bytes 24584 | tf_op jit(solution)/shard_map/ppermute | solution.py:17
  167.0 8.0 %collective-permute-start.29 = (bf16[64,64]{1,0:T(8,128)(2,1)S(1)}, bf16[64,64]{1,0:T(8,128)(2,1)S(1)}, u32[]{:S(2)}, u32[]{:S(2)}) collective-permute-start(bf16[64,64]{1,0:T(8,128)(2,1)S(1)} %get-tuple-element.16), channel_id=1, source_target_pairs={{0,16},{8,24},{16,32},{24,40},{32,48},{40,56},{48,0},{56,8},{1,17}... | collective-permute-start | bytes 24584 | tf_op jit(solution)/shard_map/ppermute | solution.py:17
  172.1 7.7 %collective-permute-start.30 = (bf16[64,64]{1,0:T(8,128)(2,1)S(1)}, bf16[64,64]{1,0:T(8,128)(2,1)S(1)}, u32[]{:S(2)}, u32[]{:S(2)}) collective-permute-start(bf16[64,64]{1,0:T(8,128)(2,1)S(1)} %get-tuple-element.14), channel_id=1, source_target_pairs={{0,8},{8,16},{16,24},{24,32},{32,40},{40,48},{48,56},{56,0},{1,9},... | collective-permute-start | bytes 24584 | tf_op jit(solution)/shard_map/ppermute | solution.py:17
  (2 other events, 23.4 us)
Sparse Core Ops, SparseCore 0:
  11.0 64.3 all-gather.1

commit v3 on v2

--- a/solution.py
+++ b/solution.py
@@ -111,21 +111,14 @@
 
         mixed = (q_lane * (near + far + skip_gain[None, :] * gated_wide)).astype(jnp.bfloat16)
 
-        tokens = [mixed] + [rotated(mixed, "clo", n_lo, by) for by in range(1, n_lo)]
-        tokens = jnp.stack(tokens)
+        spread = jnp.broadcast_to(mixed[None], (n_lo,) + mixed.shape)
+        tokens = lax.all_to_all(spread, "clo", 0, 0, tiled=True)
         partial = jnp.einsum(
             "ktc,cqo->qkto", tokens, weight, preferred_element_type=jnp.float32
         )
-        summed = lax.dynamic_index_in_dim(partial, tp, 0, keepdims=False)
-        for by in range(1, n_tp):
-            piece = lax.dynamic_index_in_dim(partial, (tp + by) % n_tp, 0, keepdims=False)
-            summed = summed + rotated(piece, "tp", n_tp, by)
-        summed = summed.astype(jnp.bfloat16)
-        back = [summed[0]] + [
-            rotated(summed[by], "clo", n_lo, n_lo - by) for by in range(1, n_lo)
-        ]
-        back = jnp.stack(back)
-        back = jnp.roll(back, clo, axis=0)
+        pieces = lax.all_to_all(partial, "tp", 0, 0, tiled=True)
+        summed = jnp.sum(pieces, axis=0).astype(jnp.bfloat16)
+        back = lax.all_to_all(summed, "clo", 0, 0, tiled=True)
         return back.transpose(1, 0, 2).reshape(rows, -1)
 
     return per_device

time: 189 us -> 185 us (0.979)
  the two profiles are of different devices: /device:TPU:32 before, /device:TPU:2 now
where the time goes in v3:
time: 185 us; the launch traced here: 184 us
  waiting for transfers between devices  64.1 us (35%)
  starting transfers between devices  52.4 us (28%)
  blocking collectives  31.7 us (17%)
  between operations  13.9 us (8%)
  local copies, waits for them, and re-layouts  9.62 us (5%)
  other arithmetic  8.77 us (5%)
  matrix products  3.41 us (2%)
    all_gather x1, waiting for transfers between devices, per_device(): weight = lax.all_gather(out_weight, 'chi', axis=1, tiled=True)  52.5 us
    ppermute x9, starting transfers between devices, digit_rotated(): return lax.ppermute(value, CTX, pairs)  45.1 us
    all_to_all x1, blocking collectives, per_device(): pieces = lax.all_to_all(partial, 'tp', 0, 0, tiled=True)  19.1 us
    all_to_all x1, blocking collectives, per_device(): back = lax.all_to_all(summed, 'clo', 0, 0, tiled=True)  12.6 us
    ppermute x9, waiting for transfers between devices, digit_rotated(): return lax.ppermute(value, CTX, pairs)  10.9 us
    all_to_all x1, starting transfers between devices, per_device(): tokens = lax.all_to_all(spread, 'clo', 0, 0, tiled=True)  3.75 us
  transfers between devices with their start and end apart: 12, of which 6 were waited for; matrix products, arithmetic and copies ran while one was open for 3% of the time, Pallas kernels for 0%

profile of v3, /device:TPU:2, one launch (start us, length us, event | category | flops | bytes accessed | tf_op | source)
XLA Modules:
  0.0 183.9 jit_solution(3685164026990246933)
XLA Ops:
  6.5 0.8 slice.29
  7.4 3.5 %collective-permute-start = (bf16[3,2,1024]{2,1,0:T(2,128)(2,1)S(1)}, bf16[3,2,1024]{2,1,0:T(2,128)(2,1)S(1)}, u32[]{:S(2)}, u32[]{:S(2)}) collective-permute-start(bf16[3,2,1024]{2,1,0:T(2,128)(2,1)S(1)} %slice.29), channel_id=1, source_target_pairs={{0,8},{8,16},{16,24},{24,32},{32,40},{40,48},{48,56},{56,64},{64,7... | collective-permute-start | bytes 36872 | tf_op jit(solution)/shard_map/ppermute | solution.py:13
  10.8 0.9 fusion.9
  11.8 0.7 negate_bitcast_fusion
  13.6 1.8 multiply_add_fusion
  15.5 0.7 multiply_reduce_fusion.1
  16.2 3.5 %collective-permute-start.1 = (f32[16,1024]{1,0:T(8,128)S(1)}, f32[16,1024]{1,0:T(8,128)S(1)}, u32[]{:S(2)}, u32[]{:S(2)}) collective-permute-start(f32[16,1024]{1,0:T(8,128)S(1)} %multiply_reduce_fusion.1), channel_id=1, source_target_pairs={{0,8},{8,16},{16,24},{24,0},{32,40},{40,48},{48,56},{56,32},{64,72... | collective-permute-start | bytes 196616 | tf_op jit(solution)/shard_map/ppermute | solution.py:25
  19.7 4.8 %collective-permute-start.2 = (f32[16,1024]{1,0:T(8,128)S(1)}, f32[16,1024]{1,0:T(8,128)S(1)}, u32[]{:S(2)}, u32[]{:S(2)}) collective-permute-start(f32[16,1024]{1,0:T(8,128)S(1)} %multiply_reduce_fusion.1), channel_id=1, source_target_pairs={{0,16},{8,24},{16,0},{24,8},{32,48},{40,56},{48,32},{56,40},{64,80... | collective-permute-start | bytes 196616 | tf_op jit(solution)/shard_map/ppermute | solution.py:25
  24.5 3.0 %collective-permute-start.3 = (f32[16,1024]{1,0:T(8,128)S(1)}, f32[16,1024]{1,0:T(8,128)S(1)}, u32[]{:S(2)}, u32[]{:S(2)}) collective-permute-start(f32[16,1024]{1,0:T(8,128)S(1)} %multiply_reduce_fusion.1), channel_id=1, source_target_pairs={{0,24},{8,0},{16,8},{24,16},{32,56},{40,32},{48,40},{56,48},{64,88... | collective-permute-start | bytes 196616 | tf_op jit(solution)/shard_map/ppermute | solution.py:25
  28.5 1.1 reshape.75
  29.6 1.1 collective-permute-done.3
  30.7 3.8 %collective-permute-start.4 = (f32[16,1024]{1,0:T(8,128)S(1)}, f32[16,1024]{1,0:T(8,128)S(1)}, u32[]{:S(2)}, u32[]{:S(2)}) collective-permute-start(f32[16,1024]{1,0:T(8,128)S(1)} %multiply_add_fusion.2), channel_id=1, source_target_pairs={{0,32},{8,40},{16,48},{24,56},{32,64},{40,72},{48,80},{56,88},{64,... | collective-permute-start | bytes 196616 | tf_op jit(solution)/shard_map/ppermute | solution.py:25
  34.6 6.4 %collective-permute-start.5 = (f32[16,1024]{1,0:T(8,128)S(1)}, f32[16,1024]{1,0:T(8,128)S(1)}, u32[]{:S(2)}, u32[]{:S(2)}) collective-permute-start(f32[16,1024]{1,0:T(8,128)S(1)} %multiply_add_fusion.2), channel_id=1, source_target_pairs={{0,64},{8,72},{16,80},{24,88},{32,96},{40,104},{48,112},{56,120},{... | collective-permute-start | bytes 196616 | tf_op jit(solution)/shard_map/ppermute | solution.py:25
  41.0 1.9 %collective-permute-start.6 = (f32[16,1024]{1,0:T(8,128)S(1)}, f32[16,1024]{1,0:T(8,128)S(1)}, u32[]{:S(2)}, u32[]{:S(2)}) collective-permute-start(f32[16,1024]{1,0:T(8,128)S(1)} %multiply_add_fusion.2), channel_id=1, source_target_pairs={{0,96},{8,104},{16,112},{24,120},{32,0},{40,8},{48,16},{56,24},{64... | collective-permute-start | bytes 196616 | tf_op jit(solution)/shard_map/ppermute | solution.py:25
  43.1 1.3 collective-permute-done.5
  44.4 2.7 %collective-permute-done.6 = f32[16,1024]{1,0:T(8,128)S(1)} collective-permute-done((f32[16,1024]{1,0:T(8,128)S(1)}, f32[16,1024]{1,0:T(8,128)S(1)}, u32[]{:S(2)}, u32[]{:S(2)}) %collective-permute-start.6) | collective-permute-done | bytes 65568 | tf_op jit(solution)/shard_map/ppermute | solution.py:25
  47.2 9.1 %collective-permute-start.7 = (f32[16,1024]{1,0:T(8,128)S(1)}, f32[16,1024]{1,0:T(8,128)S(1)}, u32[]{:S(2)}, u32[]{:S(2)}) collective-permute-start(f32[16,1024]{1,0:T(8,128)S(1)} %multiply_add_fusion.1), channel_id=1, source_target_pairs={{0,128},{8,136},{16,144},{24,152},{32,160},{40,168},{48,176},{56,1... | collective-permute-start | bytes 196616 | tf_op jit(solution)/shard_map/ppermute | solution.py:25
  56.3 7.2 %collective-permute-start.8 = (f32[16,1024]{1,0:T(8,128)S(1)}, f32[16,1024]{1,0:T(8,128)S(1)}, u32[]{:S(2)}, u32[]{:S(2)}) collective-permute-start(f32[16,1024]{1,0:T(8,128)S(1)} %multiply_add_fusion.1), channel_id=1, source_target_pairs={{0,256},{8,264},{16,272},{24,280},{32,288},{40,296},{48,304},{56,3... | collective-permute-start | bytes 196616 | tf_op jit(solution)/shard_map/ppermute | solution.py:25
  63.4 5.5 %collective-permute-start.9 = (f32[16,1024]{1,0:T(8,128)S(1)}, f32[16,1024]{1,0:T(8,128)S(1)}, u32[]{:S(2)}, u32[]{:S(2)}) collective-permute-start(f32[16,1024]{1,0:T(8,128)S(1)} %multiply_add_fusion.1), channel_id=1, source_target_pairs={{0,384},{8,392},{16,400},{24,408},{32,416},{40,424},{48,432},{56,4... | collective-permute-start | bytes 196616 | tf_op jit(solution)/shard_map/ppermute | solution.py:25
  69.8 1.8 collective-permute-done.8
  71.5 4.0 %collective-permute-done.9 = f32[16,1024]{1,0:T(8,128)S(1)} collective-permute-done((f32[16,1024]{1,0:T(8,128)S(1)}, f32[16,1024]{1,0:T(8,128)S(1)}, u32[]{:S(2)}, u32[]{:S(2)}) %collective-permute-start.9) | collective-permute-done | bytes 65568 | tf_op jit(solution)/shard_map/ppermute | solution.py:25
  75.7 1.4 multiply_reduce_fusion
  77.2 1.2 broadcast_in_dim.11
  78.3 3.7 %all-to-all-start = ((bf16[8,64,1024]{2,1,0:T(8,128)(2,1)}), bf16[8,64,1024]{2,1,0:T(8,128)(2,1)S(1)}, u32[]{:S(2)}, u32[]{:S(2)}) async-start(bf16[8,64,1024]{2,1,0:T(8,128)(2,1)} %broadcast_in_dim.11), calls=%async_computation | async-start | bytes 2097152 | tf_op jit(solution)/shard_map/all_to_all | solution.py:115
  82.8 52.5 %all-gather.2.cloned.1.call-done = bf16[1024,512]{0,1:T(8,128)(2,1)} async-done(((bf16[1024,64]{0,1:T(8,128)(2,1)}), bf16[1024,512]{0,1:T(8,128)(2,1)}) %all-gather.2.cloned.1.call-update) | async-done | bytes 1048592 | tf_op jit(solution)/shard_map/all_gather | solution.py:51
  135.3 2.5 %convolution_bitcast_fusion = f32[8,8,64,64]{3,2,0,1:T(8,128)S(1)} fusion(bf16[1024,8,64,1]{0,2,1,3:T(8,128)(2,1)} %bitcast.45, bf16[8,64,1024]{2,1,0:T(8,128)(2,1)S(1)} %all-to-all-done), kind=kOutput, calls=%fused_computation.3 | convolution fusion | flops 536870912 | bytes 3145728 | tf_op jit(solution)/shard_map/ktc,cqo->qkto/dot_general | solution.py:116
  138.1 1.3 reshape.82
  139.4 19.1 %all_to_all.15 = f32[8,1,32768]{2,1,0:T(1,128)S(1)} all-to-all(f32[8,1,32768]{2,1,0:T(1,128)S(1)} %reshape.82), channel_id=1, replica_groups=mesh['chi'=8,'clo'=8,'tp'=8] {'tp'}, dimensions={0} | all-to-all | bytes 2097152 | tf_op jit(solution)/shard_map/all_to_all | solution.py:119
  159.1 3.1 %reduce = f32[8,32768]{1,0:T(8,128)S(1)} reduce(f32[8,1,32768]{2,1,0:T(1,128)S(1)} %all_to_all.15, f32[]{:T(128)} %broadcast.33), dimensions={1}, to_apply=%all_to_all.10.reduce_sub_computation | reduce | bytes 2097156 | tf_op jit(solution)/shard_map/all_to_all | solution.py:119
  162.2 0.8 reshape.83
  163.4 12.6 %all_to_all.16 = bf16[8,2,2048]{2,1,0:T(2,128)(2,1)S(1)} all-to-all(bf16[8,2,2048]{2,1,0:T(2,128)(2,1)S(1)} %reshape.84), channel_id=1, replica_groups=mesh['chi'=8,'clo'=8,'tp'=8] {'clo'}, dimensions={0} | all-to-all | bytes 131072 | tf_op jit(solution)/shard_map/all_to_all | solution.py:121
  176.3 0.8 reshape.78
  (38 shorter events, 5.2 us)
Async XLA Ops:
  7.4 6.2 %collective-permute-start = (bf16[3,2,1024]{2,1,0:T(2,128)(2,1)S(1)}, bf16[3,2,1024]{2,1,0:T(2,128)(2,1)S(1)}, u32[]{:S(2)}, u32[]{:S(2)}) collective-permute-start(bf16[3,2,1024]{2,1,0:T(2,128)(2,1)S(1)} %slice.29), channel_id=1, source_target_pairs={{0,8},{8,16},{16,24},{24,32},{32,40},{40,48},{48,56},{56,64},{64,7... | collective-permute-start | bytes 36872 | tf_op jit(solution)/shard_map/ppermute | solution.py:13
  13.6 13.9 %copy-start = (bf16[64,4096]{1,0:T(8,128)(2,1)S(1)}, bf16[64,4096]{1,0:T(8,128)(2,1)}, u32[]{:S(2)}) copy-start(bf16[64,4096]{1,0:T(8,128)(2,1)} %constant.139.clone) | copy-start | bytes 1572868
  16.2 13.4 %collective-permute-start.1 = (f32[16,1024]{1,0:T(8,128)S(1)}, f32[16,1024]{1,0:T(8,128)S(1)}, u32[]{:S(2)}, u32[]{:S(2)}) collective-permute-start(f32[16,1024]{1,0:T(8,128)S(1)} %multiply_reduce_fusion.1), channel_id=1, source_target_pairs={{0,8},{8,16},{16,24},{24,0},{32,40},{40,48},{48,56},{56,32},{64,72... | collective-permute-start | bytes 196616 | tf_op jit(solution)/shard_map/ppermute | solution.py:25
  19.7 9.9 %collective-permute-start.2 = (f32[16,1024]{1,0:T(8,128)S(1)}, f32[16,1024]{1,0:T(8,128)S(1)}, u32[]{:S(2)}, u32[]{:S(2)}) collective-permute-start(f32[16,1024]{1,0:T(8,128)S(1)} %multiply_reduce_fusion.1), channel_id=1, source_target_pairs={{0,16},{8,24},{16,0},{24,8},{32,48},{40,56},{48,32},{56,40},{64,80... | collective-permute-start | bytes 196616 | tf_op jit(solution)/shard_map/ppermute | solution.py:25
  24.5 6.2 %collective-permute-start.3 = (f32[16,1024]{1,0:T(8,128)S(1)}, f32[16,1024]{1,0:T(8,128)S(1)}, u32[]{:S(2)}, u32[]{:S(2)}) collective-permute-start(f32[16,1024]{1,0:T(8,128)S(1)} %multiply_reduce_fusion.1), channel_id=1, source_target_pairs={{0,24},{8,0},{16,8},{24,16},{32,56},{40,32},{48,40},{56,48},{64,88... | collective-permute-start | bytes 196616 | tf_op jit(solution)/shard_map/ppermute | solution.py:25
  30.7 12.3 %collective-permute-start.4 = (f32[16,1024]{1,0:T(8,128)S(1)}, f32[16,1024]{1,0:T(8,128)S(1)}, u32[]{:S(2)}, u32[]{:S(2)}) collective-permute-start(f32[16,1024]{1,0:T(8,128)S(1)} %multiply_add_fusion.2), channel_id=1, source_target_pairs={{0,32},{8,40},{16,48},{24,56},{32,64},{40,72},{48,80},{56,88},{64,... | collective-permute-start | bytes 196616 | tf_op jit(solution)/shard_map/ppermute | solution.py:25
  34.6 9.8 %collective-permute-start.5 = (f32[16,1024]{1,0:T(8,128)S(1)}, f32[16,1024]{1,0:T(8,128)S(1)}, u32[]{:S(2)}, u32[]{:S(2)}) collective-permute-start(f32[16,1024]{1,0:T(8,128)S(1)} %multiply_add_fusion.2), channel_id=1, source_target_pairs={{0,64},{8,72},{16,80},{24,88},{32,96},{40,104},{48,112},{56,120},{... | collective-permute-start | bytes 196616 | tf_op jit(solution)/shard_map/ppermute | solution.py:25
  41.0 6.2 %collective-permute-start.6 = (f32[16,1024]{1,0:T(8,128)S(1)}, f32[16,1024]{1,0:T(8,128)S(1)}, u32[]{:S(2)}, u32[]{:S(2)}) collective-permute-start(f32[16,1024]{1,0:T(8,128)S(1)} %multiply_add_fusion.2), channel_id=1, source_target_pairs={{0,96},{8,104},{16,112},{24,120},{32,0},{40,8},{48,16},{56,24},{64... | collective-permute-start | bytes 196616 | tf_op jit(solution)/shard_map/ppermute | solution.py:25
  47.2 22.6 %collective-permute-start.7 = (f32[16,1024]{1,0:T(8,128)S(1)}, f32[16,1024]{1,0:T(8,128)S(1)}, u32[]{:S(2)}, u32[]{:S(2)}) collective-permute-start(f32[16,1024]{1,0:T(8,128)S(1)} %multiply_add_fusion.1), channel_id=1, source_target_pairs={{0,128},{8,136},{16,144},{24,152},{32,160},{40,168},{48,176},{56,1... | collective-permute-start | bytes 196616 | tf_op jit(solution)/shard_map/ppermute | solution.py:25
  56.3 15.2 %collective-permute-start.8 = (f32[16,1024]{1,0:T(8,128)S(1)}, f32[16,1024]{1,0:T(8,128)S(1)}, u32[]{:S(2)}, u32[]{:S(2)}) collective-permute-start(f32[16,1024]{1,0:T(8,128)S(1)} %multiply_add_fusion.1), channel_id=1, source_target_pairs={{0,256},{8,264},{16,272},{24,280},{32,288},{40,296},{48,304},{56,3... | collective-permute-start | bytes 196616 | tf_op jit(solution)/shard_map/ppermute | solution.py:25
  63.4 12.1 %collective-permute-start.9 = (f32[16,1024]{1,0:T(8,128)S(1)}, f32[16,1024]{1,0:T(8,128)S(1)}, u32[]{:S(2)}, u32[]{:S(2)}) collective-permute-start(f32[16,1024]{1,0:T(8,128)S(1)} %multiply_add_fusion.1), channel_id=1, source_target_pairs={{0,384},{8,392},{16,400},{24,408},{32,416},{40,424},{48,432},{56,4... | collective-permute-start | bytes 196616 | tf_op jit(solution)/shard_map/ppermute | solution.py:25
  69.5 7.5 %copy-start.1 = (f32[1024]{0:T(1024)S(1)}, f32[1024]{0:T(1024)}, u32[]{:S(2)}) copy-start(f32[1024]{0:T(1024)} %param.11) | copy-start | bytes 12292
  78.3 57.0 %all-to-all-start = ((bf16[8,64,1024]{2,1,0:T(8,128)(2,1)}), bf16[8,64,1024]{2,1,0:T(8,128)(2,1)S(1)}, u32[]{:S(2)}, u32[]{:S(2)}) async-start(bf16[8,64,1024]{2,1,0:T(8,128)(2,1)} %broadcast_in_dim.11), calls=%async_computation | async-start | bytes 2097152 | tf_op jit(solution)/shard_map/all_to_all | solution.py:115
  82.1 53.2 %all-gather.2.cloned.1.call-start = ((), (), s32[]{:S(2)}) async-start(), calls=%async_computation.3 | async-start | bytes 1179648 | tf_op jit(solution)/shard_map/all_gather | solution.py:51
Sparse Core Ops, SparseCore 0:
  85.0 50.3 all-gather.1

commit v4 on v1

--- a/solution.py
+++ b/solution.py
@@ -4,6 +4,7 @@
 from jax import lax
 from jax.sharding import Mesh
 from jax.sharding import PartitionSpec as P
+
 
 CTX = ("chi", "clo")
 
@@ -20,9 +21,13 @@
         rows = features.shape[1]
         chans = features.shape[2]
         groups = decay_rate.shape[0]
-        modes = decay_rate.shape[1]
         width = chans // groups
         taps = short_weight.shape[1]
+        chi = lax.axis_index("chi")
+        clo = lax.axis_index("clo")
+        me = chi * n_lo + clo
+
+        weight = lax.all_gather(out_weight, "clo", axis=1, tiled=True)
 
         rim = shifted(features[:, rows - (taps - 1) :, :], CTX, n_ctx, 1)
         extended = jnp.concatenate([rim, features], axis=1)
@@ -57,26 +62,40 @@
 
         rate_c = jnp.repeat(decay_rate.T, width, axis=1)
         coef_c = jnp.repeat(coef.T, width, axis=1)
+
+        def decay(blocks):
+            return jnp.exp(-rate_c * (rows * blocks.astype(jnp.float32)))
+
         end_basis = jnp.exp(-rate_c[None] * (rows - 1.0 - lags)[:, None, None])
         own_state = jnp.sum(end_basis * gated_wide[:, None, :], axis=0)
-        state = shifted(own_state, CTX, n_ctx, 1)
-        by = 1
-        while by < n_ctx:
-            decay = jnp.exp(-rate_c * float(rows * by))
-            state = state + decay * shifted(state, CTX, n_ctx, by)
-            by *= 2
+        before = jnp.zeros_like(own_state)
+        total = own_state
+        stride = 1
+        for axis, size, digit in (("clo", n_lo, clo), ("chi", n_tp, chi)):
+            spread = jnp.broadcast_to(total[None], (size,) + total.shape)
+            got = lax.all_to_all(spread, axis, 0, 0, tiled=True)
+            src_digit = jnp.arange(size)
+            gap = (digit - src_digit - 1) * stride + me % stride
+            weight_in = jnp.where(
+                (src_digit < digit)[:, None, None],
+                decay(jnp.maximum(gap, 0)[:, None, None]),
+                0.0,
+            )
+            before = before + jnp.sum(weight_in * got, axis=0)
+            total = jnp.sum(decay(((size - 1 - src_digit) * stride)[:, None, None]) * got, axis=0)
+            stride *= size
         far_basis = coef_c[None] * jnp.exp(-rate_c[None] * (lags + 1.0)[:, None, None])
-        far = jnp.sum(far_basis * state[None], axis=1)
+        far = jnp.sum(far_basis * before[None], axis=1)
 
         mixed = (q_lane * (near + far + skip_gain[None, :] * gated_wide)).astype(jnp.bfloat16)
 
-        tokens = lax.all_gather(mixed, "chi", axis=0)
-        weight = lax.all_gather(out_weight, "clo", axis=1, tiled=True)
+        spread = jnp.broadcast_to(mixed[None], (n_tp,) + mixed.shape)
+        tokens = lax.all_to_all(spread, "chi", 0, 0, tiled=True)
         partial = jnp.einsum(
             "ktc,co->kto", tokens, weight, preferred_element_type=jnp.float32
         )
-        block = lax.psum_scatter(partial, "tp", scatter_dimension=0, tiled=False)
-        block = block.astype(jnp.bfloat16)
+        pieces = lax.all_to_all(partial, "tp", 0, 0, tiled=True)
+        block = jnp.sum(pieces, axis=0).astype(jnp.bfloat16)
         swap = [(a * n_tp + b, b * n_tp + a) for a in range(n_tp) for b in range(n_tp)]
         return lax.ppermute(block, ("chi", "tp"), swap)
 

time: 211 us -> 195 us (0.924)
  the two profiles are of different devices: /device:TPU:4 before, /device:TPU:2 now
where the time goes in v4:
time: 195 us; the launch traced here: 194 us
  waiting for transfers between devices  106 us (54%)
  starting transfers between devices  40.9 us (21%)
  blocking collectives  19.2 us (10%)
  between operations  13.6 us (7%)
  local copies, waits for them, and re-layouts  7.91 us (4%)
  other arithmetic  4.28 us (2%)
  matrix products  2.89 us (1%)
    all_gather x1, waiting for transfers between devices, per_device(): weight = lax.all_gather(out_weight, 'clo', axis=1, tiled=True)  65.7 us
    all_to_all x2, waiting for transfers between devices, per_device(): got = lax.all_to_all(spread, axis, 0, 0, tiled=True)  29.7 us
    all_to_all x2, starting transfers between devices, per_device(): got = lax.all_to_all(spread, axis, 0, 0, tiled=True)  21.3 us
    all_to_all x1, blocking collectives, per_device(): pieces = lax.all_to_all(partial, 'tp', 0, 0, tiled=True)  19.2 us
    ppermute x1, waiting for transfers between devices, per_device(): return lax.ppermute(block, ('chi', 'tp'), swap)  9.54 us
    all_to_all x1, starting transfers between devices, per_device(): tokens = lax.all_to_all(spread, 'chi', 0, 0, tiled=True)  8.78 us
    ppermute x1, starting transfers between devices, per_device(): return lax.ppermute(block, ('chi', 'tp'), swap)  7.32 us
  transfers between devices with their start and end apart: 6, of which 4 were waited for; matrix products, arithmetic and copies ran while one was open for 3% of the time, Pallas kernels for 0%

profile of v4, /device:TPU:2, one launch (start us, length us, event | category | flops | bytes accessed | tf_op | source)
XLA Modules:
  0.0 194.4 jit_solution(7490007412991477736)
XLA Ops:
  6.5 0.9 slice.29
  7.4 3.5 %collective-permute-start = (bf16[3,2,1024]{2,1,0:T(2,128)(2,1)S(1)}, bf16[3,2,1024]{2,1,0:T(2,128)(2,1)S(1)}, u32[]{:S(2)}, u32[]{:S(2)}) collective-permute-start(bf16[3,2,1024]{2,1,0:T(2,128)(2,1)S(1)} %slice.29), channel_id=1, source_target_pairs={{0,8},{8,16},{16,24},{24,32},{32,40},{40,48},{48,56},{56,64},{64,7... | collective-permute-start | bytes 36872 | tf_op jit(solution)/shard_map/ppermute | solution.py:14
  10.9 0.9 fusion.10
  11.9 0.7 negate_bitcast_fusion
  12.7 0.2 broadcast_in_dim.31
  12.8 0.3 neg.28
  13.1 0.3 multiply_add_fusion
  13.5 0.7 multiply_reduce_fusion.1
  14.2 0.8 broadcast_in_dim.34
  15.1 5.7 %all-to-all-start = ((f32[8,16,1024]{2,1,0:T(8,128)}), f32[8,16,1024]{2,1,0:T(8,128)S(1)}, u32[]{:S(2)}, u32[]{:S(2)}) async-start(f32[8,16,1024]{2,1,0:T(8,128)} %broadcast_in_dim.34), calls=%async_computation | async-start | bytes 1048576 | tf_op jit(solution)/shard_map/all_to_all | solution.py:76
  20.8 9.3 %all-to-all-done = f32[8,16,1024]{2,1,0:T(8,128)S(1)} async-done(((f32[8,16,1024]{2,1,0:T(8,128)}), f32[8,16,1024]{2,1,0:T(8,128)S(1)}, u32[]{:S(2)}, u32[]{:S(2)}) %all-to-all-start) | async-done | bytes 524320 | tf_op jit(solution)/shard_map/all_to_all | solution.py:76
  30.1 0.3 multiply_reduce_fusion.3
  30.4 0.8 broadcast_in_dim.36
  31.3 15.6 %all-to-all-start.1 = ((f32[8,16,1024]{2,1,0:T(8,128)}), f32[8,16,1024]{2,1,0:T(8,128)S(1)}, u32[]{:S(2)}, u32[]{:S(2)}) async-start(f32[8,16,1024]{2,1,0:T(8,128)} %broadcast_in_dim.36), calls=%async_computation.1 | async-start | bytes 1048576 | tf_op jit(solution)/shard_map/all_to_all | solution.py:76
  47.0 0.2 broadcast_in_dim.30
  47.2 0.3 mul.230
  47.5 0.4 multiply_reduce_fusion.5
  47.9 0.3 convolution_convert_fusion
  48.2 1.1 reshape.114
  49.5 0.6 fusion.11
  50.2 0.2 copy.29
  50.4 20.3 %all-to-all-done.1 = f32[8,16,1024]{2,1,0:T(8,128)S(1)} async-done(((f32[8,16,1024]{2,1,0:T(8,128)}), f32[8,16,1024]{2,1,0:T(8,128)S(1)}, u32[]{:S(2)}, u32[]{:S(2)}) %all-to-all-start.1) | async-done | bytes 524320 | tf_op jit(solution)/shard_map/all_to_all | solution.py:76
  70.9 1.4 multiply_reduce_fusion
  72.4 1.2 broadcast_in_dim.68
  73.6 8.8 %all-to-all-start.2 = ((bf16[8,64,1024]{2,1,0:T(8,128)(2,1)}), bf16[8,64,1024]{2,1,0:T(8,128)(2,1)S(1)}, u32[]{:S(2)}, u32[]{:S(2)}) async-start(bf16[8,64,1024]{2,1,0:T(8,128)(2,1)} %broadcast_in_dim.68), calls=%async_computation.2 | async-start | bytes 2097152 | tf_op jit(solution)/shard_map/all_to_all | solution.py:93
  82.4 0.7 all-gather.2.cloned.1.call-update
  83.1 65.7 %all-gather.2.cloned.1.call-done = bf16[1024,512]{0,1:T(8,128)(2,1)} async-done(((bf16[1024,64]{0,1:T(8,128)(2,1)}), bf16[1024,512]{0,1:T(8,128)(2,1)}) %all-gather.2.cloned.1.call-update) | async-done | bytes 1048592 | tf_op jit(solution)/shard_map/all_gather | solution.py:30
  148.8 2.0 %fusion = f32[8,64,512]{2,1,0:T(8,128)S(1)} fusion(bf16[8,64,1024]{2,1,0:T(8,128)(2,1)S(1)} %all-to-all-done.2, bf16[1024,512]{0,1:T(8,128)(2,1)} %all-gather.2.cloned.1.call-done), kind=kOutput, calls=%fused_computation.3 | convolution fusion | flops 536870912 | bytes 3145728 | tf_op jit(solution)/shard_map/ktc,co->kto/dot_general | solution.py:94
  150.8 19.2 %all_to_all.20 = f32[8,64,512]{2,1,0:T(8,128)S(1)} all-to-all(f32[8,64,512]{2,1,0:T(8,128)S(1)} %fusion), channel_id=1, replica_groups=mesh['chi'=8,'clo'=8,'tp'=8] {'tp'}, dimensions={0} | all-to-all | bytes 2097152 | tf_op jit(solution)/shard_map/all_to_all | solution.py:97
  170.1 7.3 %collective-permute-start.1 = (bf16[64,512]{1,0:T(8,128)(2,1)S(1)}, bf16[64,512]{1,0:T(8,128)(2,1)S(1)}, u32[]{:S(2)}, u32[]{:S(2)}) collective-permute-start(bf16[64,512]{1,0:T(8,128)(2,1)S(1)} %reduce_sum.72), channel_id=1, source_target_pairs={{0,0},{1,64},{2,128},{3,192},{4,256},{5,320},{6,384},{7,448},{64,1... | collective-permute-start | bytes 196616 | tf_op jit(solution)/shard_map/ppermute | solution.py:100
  177.4 9.5 %collective-permute-done.1 = bf16[64,512]{1,0:T(8,128)(2,1)S(1)} collective-permute-done((bf16[64,512]{1,0:T(8,128)(2,1)S(1)}, bf16[64,512]{1,0:T(8,128)(2,1)S(1)}, u32[]{:S(2)}, u32[]{:S(2)}) %collective-permute-start.1) | collective-permute-done | bytes 65568 | tf_op jit(solution)/shard_map/ppermute | solution.py:100
  187.0 0.6 copy.38
  (25 shorter events, 0.8 us)
Async XLA Ops:
  6.5 6.6 %copy-start.1 = (bf16[3,64,1024]{2,1,0:T(8,128)(2,1)S(1)}, bf16[3,64,1024]{2,1,0:T(8,128)(2,1)}, u32[]{:S(2)}) copy-start(bf16[3,64,1024]{2,1,0:T(8,128)(2,1)} %param.7) | copy-start | bytes 1179652
  7.4 5.7 %collective-permute-start = (bf16[3,2,1024]{2,1,0:T(2,128)(2,1)S(1)}, bf16[3,2,1024]{2,1,0:T(2,128)(2,1)S(1)}, u32[]{:S(2)}, u32[]{:S(2)}) collective-permute-start(bf16[3,2,1024]{2,1,0:T(2,128)(2,1)S(1)} %slice.29), channel_id=1, source_target_pairs={{0,8},{8,16},{16,24},{24,32},{32,40},{40,48},{48,56},{56,64},{64,7... | collective-permute-start | bytes 36872 | tf_op jit(solution)/shard_map/ppermute | solution.py:14
  15.1 15.0 %all-to-all-start = ((f32[8,16,1024]{2,1,0:T(8,128)}), f32[8,16,1024]{2,1,0:T(8,128)S(1)}, u32[]{:S(2)}, u32[]{:S(2)}) async-start(f32[8,16,1024]{2,1,0:T(8,128)} %broadcast_in_dim.34), calls=%async_computation | async-start | bytes 1048576 | tf_op jit(solution)/shard_map/all_to_all | solution.py:76
  31.3 16.6 %copy-start = (bf16[64,4096]{1,0:T(8,128)(2,1)S(1)}, bf16[64,4096]{1,0:T(8,128)(2,1)}, u32[]{:S(2)}) copy-start(bf16[64,4096]{1,0:T(8,128)(2,1)} %constant.50.clone) | copy-start | bytes 1572868
  31.3 39.4 %all-to-all-start.1 = ((f32[8,16,1024]{2,1,0:T(8,128)}), f32[8,16,1024]{2,1,0:T(8,128)S(1)}, u32[]{:S(2)}, u32[]{:S(2)}) async-start(f32[8,16,1024]{2,1,0:T(8,128)} %broadcast_in_dim.36), calls=%async_computation.1 | async-start | bytes 1048576 | tf_op jit(solution)/shard_map/all_to_all | solution.py:76
  70.9 1.4 copy-start.2
  73.6 75.2 %all-to-all-start.2 = ((bf16[8,64,1024]{2,1,0:T(8,128)(2,1)}), bf16[8,64,1024]{2,1,0:T(8,128)(2,1)S(1)}, u32[]{:S(2)}, u32[]{:S(2)}) async-start(bf16[8,64,1024]{2,1,0:T(8,128)(2,1)} %broadcast_in_dim.68), calls=%async_computation.2 | async-start | bytes 2097152 | tf_op jit(solution)/shard_map/all_to_all | solution.py:93
  82.4 66.4 %all-gather.2.cloned.1.call-start = ((), (), s32[]{:S(2)}) async-start(), calls=%async_computation.4 | async-start | bytes 1179648 | tf_op jit(solution)/shard_map/all_gather | solution.py:30
  170.1 16.9 %collective-permute-start.1 = (bf16[64,512]{1,0:T(8,128)(2,1)S(1)}, bf16[64,512]{1,0:T(8,128)(2,1)S(1)}, u32[]{:S(2)}, u32[]{:S(2)}) collective-permute-start(bf16[64,512]{1,0:T(8,128)(2,1)S(1)} %reduce_sum.72), channel_id=1, source_target_pairs={{0,0},{1,64},{2,128},{3,192},{4,256},{5,320},{6,384},{7,448},{64,1... | collective-permute-start | bytes 196616 | tf_op jit(solution)/shard_map/ppermute | solution.py:100
Sparse Core Ops, SparseCore 0:
  85.3 63.4 all-gather.1

commit v5 on v1

--- a/solution.py
+++ b/solution.py
@@ -4,6 +4,7 @@
 from jax import lax
 from jax.sharding import Mesh
 from jax.sharding import PartitionSpec as P
+
 
 CTX = ("chi", "clo")
 
@@ -20,9 +21,12 @@
         rows = features.shape[1]
         chans = features.shape[2]
         groups = decay_rate.shape[0]
-        modes = decay_rate.shape[1]
         width = chans // groups
         taps = short_weight.shape[1]
+        clo = lax.axis_index("clo")
+
+        weight = lax.all_gather(out_weight, "chi", axis=1, tiled=True)
+        weight = weight.reshape(chans, n_tp, -1)
 
         rim = shifted(features[:, rows - (taps - 1) :, :], CTX, n_ctx, 1)
         extended = jnp.concatenate([rim, features], axis=1)
@@ -57,28 +61,44 @@
 
         rate_c = jnp.repeat(decay_rate.T, width, axis=1)
         coef_c = jnp.repeat(coef.T, width, axis=1)
+
+        def decay(blocks):
+            return jnp.exp(-rate_c * (rows * jnp.asarray(blocks, jnp.float32)))
+
         end_basis = jnp.exp(-rate_c[None] * (rows - 1.0 - lags)[:, None, None])
         own_state = jnp.sum(end_basis * gated_wide[:, None, :], axis=0)
-        state = shifted(own_state, CTX, n_ctx, 1)
+
+        spread = jnp.broadcast_to(own_state[None], (n_lo,) + own_state.shape)
+        got = lax.all_to_all(spread, "clo", 0, 0, tiled=True)
+        src = jnp.arange(n_lo)
+        gap = jnp.maximum(clo - src - 1, 0)[:, None, None]
+        inside = jnp.where((src < clo)[:, None, None], decay(gap), 0.0)
+        before = jnp.sum(inside * got, axis=0)
+        group_total = jnp.sum(decay((n_lo - 1 - src)[:, None, None]) * got, axis=0)
+        carried = group_total
+        earlier = jnp.zeros_like(group_total)
         by = 1
-        while by < n_ctx:
-            decay = jnp.exp(-rate_c * float(rows * by))
-            state = state + decay * shifted(state, CTX, n_ctx, by)
+        while by < n_tp:
+            came = shifted(carried, "chi", n_tp, by)
+            earlier = earlier + decay(n_lo * (by - 1)) * came
+            carried = carried + decay(n_lo * by) * came
             by *= 2
+        before = before + decay(clo) * earlier
+
         far_basis = coef_c[None] * jnp.exp(-rate_c[None] * (lags + 1.0)[:, None, None])
-        far = jnp.sum(far_basis * state[None], axis=1)
+        far = jnp.sum(far_basis * before[None], axis=1)
 
         mixed = (q_lane * (near + far + skip_gain[None, :] * gated_wide)).astype(jnp.bfloat16)
 
-        tokens = lax.all_gather(mixed, "chi", axis=0)
-        weight = lax.all_gather(out_weight, "clo", axis=1, tiled=True)
+        spread = jnp.broadcast_to(mixed[None], (n_lo,) + mixed.shape)
+        tokens = lax.all_to_all(spread, "clo", 0, 0, tiled=True)
         partial = jnp.einsum(
-            "ktc,co->kto", tokens, weight, preferred_element_type=jnp.float32
+            "ktc,cqo->qkto", tokens, weight, preferred_element_type=jnp.float32
         )
-        block = lax.psum_scatter(partial, "tp", scatter_dimension=0, tiled=False)
-        block = block.astype(jnp.bfloat16)
-        swap = [(a * n_tp + b, b * n_tp + a) for a in range(n_tp) for b in range(n_tp)]
-        return lax.ppermute(block, ("chi", "tp"), swap)
+        pieces = lax.all_to_all(partial, "tp", 0, 0, tiled=True)
+        summed = jnp.sum(pieces, axis=0).astype(jnp.bfloat16)
+        back = lax.all_to_all(summed, "clo", 0, 0, tiled=True)
+        return back.transpose(1, 0, 2).reshape(rows, -1)
 
     return per_device
 

time: 211 us -> 183 us (0.87)
  the two profiles are of different devices: /device:TPU:4 before, /device:TPU:2 now
where the time goes in v5:
time: 183 us; the launch traced here: 182 us
  waiting for transfers between devices  68.8 us (38%)
  starting transfers between devices  45 us (25%)
  blocking collectives  31.7 us (17%)
  between operations  13.7 us (7%)
  local copies, waits for them, and re-layouts  10.5 us (6%)
  other arithmetic  8.98 us (5%)
  matrix products  3.4 us (2%)
    all_gather x1, waiting for transfers between devices, per_device(): weight = lax.all_gather(out_weight, 'chi', axis=1, tiled=True)  56.6 us
    ppermute x4, starting transfers between devices, shifted(): return lax.ppermute(value, axis, pairs)  35.3 us
    all_to_all x1, blocking collectives, per_device(): pieces = lax.all_to_all(partial, 'tp', 0, 0, tiled=True)  19.1 us
    all_to_all x1, blocking collectives, per_device(): back = lax.all_to_all(summed, 'clo', 0, 0, tiled=True)  12.6 us
    all_to_all x1, waiting for transfers between devices, per_device(): got = lax.all_to_all(spread, 'clo', 0, 0, tiled=True)  8.78 us
    all_to_all x1, starting transfers between devices, per_device(): got = lax.all_to_all(spread, 'clo', 0, 0, tiled=True)  5.71 us
    all_to_all x1, starting transfers between devices, per_device(): tokens = lax.all_to_all(spread, 'clo', 0, 0, tiled=True)  3.96 us
  transfers between devices with their start and end apart: 7, of which 4 were waited for; matrix products, arithmetic and copies ran while one was open for 3% of the time, Pallas kernels for 0%

profile of v5, /device:TPU:2, one launch (start us, length us, event | category | flops | bytes accessed | tf_op | source)
XLA Modules:
  0.0 182.0 jit_solution(5821595520119395975)
XLA Ops:
  6.5 0.8 slice.29
  7.4 3.5 %collective-permute-start = (bf16[3,2,1024]{2,1,0:T(2,128)(2,1)S(1)}, bf16[3,2,1024]{2,1,0:T(2,128)(2,1)S(1)}, u32[]{:S(2)}, u32[]{:S(2)}) collective-permute-start(bf16[3,2,1024]{2,1,0:T(2,128)(2,1)S(1)} %slice.29), channel_id=1, source_target_pairs={{0,8},{8,16},{16,24},{24,32},{32,40},{40,48},{48,56},{56,64},{64,7... | collective-permute-start | bytes 36872 | tf_op jit(solution)/shard_map/ppermute | solution.py:14
  10.8 0.9 fusion.9
  11.8 0.7 negate_bitcast_fusion
  13.1 1.8 %multiply_add_fusion = f32[3,64,1024]{2,1,0:T(8,128)S(1)} fusion(bf16[3,64,1024]{2,1,0:T(8,128)(2,1)} %param.7, bf16[3,2,1024]{2,1,0:T(2,128)(2,1)S(1)} %collective-permute-done, f32[3,1024]{1,0:T(4,128)S(1)} %get-tuple-element.15, f32[3,1024]{1,0:T(4,128)S(1)} %get-tuple-element.16, f32[3,1024]{1,0:T(4,128)S(1)} %bitcast.44), kind=kLoop, calls=%fused_computation.5 | loop fusion | flops 2752512 | bytes 1228800 | tf_op jit(solution)/shard_map/add | solution.py:35
  14.9 0.7 multiply_reduce_fusion.1
  15.7 0.8 broadcast_in_dim.26
  16.5 5.7 %all-to-all-start = ((f32[8,16,1024]{2,1,0:T(8,128)}), f32[8,16,1024]{2,1,0:T(8,128)S(1)}, u32[]{:S(2)}, u32[]{:S(2)}) async-start(f32[8,16,1024]{2,1,0:T(8,128)} %broadcast_in_dim.26), calls=%async_computation | async-start | bytes 1048576 | tf_op jit(solution)/shard_map/all_to_all | solution.py:72
  22.4 0.4 multiply_reduce_fusion.4
  22.8 8.8 %all-to-all-done = f32[8,16,1024]{2,1,0:T(8,128)S(1)} async-done(((f32[8,16,1024]{2,1,0:T(8,128)}), f32[8,16,1024]{2,1,0:T(8,128)S(1)}, u32[]{:S(2)}, u32[]{:S(2)}) %all-to-all-start) | async-done | bytes 524320 | tf_op jit(solution)/shard_map/all_to_all | solution.py:72
  31.6 0.3 multiply_reduce_fusion.2
  31.9 6.4 %collective-permute-start.1 = (f32[16,1024]{1,0:T(8,128)S(1)}, f32[16,1024]{1,0:T(8,128)S(1)}, u32[]{:S(2)}, u32[]{:S(2)}) collective-permute-start(f32[16,1024]{1,0:T(8,128)S(1)} %get-tuple-element.5), channel_id=1, source_target_pairs={{0,64},{64,128},{128,192},{192,256},{256,320},{320,384},{384,448},... | collective-permute-start | bytes 196616 | tf_op jit(solution)/shard_map/ppermute | solution.py:14
  38.3 0.3 convolution_convert_fusion
  39.1 1.1 reshape.99
  40.2 9.5 %collective-permute-start.2 = (f32[16,1024]{1,0:T(8,128)S(1)}, f32[16,1024]{1,0:T(8,128)S(1)}, u32[]{:S(2)}, u32[]{:S(2)}) collective-permute-start(f32[16,1024]{1,0:T(8,128)S(1)} %multiply_add_fusion.3), channel_id=1, source_target_pairs={{0,128},{64,192},{128,256},{192,320},{256,384},{320,448},{1,129},{... | collective-permute-start | bytes 196616 | tf_op jit(solution)/shard_map/ppermute | solution.py:14
  50.0 1.7 collective-permute-done.2
  51.7 15.9 %collective-permute-start.3 = (f32[16,1024]{1,0:T(8,128)S(1)}, f32[16,1024]{1,0:T(8,128)S(1)}, u32[]{:S(2)}, u32[]{:S(2)}) collective-permute-start(f32[16,1024]{1,0:T(8,128)S(1)} %multiply_add_fusion.2), channel_id=1, source_target_pairs={{0,256},{64,320},{128,384},{192,448},{1,257},{65,321},{129,385},{1... | collective-permute-start | bytes 196616 | tf_op jit(solution)/shard_map/ppermute | solution.py:14
  67.6 0.6 fusion.10
  68.5 1.0 collective-permute-done.3
  69.5 1.4 multiply_reduce_fusion
  71.0 1.2 broadcast_in_dim.28
  72.2 4.0 %all-to-all-start.1 = ((bf16[8,64,1024]{2,1,0:T(8,128)(2,1)}), bf16[8,64,1024]{2,1,0:T(8,128)(2,1)S(1)}, u32[]{:S(2)}, u32[]{:S(2)}) async-start(bf16[8,64,1024]{2,1,0:T(8,128)(2,1)} %broadcast_in_dim.28), calls=%async_computation.1 | async-start | bytes 2097152 | tf_op jit(solution)/shard_map/all_to_all | solution.py:94
  76.2 0.7 all-gather.2.cloned.1.call-update
  76.9 56.6 %all-gather.2.cloned.1.call-done = bf16[1024,512]{0,1:T(8,128)(2,1)} async-done(((bf16[1024,64]{0,1:T(8,128)(2,1)}), bf16[1024,512]{0,1:T(8,128)(2,1)}) %all-gather.2.cloned.1.call-update) | async-done | bytes 1048592 | tf_op jit(solution)/shard_map/all_gather | solution.py:28
  133.5 2.5 %convolution_bitcast_fusion = f32[8,8,64,64]{3,2,0,1:T(8,128)S(1)} fusion(bf16[1024,8,64,1]{0,2,1,3:T(8,128)(2,1)} %bitcast.45, bf16[8,64,1024]{2,1,0:T(8,128)(2,1)S(1)} %all-to-all-done.1), kind=kOutput, calls=%fused_computation.3 | convolution fusion | flops 536870912 | bytes 3145728 | tf_op jit(solution)/shard_map/ktc,cqo->qkto/dot_general | solution.py:95
  136.2 1.3 reshape.106
  137.6 19.1 %all_to_all.20 = f32[8,1,32768]{2,1,0:T(1,128)S(1)} all-to-all(f32[8,1,32768]{2,1,0:T(1,128)S(1)} %reshape.106), channel_id=1, replica_groups=mesh['chi'=8,'clo'=8,'tp'=8] {'tp'}, dimensions={0} | all-to-all | bytes 2097152 | tf_op jit(solution)/shard_map/all_to_all | solution.py:98
  156.7 0.5 broadcast.76
  157.2 3.1 %reduce = f32[8,32768]{1,0:T(8,128)S(1)} reduce(f32[8,1,32768]{2,1,0:T(1,128)S(1)} %all_to_all.20, f32[]{:T(128)} %broadcast.76), dimensions={1}, to_apply=%all_to_all.14.reduce_sub_computation | reduce | bytes 2097156 | tf_op jit(solution)/shard_map/all_to_all | solution.py:98
  160.3 0.8 reshape.107
  161.6 12.6 %all_to_all.21 = bf16[8,2,2048]{2,1,0:T(2,128)(2,1)S(1)} all-to-all(bf16[8,2,2048]{2,1,0:T(2,128)(2,1)S(1)} %reshape.108), channel_id=1, replica_groups=mesh['chi'=8,'clo'=8,'tp'=8] {'clo'}, dimensions={0} | all-to-all | bytes 131072 | tf_op jit(solution)/shard_map/all_to_all | solution.py:100
  174.4 0.8 reshape.102
  (32 shorter events, 2.6 us)
Async XLA Ops:
  7.4 5.7 %collective-permute-start = (bf16[3,2,1024]{2,1,0:T(2,128)(2,1)S(1)}, bf16[3,2,1024]{2,1,0:T(2,128)(2,1)S(1)}, u32[]{:S(2)}, u32[]{:S(2)}) collective-permute-start(bf16[3,2,1024]{2,1,0:T(2,128)(2,1)S(1)} %slice.29), channel_id=1, source_target_pairs={{0,8},{8,16},{16,24},{24,32},{32,40},{40,48},{48,56},{56,64},{64,7... | collective-permute-start | bytes 36872 | tf_op jit(solution)/shard_map/ppermute | solution.py:14
  14.9 23.4 %copy-start = (bf16[64,4096]{1,0:T(8,128)(2,1)S(1)}, bf16[64,4096]{1,0:T(8,128)(2,1)}, u32[]{:S(2)}) copy-start(bf16[64,4096]{1,0:T(8,128)(2,1)} %constant.32.clone) | copy-start | bytes 1572868
  16.5 15.0 %all-to-all-start = ((f32[8,16,1024]{2,1,0:T(8,128)}), f32[8,16,1024]{2,1,0:T(8,128)S(1)}, u32[]{:S(2)}, u32[]{:S(2)}) async-start(f32[8,16,1024]{2,1,0:T(8,128)} %broadcast_in_dim.26), calls=%async_computation | async-start | bytes 1048576 | tf_op jit(solution)/shard_map/all_to_all | solution.py:72
  31.9 8.3 %collective-permute-start.1 = (f32[16,1024]{1,0:T(8,128)S(1)}, f32[16,1024]{1,0:T(8,128)S(1)}, u32[]{:S(2)}, u32[]{:S(2)}) collective-permute-start(f32[16,1024]{1,0:T(8,128)S(1)} %get-tuple-element.5), channel_id=1, source_target_pairs={{0,64},{64,128},{128,192},{192,256},{256,320},{320,384},{384,448},... | collective-permute-start | bytes 196616 | tf_op jit(solution)/shard_map/ppermute | solution.py:14
  40.2 11.4 %collective-permute-start.2 = (f32[16,1024]{1,0:T(8,128)S(1)}, f32[16,1024]{1,0:T(8,128)S(1)}, u32[]{:S(2)}, u32[]{:S(2)}) collective-permute-start(f32[16,1024]{1,0:T(8,128)S(1)} %multiply_add_fusion.3), channel_id=1, source_target_pairs={{0,128},{64,192},{128,256},{192,320},{256,384},{320,448},{1,129},{... | collective-permute-start | bytes 196616 | tf_op jit(solution)/shard_map/ppermute | solution.py:14
  51.7 17.8 %collective-permute-start.3 = (f32[16,1024]{1,0:T(8,128)S(1)}, f32[16,1024]{1,0:T(8,128)S(1)}, u32[]{:S(2)}, u32[]{:S(2)}) collective-permute-start(f32[16,1024]{1,0:T(8,128)S(1)} %multiply_add_fusion.2), channel_id=1, source_target_pairs={{0,256},{64,320},{128,384},{192,448},{1,257},{65,321},{129,385},{1... | collective-permute-start | bytes 196616 | tf_op jit(solution)/shard_map/ppermute | solution.py:14
  67.6 3.4 %copy-start.1 = (f32[1024]{0:T(1024)S(1)}, f32[1024]{0:T(1024)}, u32[]{:S(2)}) copy-start(f32[1024]{0:T(1024)} %param.11) | copy-start | bytes 12292
  72.2 61.3 %all-to-all-start.1 = ((bf16[8,64,1024]{2,1,0:T(8,128)(2,1)}), bf16[8,64,1024]{2,1,0:T(8,128)(2,1)S(1)}, u32[]{:S(2)}, u32[]{:S(2)}) async-start(bf16[8,64,1024]{2,1,0:T(8,128)(2,1)} %broadcast_in_dim.28), calls=%async_computation.1 | async-start | bytes 2097152 | tf_op jit(solution)/shard_map/all_to_all | solution.py:94
  76.2 57.3 %all-gather.2.cloned.1.call-start = ((), (), s32[]{:S(2)}) async-start(), calls=%async_computation.4 | async-start | bytes 1179648 | tf_op jit(solution)/shard_map/all_gather | solution.py:28
Sparse Core Ops, SparseCore 0:
  79.0 54.3 all-gather.1

commit v6 on v5

--- a/solution.py
+++ b/solution.py
@@ -23,6 +23,7 @@
         groups = decay_rate.shape[0]
         width = chans // groups
         taps = short_weight.shape[1]
+        chi = lax.axis_index("chi")
         clo = lax.axis_index("clo")
 
         weight = lax.all_gather(out_weight, "chi", axis=1, tiled=True)
@@ -75,15 +76,17 @@
         inside = jnp.where((src < clo)[:, None, None], decay(gap), 0.0)
         before = jnp.sum(inside * got, axis=0)
         group_total = jnp.sum(decay((n_lo - 1 - src)[:, None, None]) * got, axis=0)
-        carried = group_total
-        earlier = jnp.zeros_like(group_total)
-        by = 1
-        while by < n_tp:
-            came = shifted(carried, "chi", n_tp, by)
-            earlier = earlier + decay(n_lo * (by - 1)) * came
-            carried = carried + decay(n_lo * by) * came
-            by *= 2
-        before = before + decay(clo) * earlier
+        flip = [
+            (c * n_lo + m, m * n_lo + c) for c in range(n_tp) for m in range(n_tp) if c != m
+        ]
+        turned = lax.ppermute(group_total, CTX, flip)
+        turned = jnp.where(chi == clo, group_total, turned)
+        spread = jnp.broadcast_to(turned[None], (n_lo,) + turned.shape)
+        totals = lax.all_to_all(spread, "clo", 0, 0, tiled=True)[:n_tp]
+        rows_before = jnp.arange(n_tp)
+        lag = jnp.maximum(chi - rows_before - 1, 0)[:, None, None]
+        outside = jnp.where((rows_before < chi)[:, None, None], decay(n_lo * lag), 0.0)
+        before = before + decay(clo) * jnp.sum(outside * totals, axis=0)
 
         far_basis = coef_c[None] * jnp.exp(-rate_c[None] * (lags + 1.0)[:, None, None])
         far = jnp.sum(far_basis * before[None], axis=1)
@@ -95,10 +98,11 @@
         partial = jnp.einsum(
             "ktc,cqo->qkto", tokens, weight, preferred_element_type=jnp.float32
         )
-        pieces = lax.all_to_all(partial, "tp", 0, 0, tiled=True)
-        summed = jnp.sum(pieces, axis=0).astype(jnp.bfloat16)
-        back = lax.all_to_all(summed, "clo", 0, 0, tiled=True)
-        return back.transpose(1, 0, 2).reshape(rows, -1)
+        partial = partial.transpose(1, 0, 2, 3).reshape((n_lo * n_tp,) + partial.shape[2:])
+        pieces = lax.all_to_all(partial, ("clo", "tp"), 0, 0, tiled=True)
+        pieces = pieces.reshape((n_lo, n_tp) + pieces.shape[1:])
+        summed = jnp.sum(pieces, axis=1).astype(jnp.bfloat16)
+        return summed.transpose(1, 0, 2).reshape(rows, -1)
 
     return per_device
 

time: 183 us -> 170 us (0.929)
  the two profiles are of different devices: /device:TPU:2 before, /device:TPU:1 now
where the time goes in v6:
time: 170 us; the launch traced here: 169 us
  waiting for transfers between devices  70.8 us (42%)
  starting transfers between devices  32.3 us (19%)
  blocking collectives  28.8 us (17%)
  between operations  13.7 us (8%)
  local copies, waits for them, and re-layouts  10.7 us (6%)
  other arithmetic  9.24 us (5%)
  matrix products  3.41 us (2%)
    all_gather x1, waiting for transfers between devices, per_device(): weight = lax.all_gather(out_weight, 'chi', axis=1, tiled=True)  59.3 us
    all_to_all x1, blocking collectives, per_device(): pieces = lax.all_to_all(partial, ('clo', 'tp'), 0, 0, tiled=True)  28.8 us
    all_to_all x1, starting transfers between devices, per_device(): totals = lax.all_to_all(spread, 'clo', 0, 0, tiled=True)[:n_tp]  18.7 us
    all_to_all x1, waiting for transfers between devices, per_device(): got = lax.all_to_all(spread, 'clo', 0, 0, tiled=True)  7.14 us
    all_to_all x1, starting transfers between devices, per_device(): got = lax.all_to_all(spread, 'clo', 0, 0, tiled=True)  5.37 us
    ppermute x1, starting transfers between devices, shifted(): return lax.ppermute(value, axis, pairs)  4.02 us
    all_to_all x1, waiting for transfers between devices, per_device(): totals = lax.all_to_all(spread, 'clo', 0, 0, tiled=True)[:n_tp]  3.63 us
    all_to_all x1, starting transfers between devices, per_device(): tokens = lax.all_to_all(spread, 'clo', 0, 0, tiled=True)  3.56 us
  transfers between devices with their start and end apart: 6, of which 3 were waited for; matrix products, arithmetic and copies ran while one was open for 3% of the time, Pallas kernels for 0%

profile of v6, /device:TPU:1, one launch (start us, length us, event | category | flops | bytes accessed | tf_op | source)
XLA Modules:
  0.0 168.9 jit_solution(997794766001627721)
XLA Ops:
  6.5 0.8 slice.29
  7.4 4.0 %collective-permute-start = (bf16[3,2,1024]{2,1,0:T(2,128)(2,1)S(1)}, bf16[3,2,1024]{2,1,0:T(2,128)(2,1)S(1)}, u32[]{:S(2)}, u32[]{:S(2)}) collective-permute-start(bf16[3,2,1024]{2,1,0:T(2,128)(2,1)S(1)} %slice.29), channel_id=1, source_target_pairs={{0,8},{8,16},{16,24},{24,32},{32,40},{40,48},{48,56},{56,64},{64,7... | collective-permute-start | bytes 36872 | tf_op jit(solution)/shard_map/ppermute | solution.py:14
  11.4 0.9 fusion.10
  12.3 0.7 negate_bitcast_fusion
  13.3 0.3 neg.32
  13.6 1.8 %multiply_add_fusion = f32[3,64,1024]{2,1,0:T(8,128)S(1)} fusion(bf16[3,64,1024]{2,1,0:T(8,128)(2,1)} %param.7, bf16[3,2,1024]{2,1,0:T(2,128)(2,1)S(1)} %collective-permute-done, f32[3,1024]{1,0:T(4,128)S(1)} %get-tuple-element.15, f32[3,1024]{1,0:T(4,128)S(1)} %get-tuple-element.16, f32[3,1024]{1,0:T(4,128)S(1)} %bitcast.50), kind=kLoop, calls=%fused_computation.6 | loop fusion | flops 2752512 | bytes 1228800 | tf_op jit(solution)/shard_map/add | solution.py:36
  15.5 0.7 multiply_reduce_fusion.1
  16.2 0.8 broadcast_in_dim.34
  17.0 5.4 %all-to-all-start = ((f32[8,16,1024]{2,1,0:T(8,128)}), f32[8,16,1024]{2,1,0:T(8,128)S(1)}, u32[]{:S(2)}, u32[]{:S(2)}) async-start(f32[8,16,1024]{2,1,0:T(8,128)} %broadcast_in_dim.34), calls=%async_computation | async-start | bytes 1048576 | tf_op jit(solution)/shard_map/all_to_all | solution.py:73
  22.5 7.1 %all-to-all-done = f32[8,16,1024]{2,1,0:T(8,128)S(1)} async-done(((f32[8,16,1024]{2,1,0:T(8,128)}), f32[8,16,1024]{2,1,0:T(8,128)S(1)}, u32[]{:S(2)}, u32[]{:S(2)}) %all-to-all-start) | async-done | bytes 524320 | tf_op jit(solution)/shard_map/all_to_all | solution.py:73
  29.6 0.3 multiply_reduce_fusion.3
  29.9 0.7 collective-permute-start.1
  30.6 0.8 broadcast_in_dim.36
  31.5 18.7 %all-to-all-start.1 = ((f32[8,16,1024]{2,1,0:T(8,128)}), f32[8,16,1024]{2,1,0:T(8,128)S(1)}, u32[]{:S(2)}, u32[]{:S(2)}) async-start(f32[8,16,1024]{2,1,0:T(8,128)} %broadcast_in_dim.36), calls=%async_computation.1 | async-start | bytes 1048576 | tf_op jit(solution)/shard_map/all_to_all | solution.py:85
  50.4 0.3 mul.248
  50.8 0.4 multiply_reduce_fusion.5
  51.2 0.3 convolution_convert_fusion
  51.5 1.1 reshape.132
  52.8 0.6 fusion.11
  53.7 3.6 %all-to-all-done.1 = f32[8,16,1024]{2,1,0:T(8,128)S(1)} async-done(((f32[8,16,1024]{2,1,0:T(8,128)}), f32[8,16,1024]{2,1,0:T(8,128)S(1)}, u32[]{:S(2)}, u32[]{:S(2)}) %all-to-all-start.1) | async-done | bytes 524320 | tf_op jit(solution)/shard_map/all_to_all | solution.py:85
  57.5 1.4 multiply_reduce_fusion
  59.0 1.2 broadcast_in_dim.68
  60.2 3.6 %all-to-all-start.2 = ((bf16[8,64,1024]{2,1,0:T(8,128)(2,1)}), bf16[8,64,1024]{2,1,0:T(8,128)(2,1)S(1)}, u32[]{:S(2)}, u32[]{:S(2)}) async-start(bf16[8,64,1024]{2,1,0:T(8,128)(2,1)} %broadcast_in_dim.68), calls=%async_computation.2 | async-start | bytes 2097152 | tf_op jit(solution)/shard_map/all_to_all | solution.py:97
  63.8 0.7 all-gather.2.cloned.1.call-update
  64.5 59.3 %all-gather.2.cloned.1.call-done = bf16[1024,512]{0,1:T(8,128)(2,1)} async-done(((bf16[1024,64]{0,1:T(8,128)(2,1)}), bf16[1024,512]{0,1:T(8,128)(2,1)}) %all-gather.2.cloned.1.call-update) | async-done | bytes 1048592 | tf_op jit(solution)/shard_map/all_gather | solution.py:29
  123.8 2.5 %fusion = f32[8,64,8,64]{3,1,2,0:T(8,128)S(1)} fusion(bf16[1024,8,64,1]{0,2,1,3:T(8,128)(2,1)} %bitcast.51, bf16[8,64,1024]{2,1,0:T(8,128)(2,1)S(1)} %all-to-all-done.2), kind=kOutput, calls=%fused_computation.4 | convolution fusion | flops 536870912 | bytes 3145728 | tf_op jit(solution)/shard_map/ktc,cqo->qkto/dot_general | solution.py:98
  126.3 1.3 reshape.141
  127.6 28.8 %all_to_all.20 = f32[64,1,4096]{2,1,0:T(1,128)S(1)} all-to-all(f32[64,1,4096]{2,1,0:T(1,128)S(1)} %reshape.141), channel_id=1, replica_groups=mesh['chi'=8,'clo'=8,'tp'=8] {'clo','tp'}, dimensions={0} | all-to-all | bytes 2097152 | tf_op jit(solution)/shard_map/all_to_all | solution.py:102
  156.4 0.5 broadcast.109
  156.9 3.3 %reduce = f32[64,4096]{1,0:T(8,128)S(1)} reduce(f32[64,1,4096]{2,1,0:T(1,128)S(1)} %all_to_all.20, f32[]{:T(128)} %broadcast.109), dimensions={1}, to_apply=%all_to_all.15.reduce_sub_computation | reduce | bytes 2097156 | tf_op jit(solution)/shard_map/all_to_all | solution.py:102
  160.2 0.8 reshape.142
  161.3 0.8 reshape.137
  (29 shorter events, 1.6 us)
Async XLA Ops:
  7.4 6.2 %collective-permute-start = (bf16[3,2,1024]{2,1,0:T(2,128)(2,1)S(1)}, bf16[3,2,1024]{2,1,0:T(2,128)(2,1)S(1)}, u32[]{:S(2)}, u32[]{:S(2)}) collective-permute-start(bf16[3,2,1024]{2,1,0:T(2,128)(2,1)S(1)} %slice.29), channel_id=1, source_target_pairs={{0,8},{8,16},{16,24},{24,32},{32,40},{40,48},{48,56},{56,64},{64,7... | collective-permute-start | bytes 36872 | tf_op jit(solution)/shard_map/ppermute | solution.py:14
  17.0 12.5 %all-to-all-start = ((f32[8,16,1024]{2,1,0:T(8,128)}), f32[8,16,1024]{2,1,0:T(8,128)S(1)}, u32[]{:S(2)}, u32[]{:S(2)}) async-start(f32[8,16,1024]{2,1,0:T(8,128)} %broadcast_in_dim.34), calls=%async_computation | async-start | bytes 1048576 | tf_op jit(solution)/shard_map/all_to_all | solution.py:73
  22.4 28.7 %copy-start = (bf16[64,4096]{1,0:T(8,128)(2,1)S(1)}, bf16[64,4096]{1,0:T(8,128)(2,1)}, u32[]{:S(2)}) copy-start(bf16[64,4096]{1,0:T(8,128)(2,1)} %constant.32.clone) | copy-start | bytes 1572868
  29.9 0.7 collective-permute-start.1
  31.5 25.8 %all-to-all-start.1 = ((f32[8,16,1024]{2,1,0:T(8,128)}), f32[8,16,1024]{2,1,0:T(8,128)S(1)}, u32[]{:S(2)}, u32[]{:S(2)}) async-start(f32[8,16,1024]{2,1,0:T(8,128)} %broadcast_in_dim.36), calls=%async_computation.1 | async-start | bytes 1048576 | tf_op jit(solution)/shard_map/all_to_all | solution.py:85
  53.4 5.5 %copy-start.1 = (f32[1024]{0:T(1024)S(1)}, f32[1024]{0:T(1024)}, u32[]{:S(2)}) copy-start(f32[1024]{0:T(1024)} %param.11) | copy-start | bytes 12292
  60.2 63.6 %all-to-all-start.2 = ((bf16[8,64,1024]{2,1,0:T(8,128)(2,1)}), bf16[8,64,1024]{2,1,0:T(8,128)(2,1)S(1)}, u32[]{:S(2)}, u32[]{:S(2)}) async-start(bf16[8,64,1024]{2,1,0:T(8,128)(2,1)} %broadcast_in_dim.68), calls=%async_computation.2 | async-start | bytes 2097152 | tf_op jit(solution)/shard_map/all_to_all | solution.py:97
  63.7 60.1 %all-gather.2.cloned.1.call-start = ((), (), s32[]{:S(2)}) async-start(), calls=%async_computation.4 | async-start | bytes 1179648 | tf_op jit(solution)/shard_map/all_gather | solution.py:29
Sparse Core Ops, SparseCore 0:
  66.6 57.1 all-gather.1

commit v7 on v6

--- a/solution.py
+++ b/solution.py
@@ -7,6 +7,7 @@
 
 
 CTX = ("chi", "clo")
+TP = ("x", "core")
 
 
 def shifted(value, axis, count, by):
@@ -16,6 +17,7 @@
 
 def make_per_device(n_ctx, n_tp):
     n_lo = n_ctx // n_tp
+    n_x = n_tp // 2
 
     def per_device(features, short_weight, decay_rate, residue, skip_gain, out_weight):
         rows = features.shape[1]
@@ -96,11 +98,16 @@
         spread = jnp.broadcast_to(mixed[None], (n_lo,) + mixed.shape)
         tokens = lax.all_to_all(spread, "clo", 0, 0, tiled=True)
         partial = jnp.einsum(
-            "ktc,cqo->qkto", tokens, weight, preferred_element_type=jnp.float32
+            "ktc,cqo->kqto", tokens, weight, preferred_element_type=jnp.float32
         )
-        partial = partial.transpose(1, 0, 2, 3).reshape((n_lo * n_tp,) + partial.shape[2:])
-        pieces = lax.all_to_all(partial, ("clo", "tp"), 0, 0, tiled=True)
-        pieces = pieces.reshape((n_lo, n_tp) + pieces.shape[1:])
+        partial = partial.reshape((n_lo, n_x, 2) + partial.shape[2:])
+        core = lax.axis_index("core")
+        mine = lax.dynamic_index_in_dim(partial, core, 2, keepdims=False)
+        other = lax.dynamic_index_in_dim(partial, 1 - core, 2, keepdims=False)
+        mine = mine + lax.ppermute(other, "core", [(0, 1), (1, 0)])
+        mine = mine.reshape((n_lo * n_x,) + mine.shape[2:])
+        pieces = lax.all_to_all(mine, ("clo", "x"), 0, 0, tiled=True)
+        pieces = pieces.reshape((n_lo, n_x) + pieces.shape[1:])
         summed = jnp.sum(pieces, axis=1).astype(jnp.bfloat16)
         return summed.transpose(1, 0, 2).reshape(rows, -1)
 
@@ -110,20 +117,20 @@
 def solution(mesh):
     n_ctx = mesh.shape["ctx"]
     n_tp = mesh.shape["tp"]
-    devices = np.asarray(mesh.devices).reshape(n_tp, n_ctx // n_tp, n_tp)
-    split = Mesh(devices, ("chi", "clo", "tp"))
+    devices = np.asarray(mesh.devices).reshape(n_tp, n_ctx // n_tp, n_tp // 2, 2)
+    split = Mesh(devices, ("chi", "clo", "x", "core"))
     placed = (
-        P(None, CTX, "tp"),
-        P(None, None, "tp"),
-        P("tp", None),
-        P("tp", None),
-        P("tp"),
-        P("tp", CTX),
+        P(None, CTX, TP),
+        P(None, None, TP),
+        P(TP, None),
+        P(TP, None),
+        P(TP),
+        P(TP, CTX),
     )
     return jax.shard_map(
         make_per_device(n_ctx, n_tp),
         mesh=split,
         in_specs=placed,
-        out_specs=P(CTX, "tp"),
+        out_specs=P(CTX, TP),
         check_vma=False,
     )

time: 170 us -> 166 us (0.976)
  blocking collectives: 28.8 us -> 18.5 us
  starting transfers between devices: 32.3 us -> 37.3 us
  waiting for transfers between devices: 70.8 us -> 73.2 us
    all_to_all x1, blocking collectives: 28.8 us -> 18.5 us  [per_device(): pieces = lax.all_to_all(mine, ('clo', 'x'), 0, 0, tiled=True)]
    ppermute x0 -> x1, starting transfers between devices: none -> 5.02 us  [per_device(): mine = mine + lax.ppermute(other, 'core', [(0, 1), (1, 0)])]
    ppermute x0 -> x1, waiting for transfers between devices: none -> 2.4 us  [per_device(): mine = mine + lax.ppermute(other, 'core', [(0, 1), (1, 0)])]
  transfers between devices with their start and end apart: 6 -> 7, of which waited for: 3 -> 4; matrix products, arithmetic and copies ran while one was open for 3% -> 3% of each run, Pallas kernels for 0% -> 0%
where the time goes in v7:
time: 166 us; the launch traced here: 165 us
  waiting for transfers between devices  73.2 us (44%)
  starting transfers between devices  37.3 us (22%)
  blocking collectives  18.5 us (11%)
  between operations  13.7 us (8%)
  local copies, waits for them, and re-layouts  9.75 us (6%)
  other arithmetic  9.11 us (5%)
  matrix products  3.41 us (2%)
    all_gather x1, waiting for transfers between devices, per_device(): weight = lax.all_gather(out_weight, 'chi', axis=1, tiled=True)  59.3 us
    all_to_all x1, starting transfers between devices, per_device(): totals = lax.all_to_all(spread, 'clo', 0, 0, tiled=True)[:n_tp]  18.7 us
    all_to_all x1, blocking collectives, per_device(): pieces = lax.all_to_all(mine, ('clo', 'x'), 0, 0, tiled=True)  18.5 us
    all_to_all x1, waiting for transfers between devices, per_device(): got = lax.all_to_all(spread, 'clo', 0, 0, tiled=True)  7.14 us
    all_to_all x1, starting transfers between devices, per_device(): got = lax.all_to_all(spread, 'clo', 0, 0, tiled=True)  5.37 us
    ppermute x1, starting transfers between devices, per_device(): mine = mine + lax.ppermute(other, 'core', [(0, 1), (1, 0)])  5.02 us
    ppermute x1, starting transfers between devices, shifted(): return lax.ppermute(value, axis, pairs)  4.02 us
    all_to_all x1, waiting for transfers between devices, per_device(): totals = lax.all_to_all(spread, 'clo', 0, 0, tiled=True)[:n_tp]  3.63 us
  transfers between devices with their start and end apart: 7, of which 4 were waited for; matrix products, arithmetic and copies ran while one was open for 3% of the time, Pallas kernels for 0%

profile of v7, /device:TPU:1, one launch (start us, length us, event | category | flops | bytes accessed | tf_op | source)
XLA Modules:
  0.0 165.0 jit_solution(9104476225490384839)
XLA Ops:
  6.5 0.8 slice.29
  7.4 4.0 %collective-permute-start = (bf16[3,2,1024]{2,1,0:T(2,128)(2,1)S(1)}, bf16[3,2,1024]{2,1,0:T(2,128)(2,1)S(1)}, u32[]{:S(2)}, u32[]{:S(2)}) collective-permute-start(bf16[3,2,1024]{2,1,0:T(2,128)(2,1)S(1)} %slice.29), channel_id=1, source_target_pairs={{0,8},{8,16},{16,24},{24,32},{32,40},{40,48},{48,56},{56,64},{64,7... | collective-permute-start | bytes 36872 | tf_op jit(solution)/shard_map/ppermute | solution.py:15
  11.4 0.9 fusion.10
  12.3 0.7 negate_bitcast_fusion
  13.6 1.8 %multiply_add_fusion = f32[3,64,1024]{2,1,0:T(8,128)S(1)} fusion(bf16[3,64,1024]{2,1,0:T(8,128)(2,1)} %param.7, bf16[3,2,1024]{2,1,0:T(2,128)(2,1)S(1)} %collective-permute-done, f32[3,1024]{1,0:T(4,128)S(1)} %get-tuple-element.15, f32[3,1024]{1,0:T(4,128)S(1)} %get-tuple-element.16, f32[3,1024]{1,0:T(4,128)S(1)} %bitcast.57), kind=kLoop, calls=%fused_computation.8 | loop fusion | flops 2752512 | bytes 1228800 | tf_op jit(solution)/shard_map/add | solution.py:38
  15.5 0.7 multiply_reduce_fusion.1
  16.2 0.8 broadcast_in_dim.34
  17.0 5.4 %all-to-all-start = ((f32[8,16,1024]{2,1,0:T(8,128)}), f32[8,16,1024]{2,1,0:T(8,128)S(1)}, u32[]{:S(2)}, u32[]{:S(2)}) async-start(f32[8,16,1024]{2,1,0:T(8,128)} %broadcast_in_dim.34), calls=%async_computation | async-start | bytes 1048576 | tf_op jit(solution)/shard_map/all_to_all | solution.py:75
  22.5 7.1 %all-to-all-done = f32[8,16,1024]{2,1,0:T(8,128)S(1)} async-done(((f32[8,16,1024]{2,1,0:T(8,128)}), f32[8,16,1024]{2,1,0:T(8,128)S(1)}, u32[]{:S(2)}, u32[]{:S(2)}) %all-to-all-start) | async-done | bytes 524320 | tf_op jit(solution)/shard_map/all_to_all | solution.py:75
  29.6 0.3 multiply_reduce_fusion.3
  29.9 0.7 collective-permute-start.1
  30.6 0.8 broadcast_in_dim.36
  31.5 18.7 %all-to-all-start.1 = ((f32[8,16,1024]{2,1,0:T(8,128)}), f32[8,16,1024]{2,1,0:T(8,128)S(1)}, u32[]{:S(2)}, u32[]{:S(2)}) async-start(f32[8,16,1024]{2,1,0:T(8,128)} %broadcast_in_dim.36), calls=%async_computation.1 | async-start | bytes 1048576 | tf_op jit(solution)/shard_map/all_to_all | solution.py:87
  50.8 0.4 multiply_reduce_fusion.5
  51.4 1.1 reshape.135
  52.8 0.6 fusion.11
  53.6 3.6 %all-to-all-done.1 = f32[8,16,1024]{2,1,0:T(8,128)S(1)} async-done(((f32[8,16,1024]{2,1,0:T(8,128)}), f32[8,16,1024]{2,1,0:T(8,128)S(1)}, u32[]{:S(2)}, u32[]{:S(2)}) %all-to-all-start.1) | async-done | bytes 524320 | tf_op jit(solution)/shard_map/all_to_all | solution.py:87
  57.5 1.4 multiply_reduce_fusion
  59.0 1.2 broadcast_in_dim.68
  60.2 3.6 %all-to-all-start.2 = ((bf16[8,64,1024]{2,1,0:T(8,128)(2,1)}), bf16[8,64,1024]{2,1,0:T(8,128)(2,1)S(1)}, u32[]{:S(2)}, u32[]{:S(2)}) async-start(bf16[8,64,1024]{2,1,0:T(8,128)(2,1)} %broadcast_in_dim.68), calls=%async_computation.2 | async-start | bytes 2097152 | tf_op jit(solution)/shard_map/all_to_all | solution.py:99
  63.8 0.7 all-gather.2.cloned.1.call-update
  64.5 59.3 %all-gather.2.cloned.1.call-done = bf16[1024,512]{0,1:T(8,128)(2,1)} async-done(((bf16[1024,64]{0,1:T(8,128)(2,1)}), bf16[1024,512]{0,1:T(8,128)(2,1)}) %all-gather.2.cloned.1.call-update) | async-done | bytes 1048592 | tf_op jit(solution)/shard_map/all_gather | solution.py:31
  123.8 2.5 %fusion = f32[8,64,8,64]{3,1,2,0:T(8,128)S(1)} fusion(bf16[1024,8,64,1]{0,2,1,3:T(8,128)(2,1)} %bitcast.58, bf16[8,64,1024]{2,1,0:T(8,128)(2,1)S(1)} %all-to-all-done.2), kind=kOutput, calls=%fused_computation.3 | convolution fusion | flops 536870912 | bytes 3145728 | tf_op jit(solution)/shard_map/ktc,cqo->kqto/dot_general | solution.py:100
  126.4 5.0 %collective-permute-start.2 = (f32[8,4,64,64]{3,2,1,0:T(8,128)S(1)}, f32[8,4,64,64]{3,2,1,0:T(8,128)}, u32[]{:S(2)}, u32[]{:S(2)}) collective-permute-start(f32[8,4,64,64]{3,2,1,0:T(8,128)S(1)} %dynamic-slice_bitcast_fusion), channel_id=1, source_target_pairs={{0,1},{1,0},{2,3},{3,2},{4,5},{5,4},{6,7},{7,6},{8,9},{9,8},{10,11... | collective-permute-start | bytes 1572872 | tf_op jit(solution)/shard_map/ppermute | solution.py:107
  131.4 2.4 %collective-permute-done.2 = f32[8,4,64,64]{3,2,1,0:T(8,128)} collective-permute-done((f32[8,4,64,64]{3,2,1,0:T(8,128)S(1)}, f32[8,4,64,64]{3,2,1,0:T(8,128)}, u32[]{:S(2)}, u32[]{:S(2)}) %collective-permute-start.2) | collective-permute-done | bytes 524320 | tf_op jit(solution)/shard_map/ppermute | solution.py:107
  133.8 1.4 bitcast_add_fusion
  135.2 0.7 reshape.145
  135.8 18.5 %all_to_all.20 = f32[32,1,4096]{2,1,0:T(1,128)S(1)} all-to-all(f32[32,1,4096]{2,1,0:T(1,128)S(1)} %reshape.145), channel_id=1, replica_groups=mesh['chi'=8,'clo'=8,'x'=4,'core'=2] {'clo','x'}, dimensions={0} | all-to-all | bytes 1048576 | tf_op jit(solution)/shard_map/all_to_all | solution.py:109
  154.3 0.5 broadcast.109
  154.8 1.9 %reduce = f32[32,4096]{1,0:T(8,128)S(1)} reduce(f32[32,1,4096]{2,1,0:T(1,128)S(1)} %all_to_all.20, f32[]{:T(128)} %broadcast.109), dimensions={1}, to_apply=%all_to_all.15.reduce_sub_computation | reduce | bytes 1048580 | tf_op jit(solution)/shard_map/all_to_all | solution.py:109
  156.7 0.4 reshape.146
  157.4 0.8 reshape.141
  (33 shorter events, 2.4 us)
Async XLA Ops:
  7.4 6.2 %collective-permute-start = (bf16[3,2,1024]{2,1,0:T(2,128)(2,1)S(1)}, bf16[3,2,1024]{2,1,0:T(2,128)(2,1)S(1)}, u32[]{:S(2)}, u32[]{:S(2)}) collective-permute-start(bf16[3,2,1024]{2,1,0:T(2,128)(2,1)S(1)} %slice.29), channel_id=1, source_target_pairs={{0,8},{8,16},{16,24},{24,32},{32,40},{40,48},{48,56},{56,64},{64,7... | collective-permute-start | bytes 36872 | tf_op jit(solution)/shard_map/ppermute | solution.py:15
  17.0 12.5 %all-to-all-start = ((f32[8,16,1024]{2,1,0:T(8,128)}), f32[8,16,1024]{2,1,0:T(8,128)S(1)}, u32[]{:S(2)}, u32[]{:S(2)}) async-start(f32[8,16,1024]{2,1,0:T(8,128)} %broadcast_in_dim.34), calls=%async_computation | async-start | bytes 1048576 | tf_op jit(solution)/shard_map/all_to_all | solution.py:75
  22.4 28.7 %copy-start = (bf16[64,4096]{1,0:T(8,128)(2,1)S(1)}, bf16[64,4096]{1,0:T(8,128)(2,1)}, u32[]{:S(2)}) copy-start(bf16[64,4096]{1,0:T(8,128)(2,1)} %constant.47.clone) | copy-start | bytes 1572868
  29.9 0.7 collective-permute-start.1
  31.5 25.8 %all-to-all-start.1 = ((f32[8,16,1024]{2,1,0:T(8,128)}), f32[8,16,1024]{2,1,0:T(8,128)S(1)}, u32[]{:S(2)}, u32[]{:S(2)}) async-start(f32[8,16,1024]{2,1,0:T(8,128)} %broadcast_in_dim.36), calls=%async_computation.1 | async-start | bytes 1048576 | tf_op jit(solution)/shard_map/all_to_all | solution.py:87
  53.4 5.5 %copy-start.1 = (f32[1024]{0:T(1024)S(1)}, f32[1024]{0:T(1024)}, u32[]{:S(2)}) copy-start(f32[1024]{0:T(1024)} %param.11) | copy-start | bytes 12292
  60.2 63.6 %all-to-all-start.2 = ((bf16[8,64,1024]{2,1,0:T(8,128)(2,1)}), bf16[8,64,1024]{2,1,0:T(8,128)(2,1)S(1)}, u32[]{:S(2)}, u32[]{:S(2)}) async-start(bf16[8,64,1024]{2,1,0:T(8,128)(2,1)} %broadcast_in_dim.68), calls=%async_computation.2 | async-start | bytes 2097152 | tf_op jit(solution)/shard_map/all_to_all | solution.py:99
  63.7 60.1 %all-gather.2.cloned.1.call-start = ((), (), s32[]{:S(2)}) async-start(), calls=%async_computation.4 | async-start | bytes 1179648 | tf_op jit(solution)/shard_map/all_gather | solution.py:31
  126.4 7.4 %collective-permute-start.2 = (f32[8,4,64,64]{3,2,1,0:T(8,128)S(1)}, f32[8,4,64,64]{3,2,1,0:T(8,128)}, u32[]{:S(2)}, u32[]{:S(2)}) collective-permute-start(f32[8,4,64,64]{3,2,1,0:T(8,128)S(1)} %dynamic-slice_bitcast_fusion), channel_id=1, source_target_pairs={{0,1},{1,0},{2,3},{3,2},{4,5},{5,4},{6,7},{7,6},{8,9},{9,8},{10,11... | collective-permute-start | bytes 1572872 | tf_op jit(solution)/shard_map/ppermute | solution.py:107
Sparse Core Ops, SparseCore 0:
  66.6 57.1 all-gather.1

commit v8 on v7

--- a/solution.py
+++ b/solution.py
@@ -78,13 +78,16 @@
         inside = jnp.where((src < clo)[:, None, None], decay(gap), 0.0)
         before = jnp.sum(inside * got, axis=0)
         group_total = jnp.sum(decay((n_lo - 1 - src)[:, None, None]) * got, axis=0)
-        flip = [
-            (c * n_lo + m, m * n_lo + c) for c in range(n_tp) for m in range(n_tp) if c != m
+        down = [
+            (c * n_lo + b, ((c - b) % n_tp) * n_lo + b)
+            for c in range(n_tp)
+            for b in range(1, n_tp)
         ]
-        turned = lax.ppermute(group_total, CTX, flip)
-        turned = jnp.where(chi == clo, group_total, turned)
+        turned = lax.ppermute(group_total, CTX, down)
+        turned = jnp.where(clo == 0, group_total, turned)
         spread = jnp.broadcast_to(turned[None], (n_lo,) + turned.shape)
         totals = lax.all_to_all(spread, "clo", 0, 0, tiled=True)[:n_tp]
+        totals = jnp.roll(totals, chi, axis=0)
         rows_before = jnp.arange(n_tp)
         lag = jnp.maximum(chi - rows_before - 1, 0)[:, None, None]
         outside = jnp.where((rows_before < chi)[:, None, None], decay(n_lo * lag), 0.0)

time: 166 us -> 169 us (1.018)
  waiting for transfers between devices: 73.2 us -> 75.1 us
    all_gather x1, waiting for transfers between devices: 59.3 us -> 61.3 us  [per_device(): weight = lax.all_gather(out_weight, 'chi', axis=1, tiled=True)]
where the time goes in v8:
time: 169 us; the launch traced here: 168 us
  waiting for transfers between devices  75.1 us (44%)
  starting transfers between devices  38.8 us (23%)
  blocking collectives  18.5 us (11%)
  between operations  13.7 us (8%)
  local copies, waits for them, and re-layouts  9.75 us (6%)
  other arithmetic  9.18 us (5%)
  matrix products  3.41 us (2%)
    all_gather x1, waiting for transfers between devices, per_device(): weight = lax.all_gather(out_weight, 'chi', axis=1, tiled=True)  61.3 us
    all_to_all x1, starting transfers between devices, per_device(): totals = lax.all_to_all(spread, 'clo', 0, 0, tiled=True)[:n_tp]  20.1 us
    all_to_all x1, blocking collectives, per_device(): pieces = lax.all_to_all(mine, ('clo', 'x'), 0, 0, tiled=True)  18.5 us
    all_to_all x1, waiting for transfers between devices, per_device(): got = lax.all_to_all(spread, 'clo', 0, 0, tiled=True)  7.14 us
    all_to_all x1, starting transfers between devices, per_device(): got = lax.all_to_all(spread, 'clo', 0, 0, tiled=True)  5.37 us
    ppermute x1, starting transfers between devices, per_device(): mine = mine + lax.ppermute(other, 'core', [(0, 1), (1, 0)])  5.02 us
    ppermute x1, starting transfers between devices, shifted(): return lax.ppermute(value, axis, pairs)  4.02 us
    all_to_all x1, waiting for transfers between devices, per_device(): totals = lax.all_to_all(spread, 'clo', 0, 0, tiled=True)[:n_tp]  3.63 us
  transfers between devices with their start and end apart: 7, of which 4 were waited for; matrix products, arithmetic and copies ran while one was open for 3% of the time, Pallas kernels for 0%

profile of v8, /device:TPU:1, one launch (start us, length us, event | category | flops | bytes accessed | tf_op | source)
XLA Modules:
  0.0 168.5 jit_solution(9620283948181319532)
XLA Ops:
  6.5 0.8 slice.29
  7.4 4.0 %collective-permute-start = (bf16[3,2,1024]{2,1,0:T(2,128)(2,1)S(1)}, bf16[3,2,1024]{2,1,0:T(2,128)(2,1)S(1)}, u32[]{:S(2)}, u32[]{:S(2)}) collective-permute-start(bf16[3,2,1024]{2,1,0:T(2,128)(2,1)S(1)} %slice.29), channel_id=1, source_target_pairs={{0,8},{8,16},{16,24},{24,32},{32,40},{40,48},{48,56},{56,64},{64,7... | collective-permute-start | bytes 36872 | tf_op jit(solution)/shard_map/ppermute | solution.py:15
  11.4 0.9 fusion.13
  12.3 0.7 negate_bitcast_fusion
  13.6 1.8 %multiply_add_fusion = f32[3,64,1024]{2,1,0:T(8,128)S(1)} fusion(bf16[3,64,1024]{2,1,0:T(8,128)(2,1)} %param.7, bf16[3,2,1024]{2,1,0:T(2,128)(2,1)S(1)} %collective-permute-done, f32[3,1024]{1,0:T(4,128)S(1)} %get-tuple-element.15, f32[3,1024]{1,0:T(4,128)S(1)} %get-tuple-element.16, f32[3,1024]{1,0:T(4,128)S(1)} %bitcast.57), kind=kLoop, calls=%fused_computation.10 | loop fusion | flops 2752512 | bytes 1228800 | tf_op jit(solution)/shard_map/add | solution.py:38
  15.5 0.7 multiply_reduce_fusion.1
  16.2 0.8 broadcast_in_dim.34
  17.0 5.4 %all-to-all-start = ((f32[8,16,1024]{2,1,0:T(8,128)}), f32[8,16,1024]{2,1,0:T(8,128)S(1)}, u32[]{:S(2)}, u32[]{:S(2)}) async-start(f32[8,16,1024]{2,1,0:T(8,128)} %broadcast_in_dim.34), calls=%async_computation | async-start | bytes 1048576 | tf_op jit(solution)/shard_map/all_to_all | solution.py:75
  22.5 7.1 %all-to-all-done = f32[8,16,1024]{2,1,0:T(8,128)S(1)} async-done(((f32[8,16,1024]{2,1,0:T(8,128)}), f32[8,16,1024]{2,1,0:T(8,128)S(1)}, u32[]{:S(2)}, u32[]{:S(2)}) %all-to-all-start) | async-done | bytes 524320 | tf_op jit(solution)/shard_map/all_to_all | solution.py:75
  29.6 0.3 multiply_reduce_fusion.2
  29.9 0.7 collective-permute-start.1
  30.6 0.8 broadcast_in_dim.36
  31.5 20.1 %all-to-all-start.1 = ((f32[8,16,1024]{2,1,0:T(8,128)}), f32[8,16,1024]{2,1,0:T(8,128)S(1)}, u32[]{:S(2)}, u32[]{:S(2)}) async-start(f32[8,16,1024]{2,1,0:T(8,128)} %broadcast_in_dim.36), calls=%async_computation.1 | async-start | bytes 1048576 | tf_op jit(solution)/shard_map/all_to_all | solution.py:89
  52.3 0.4 multiply_reduce_fusion.4
  52.9 1.1 reshape.135
  54.3 0.6 fusion.14
  55.1 3.6 %all-to-all-done.1 = f32[8,16,1024]{2,1,0:T(8,128)S(1)} async-done(((f32[8,16,1024]{2,1,0:T(8,128)}), f32[8,16,1024]{2,1,0:T(8,128)S(1)}, u32[]{:S(2)}, u32[]{:S(2)}) %all-to-all-start.1) | async-done | bytes 524320 | tf_op jit(solution)/shard_map/all_to_all | solution.py:89
  59.0 1.4 multiply_reduce_fusion
  60.5 1.2 broadcast_in_dim.68
  61.7 3.6 %all-to-all-start.2 = ((bf16[8,64,1024]{2,1,0:T(8,128)(2,1)}), bf16[8,64,1024]{2,1,0:T(8,128)(2,1)S(1)}, u32[]{:S(2)}, u32[]{:S(2)}) async-start(bf16[8,64,1024]{2,1,0:T(8,128)(2,1)} %broadcast_in_dim.68), calls=%async_computation.2 | async-start | bytes 2097152 | tf_op jit(solution)/shard_map/all_to_all | solution.py:102
  65.3 0.7 all-gather.2.cloned.1.call-update
  66.0 61.3 %all-gather.2.cloned.1.call-done = bf16[1024,512]{0,1:T(8,128)(2,1)} async-done(((bf16[1024,64]{0,1:T(8,128)(2,1)}), bf16[1024,512]{0,1:T(8,128)(2,1)}) %all-gather.2.cloned.1.call-update) | async-done | bytes 1048592 | tf_op jit(solution)/shard_map/all_gather | solution.py:31
  127.3 2.5 %fusion = f32[8,64,8,64]{3,1,2,0:T(8,128)S(1)} fusion(bf16[1024,8,64,1]{0,2,1,3:T(8,128)(2,1)} %bitcast.58, bf16[8,64,1024]{2,1,0:T(8,128)(2,1)S(1)} %all-to-all-done.2), kind=kOutput, calls=%fused_computation.5 | convolution fusion | flops 536870912 | bytes 3145728 | tf_op jit(solution)/shard_map/ktc,cqo->kqto/dot_general | solution.py:103
  129.9 5.0 %collective-permute-start.2 = (f32[8,4,64,64]{3,2,1,0:T(8,128)S(1)}, f32[8,4,64,64]{3,2,1,0:T(8,128)}, u32[]{:S(2)}, u32[]{:S(2)}) collective-permute-start(f32[8,4,64,64]{3,2,1,0:T(8,128)S(1)} %dynamic-slice_bitcast_fusion), channel_id=1, source_target_pairs={{0,1},{1,0},{2,3},{3,2},{4,5},{5,4},{6,7},{7,6},{8,9},{9,8},{10,11... | collective-permute-start | bytes 1572872 | tf_op jit(solution)/shard_map/ppermute | solution.py:110
  134.9 2.4 %collective-permute-done.2 = f32[8,4,64,64]{3,2,1,0:T(8,128)} collective-permute-done((f32[8,4,64,64]{3,2,1,0:T(8,128)S(1)}, f32[8,4,64,64]{3,2,1,0:T(8,128)}, u32[]{:S(2)}, u32[]{:S(2)}) %collective-permute-start.2) | collective-permute-done | bytes 524320 | tf_op jit(solution)/shard_map/ppermute | solution.py:110
  137.3 1.4 bitcast_add_fusion
  138.7 0.7 reshape.145
  139.3 18.5 %all_to_all.20 = f32[32,1,4096]{2,1,0:T(1,128)S(1)} all-to-all(f32[32,1,4096]{2,1,0:T(1,128)S(1)} %reshape.145), channel_id=1, replica_groups=mesh['chi'=8,'clo'=8,'x'=4,'core'=2] {'clo','x'}, dimensions={0} | all-to-all | bytes 1048576 | tf_op jit(solution)/shard_map/all_to_all | solution.py:112
  157.8 0.5 broadcast.110
  158.3 1.9 %reduce = f32[32,4096]{1,0:T(8,128)S(1)} reduce(f32[32,1,4096]{2,1,0:T(1,128)S(1)} %all_to_all.20, f32[]{:T(128)} %broadcast.110), dimensions={1}, to_apply=%all_to_all.15.reduce_sub_computation | reduce | bytes 1048580 | tf_op jit(solution)/shard_map/all_to_all | solution.py:112
  160.2 0.4 reshape.146
  160.8 0.8 reshape.141
  (33 shorter events, 2.5 us)
Async XLA Ops:
  7.4 6.2 %collective-permute-start = (bf16[3,2,1024]{2,1,0:T(2,128)(2,1)S(1)}, bf16[3,2,1024]{2,1,0:T(2,128)(2,1)S(1)}, u32[]{:S(2)}, u32[]{:S(2)}) collective-permute-start(bf16[3,2,1024]{2,1,0:T(2,128)(2,1)S(1)} %slice.29), channel_id=1, source_target_pairs={{0,8},{8,16},{16,24},{24,32},{32,40},{40,48},{48,56},{56,64},{64,7... | collective-permute-start | bytes 36872 | tf_op jit(solution)/shard_map/ppermute | solution.py:15
  17.0 12.5 %all-to-all-start = ((f32[8,16,1024]{2,1,0:T(8,128)}), f32[8,16,1024]{2,1,0:T(8,128)S(1)}, u32[]{:S(2)}, u32[]{:S(2)}) async-start(f32[8,16,1024]{2,1,0:T(8,128)} %broadcast_in_dim.34), calls=%async_computation | async-start | bytes 1048576 | tf_op jit(solution)/shard_map/all_to_all | solution.py:75
  22.4 30.2 %copy-start = (bf16[64,4096]{1,0:T(8,128)(2,1)S(1)}, bf16[64,4096]{1,0:T(8,128)(2,1)}, u32[]{:S(2)}) copy-start(bf16[64,4096]{1,0:T(8,128)(2,1)} %constant.67.clone) | copy-start | bytes 1572868
  29.9 0.7 collective-permute-start.1
  31.5 27.3 %all-to-all-start.1 = ((f32[8,16,1024]{2,1,0:T(8,128)}), f32[8,16,1024]{2,1,0:T(8,128)S(1)}, u32[]{:S(2)}, u32[]{:S(2)}) async-start(f32[8,16,1024]{2,1,0:T(8,128)} %broadcast_in_dim.36), calls=%async_computation.1 | async-start | bytes 1048576 | tf_op jit(solution)/shard_map/all_to_all | solution.py:89
  54.9 5.5 %copy-start.1 = (f32[1024]{0:T(1024)S(1)}, f32[1024]{0:T(1024)}, u32[]{:S(2)}) copy-start(f32[1024]{0:T(1024)} %param.11) | copy-start | bytes 12292
  61.7 65.6 %all-to-all-start.2 = ((bf16[8,64,1024]{2,1,0:T(8,128)(2,1)}), bf16[8,64,1024]{2,1,0:T(8,128)(2,1)S(1)}, u32[]{:S(2)}, u32[]{:S(2)}) async-start(bf16[8,64,1024]{2,1,0:T(8,128)(2,1)} %broadcast_in_dim.68), calls=%async_computation.2 | async-start | bytes 2097152 | tf_op jit(solution)/shard_map/all_to_all | solution.py:102
  65.3 62.0 %all-gather.2.cloned.1.call-start = ((), (), s32[]{:S(2)}) async-start(), calls=%async_computation.4 | async-start | bytes 1179648 | tf_op jit(solution)/shard_map/all_gather | solution.py:31
  129.9 7.4 %collective-permute-start.2 = (f32[8,4,64,64]{3,2,1,0:T(8,128)S(1)}, f32[8,4,64,64]{3,2,1,0:T(8,128)}, u32[]{:S(2)}, u32[]{:S(2)}) collective-permute-start(f32[8,4,64,64]{3,2,1,0:T(8,128)S(1)} %dynamic-slice_bitcast_fusion), channel_id=1, source_target_pairs={{0,1},{1,0},{2,3},{3,2},{4,5},{5,4},{6,7},{7,6},{8,9},{9,8},{10,11... | collective-permute-start | bytes 1572872 | tf_op jit(solution)/shard_map/ppermute | solution.py:110
Sparse Core Ops, SparseCore 0:
  68.2 59.0 all-gather.1

commit v9 on v7

--- a/solution.py
+++ b/solution.py
@@ -31,15 +31,24 @@
         weight = lax.all_gather(out_weight, "chi", axis=1, tiled=True)
         weight = weight.reshape(chans, n_tp, -1)
 
-        rim = shifted(features[:, rows - (taps - 1) :, :], CTX, n_ctx, 1)
-        extended = jnp.concatenate([rim, features], axis=1)
-        conv = jnp.zeros(features.shape, jnp.float32)
-        for j in range(taps):
-            conv = conv + short_weight[:, j][:, None, :] * extended[
-                :, taps - 1 - j : taps - 1 - j + rows, :
-            ].astype(jnp.float32)
+        edge = taps - 1
+        rim = shifted(features[:, rows - edge :, :], CTX, n_ctx, 1)
+
+        def conv_of(extended, count):
+            total = jnp.zeros((features.shape[0], count, chans), jnp.float32)
+            for j in range(taps):
+                total = total + short_weight[:, j][:, None, :] * extended[
+                    :, edge - j : edge - j + count, :
+                ].astype(jnp.float32)
+            return total
+
+        inner = conv_of(features, rows - edge)
+        outer = conv_of(jnp.concatenate([rim, features[:, :edge, :]], axis=1), edge)
+        conv = jnp.concatenate([outer, inner], axis=1)
         q_lane = conv[0]
-        gated = (conv[1] * conv[2]).astype(jnp.bfloat16)
+        gated_inner = (inner[1] * inner[2]).astype(jnp.bfloat16)
+        gated_outer = (outer[1] * outer[2]).astype(jnp.bfloat16)
+        gated = jnp.concatenate([gated_outer, gated_inner], axis=0)
         gated_wide = gated.astype(jnp.float32)
 
         coef = residue * jnp.sqrt(-jnp.expm1(-2.0 * decay_rate))
@@ -69,7 +78,9 @@
             return jnp.exp(-rate_c * (rows * jnp.asarray(blocks, jnp.float32)))
 
         end_basis = jnp.exp(-rate_c[None] * (rows - 1.0 - lags)[:, None, None])
-        own_state = jnp.sum(end_basis * gated_wide[:, None, :], axis=0)
+        own_state = jnp.sum(
+            end_basis[edge:] * gated_inner.astype(jnp.float32)[:, None, :], axis=0
+        ) + jnp.sum(end_basis[:edge] * gated_outer.astype(jnp.float32)[:, None, :], axis=0)
 
         spread = jnp.broadcast_to(own_state[None], (n_lo,) + own_state.shape)
         got = lax.all_to_all(spread, "clo", 0, 0, tiled=True)

time: 166 us -> 165 us (level)
  waiting for transfers between devices: 73.2 us -> 70.2 us
    all_to_all x1, waiting for transfers between devices: 3.63 us -> 1.72 us  [per_device(): totals = lax.all_to_all(spread, 'clo', 0, 0, tiled=True)[:n_tp]]
  transfers between devices with their start and end apart: 7 -> 7, of which waited for: 4 -> 4; matrix products, arithmetic and copies ran while one was open for 3% -> 7% of each run, Pallas kernels for 0% -> 0%
where the time goes in v9:
time: 165 us
  waiting for transfers between devices  70.2 us (43%)
  starting transfers between devices  37 us (22%)
  blocking collectives  18.8 us (11%)
  between operations  13.7 us (8%)
  local copies, waits for them, and re-layouts  10.7 us (6%)
  other arithmetic  9.86 us (6%)
  matrix products  4.41 us (3%)
    all_gather x1, waiting for transfers between devices, per_device(): weight = lax.all_gather(out_weight, 'chi', axis=1, tiled=True)  58.2 us
    all_to_all x1, blocking collectives, per_device(): pieces = lax.all_to_all(mine, ('clo', 'x'), 0, 0, tiled=True)  18.8 us
    all_to_all x1, starting transfers between devices, per_device(): totals = lax.all_to_all(spread, 'clo', 0, 0, tiled=True)[:n_tp]  18.4 us
    all_to_all x1, waiting for transfers between devices, per_device(): got = lax.all_to_all(spread, 'clo', 0, 0, tiled=True)  7.16 us
    all_to_all x1, starting transfers between devices, per_device(): got = lax.all_to_all(spread, 'clo', 0, 0, tiled=True)  5.37 us
    ppermute x1, starting transfers between devices, per_device(): mine = mine + lax.ppermute(other, 'core', [(0, 1), (1, 0)])  4.96 us
    ppermute x1, starting transfers between devices, shifted(): return lax.ppermute(value, axis, pairs)  4.02 us
    all_to_all x1, starting transfers between devices, per_device(): tokens = lax.all_to_all(spread, 'clo', 0, 0, tiled=True)  3.56 us
  transfers between devices with their start and end apart: 7, of which 4 were waited for; matrix products, arithmetic and copies ran while one was open for 7% of the time, Pallas kernels for 0%

profile of v9, /device:TPU:1, one launch (start us, length us, event | category | flops | bytes accessed | tf_op | source)
XLA Modules:
  0.0 164.7 jit_solution(9067438774506481698)
XLA Ops:
  6.5 0.8 fusion.18
  7.4 4.0 %collective-permute-start = (bf16[3,2,1024]{2,1,0:T(2,128)(2,1)S(1)}, bf16[3,2,1024]{2,1,0:T(2,128)(2,1)S(1)}, u32[]{:S(2)}, u32[]{:S(2)}) collective-permute-start(bf16[3,2,1024]{2,1,0:T(2,128)(2,1)S(1)} %get-tuple-element.12), channel_id=1, source_target_pairs={{0,8},{8,16},{16,24},{24,32},{32,40},{40,48},{48,56},{56,64},{64,7... | collective-permute-start | bytes 36872 | tf_op jit(solution)/shard_map/ppermute | solution.py:15
  11.4 0.9 fusion.19
  12.4 0.7 negate_bitcast_fusion
  13.6 1.8 %multiply_add_fusion = f32[3,62,1024]{2,1,0:T(8,128)S(1)} fusion(bf16[3,64,1024]{2,1,0:T(8,128)(2,1)} %param.7, f32[3,1024]{1,0:T(4,128)S(1)} %get-tuple-element.19, f32[3,1024]{1,0:T(4,128)S(1)} %get-tuple-element.20, f32[3,1024]{1,0:T(4,128)S(1)} %bitcast.63), kind=kLoop, calls=%fused_computation.10 | loop fusion | flops 1523712 | bytes 1941504 | tf_op jit(solution)/shard_map/add | solution.py:40
  15.5 0.6 multiply_exponential_fusion
  16.1 0.8 fusion
  17.0 0.8 broadcast_in_dim.34
  17.8 5.4 %all-to-all-start = ((f32[8,16,1024]{2,1,0:T(8,128)}), f32[8,16,1024]{2,1,0:T(8,128)S(1)}, u32[]{:S(2)}, u32[]{:S(2)}) async-start(f32[8,16,1024]{2,1,0:T(8,128)} %broadcast_in_dim.34), calls=%async_computation | async-start | bytes 1048576 | tf_op jit(solution)/shard_map/all_to_all | solution.py:86
  23.2 7.2 %all-to-all-done = f32[8,16,1024]{2,1,0:T(8,128)S(1)} async-done(((f32[8,16,1024]{2,1,0:T(8,128)}), f32[8,16,1024]{2,1,0:T(8,128)S(1)}, u32[]{:S(2)}, u32[]{:S(2)}) %all-to-all-start) | async-done | bytes 524320 | tf_op jit(solution)/shard_map/all_to_all | solution.py:86
  30.7 0.7 collective-permute-start.1
  31.4 0.8 broadcast_in_dim.36
  32.3 18.4 %all-to-all-start.1 = ((f32[8,16,1024]{2,1,0:T(8,128)}), f32[8,16,1024]{2,1,0:T(8,128)S(1)}, u32[]{:S(2)}, u32[]{:S(2)}) async-start(f32[8,16,1024]{2,1,0:T(8,128)} %broadcast_in_dim.36), calls=%async_computation.1 | async-start | bytes 1048576 | tf_op jit(solution)/shard_map/all_to_all | solution.py:98
  52.1 1.1 reshape.204
  53.3 0.9 copy.29
  54.2 1.6 fusion.6
  56.0 1.7 %all-to-all-done.1 = f32[8,16,1024]{2,1,0:T(8,128)S(1)} async-done(((f32[8,16,1024]{2,1,0:T(8,128)}), f32[8,16,1024]{2,1,0:T(8,128)S(1)}, u32[]{:S(2)}, u32[]{:S(2)}) %all-to-all-start.1) | async-done | bytes 524320 | tf_op jit(solution)/shard_map/all_to_all | solution.py:98
  58.0 1.4 multiply_reduce_fusion
  59.5 1.2 broadcast_in_dim.38
  60.7 3.6 %all-to-all-start.2 = ((bf16[8,64,1024]{2,1,0:T(8,128)(2,1)}), bf16[8,64,1024]{2,1,0:T(8,128)(2,1)S(1)}, u32[]{:S(2)}, u32[]{:S(2)}) async-start(bf16[8,64,1024]{2,1,0:T(8,128)(2,1)} %broadcast_in_dim.38), calls=%async_computation.2 | async-start | bytes 2097152 | tf_op jit(solution)/shard_map/all_to_all | solution.py:110
  64.3 0.7 all-gather.2.cloned.1.call-update
  65.0 58.2 %all-gather.2.cloned.1.call-done = bf16[1024,512]{0,1:T(8,128)(2,1)} async-done(((bf16[1024,64]{0,1:T(8,128)(2,1)}), bf16[1024,512]{0,1:T(8,128)(2,1)}) %all-gather.2.cloned.1.call-update) | async-done | bytes 1048592 | tf_op jit(solution)/shard_map/all_gather | solution.py:31
  123.2 2.5 %fusion.1 = f32[8,64,8,64]{3,1,2,0:T(8,128)S(1)} fusion(bf16[1024,8,64,1]{0,2,1,3:T(8,128)(2,1)} %bitcast.66, bf16[8,64,1024]{2,1,0:T(8,128)(2,1)S(1)} %all-to-all-done.2), kind=kOutput, calls=%fused_computation.5 | convolution fusion | flops 536870912 | bytes 3145728 | tf_op jit(solution)/shard_map/ktc,cqo->kqto/dot_general | solution.py:111
  125.8 5.0 %collective-permute-start.2 = (f32[8,4,64,64]{3,2,1,0:T(8,128)S(1)}, f32[8,4,64,64]{3,2,1,0:T(8,128)}, u32[]{:S(2)}, u32[]{:S(2)}) collective-permute-start(f32[8,4,64,64]{3,2,1,0:T(8,128)S(1)} %dynamic-slice_bitcast_fusion), channel_id=1, source_target_pairs={{0,1},{1,0},{2,3},{3,2},{4,5},{5,4},{6,7},{7,6},{8,9},{9,8},{10,11... | collective-permute-start | bytes 1572872 | tf_op jit(solution)/shard_map/ppermute | solution.py:118
  130.8 2.4 %collective-permute-done.2 = f32[8,4,64,64]{3,2,1,0:T(8,128)} collective-permute-done((f32[8,4,64,64]{3,2,1,0:T(8,128)S(1)}, f32[8,4,64,64]{3,2,1,0:T(8,128)}, u32[]{:S(2)}, u32[]{:S(2)}) %collective-permute-start.2) | collective-permute-done | bytes 524320 | tf_op jit(solution)/shard_map/ppermute | solution.py:118
  133.2 1.4 bitcast_add_fusion
  134.5 0.7 reshape.215
  135.2 18.8 %all_to_all.20 = f32[32,1,4096]{2,1,0:T(1,128)S(1)} all-to-all(f32[32,1,4096]{2,1,0:T(1,128)S(1)} %reshape.215), channel_id=1, replica_groups=mesh['chi'=8,'clo'=8,'x'=4,'core'=2] {'clo','x'}, dimensions={0} | all-to-all | bytes 1048576 | tf_op jit(solution)/shard_map/all_to_all | solution.py:120
  154.0 0.5 broadcast.126
  154.5 1.9 %reduce = f32[32,4096]{1,0:T(8,128)S(1)} reduce(f32[32,1,4096]{2,1,0:T(1,128)S(1)} %all_to_all.20, f32[]{:T(128)} %broadcast.126), dimensions={1}, to_apply=%all_to_all.15.reduce_sub_computation | reduce | bytes 1048580 | tf_op jit(solution)/shard_map/all_to_all | solution.py:120
  156.4 0.4 reshape.216
  157.0 0.8 reshape.210
  (39 shorter events, 3.3 us)
Async XLA Ops:
  7.4 9.5 %collective-permute-start = (bf16[3,2,1024]{2,1,0:T(2,128)(2,1)S(1)}, bf16[3,2,1024]{2,1,0:T(2,128)(2,1)S(1)}, u32[]{:S(2)}, u32[]{:S(2)}) collective-permute-start(bf16[3,2,1024]{2,1,0:T(2,128)(2,1)S(1)} %get-tuple-element.12), channel_id=1, source_target_pairs={{0,8},{8,16},{16,24},{24,32},{32,40},{40,48},{48,56},{56,64},{64,7... | collective-permute-start | bytes 36872 | tf_op jit(solution)/shard_map/ppermute | solution.py:15
  16.9 35.0 %copy-start = (bf16[64,4096]{1,0:T(8,128)(2,1)S(1)}, bf16[64,4096]{1,0:T(8,128)(2,1)}, u32[]{:S(2)}) copy-start(bf16[64,4096]{1,0:T(8,128)(2,1)} %constant.47.clone) | copy-start | bytes 1572868
  17.8 12.5 %all-to-all-start = ((f32[8,16,1024]{2,1,0:T(8,128)}), f32[8,16,1024]{2,1,0:T(8,128)S(1)}, u32[]{:S(2)}, u32[]{:S(2)}) async-start(f32[8,16,1024]{2,1,0:T(8,128)} %broadcast_in_dim.34), calls=%async_computation | async-start | bytes 1048576 | tf_op jit(solution)/shard_map/all_to_all | solution.py:86
  30.7 0.7 collective-permute-start.1
  32.3 25.5 %all-to-all-start.1 = ((f32[8,16,1024]{2,1,0:T(8,128)}), f32[8,16,1024]{2,1,0:T(8,128)S(1)}, u32[]{:S(2)}, u32[]{:S(2)}) async-start(f32[8,16,1024]{2,1,0:T(8,128)} %broadcast_in_dim.36), calls=%async_computation.1 | async-start | bytes 1048576 | tf_op jit(solution)/shard_map/all_to_all | solution.py:98
  51.8 7.6 %copy-start.1 = (f32[1024]{0:T(1024)S(1)}, f32[1024]{0:T(1024)}, u32[]{:S(2)}) copy-start(f32[1024]{0:T(1024)} %param.11) | copy-start | bytes 12292
  60.7 62.5 %all-to-all-start.2 = ((bf16[8,64,1024]{2,1,0:T(8,128)(2,1)}), bf16[8,64,1024]{2,1,0:T(8,128)(2,1)S(1)}, u32[]{:S(2)}, u32[]{:S(2)}) async-start(bf16[8,64,1024]{2,1,0:T(8,128)(2,1)} %broadcast_in_dim.38), calls=%async_computation.2 | async-start | bytes 2097152 | tf_op jit(solution)/shard_map/all_to_all | solution.py:110
  64.2 59.0 %all-gather.2.cloned.1.call-start = ((), (), s32[]{:S(2)}) async-start(), calls=%async_computation.4 | async-start | bytes 1179648 | tf_op jit(solution)/shard_map/all_gather | solution.py:31
  125.8 7.4 %collective-permute-start.2 = (f32[8,4,64,64]{3,2,1,0:T(8,128)S(1)}, f32[8,4,64,64]{3,2,1,0:T(8,128)}, u32[]{:S(2)}, u32[]{:S(2)}) collective-permute-start(f32[8,4,64,64]{3,2,1,0:T(8,128)S(1)} %dynamic-slice_bitcast_fusion), channel_id=1, source_target_pairs={{0,1},{1,0},{2,3},{3,2},{4,5},{5,4},{6,7},{7,6},{8,9},{9,8},{10,11... | collective-permute-start | bytes 1572872 | tf_op jit(solution)/shard_map/ppermute | solution.py:118
Sparse Core Ops, SparseCore 0:
  67.1 56.0 all-gather.1

commit v10 on v7

--- a/solution.py
+++ b/solution.py
@@ -97,14 +97,15 @@
 
         spread = jnp.broadcast_to(mixed[None], (n_lo,) + mixed.shape)
         tokens = lax.all_to_all(spread, "clo", 0, 0, tiled=True)
-        partial = jnp.einsum(
-            "ktc,cqo->kqto", tokens, weight, preferred_element_type=jnp.float32
-        )
-        partial = partial.reshape((n_lo, n_x, 2) + partial.shape[2:])
+        halves = weight.reshape(chans, n_x, 2, -1)
         core = lax.axis_index("core")
-        mine = lax.dynamic_index_in_dim(partial, core, 2, keepdims=False)
-        other = lax.dynamic_index_in_dim(partial, 1 - core, 2, keepdims=False)
-        mine = mine + lax.ppermute(other, "core", [(0, 1), (1, 0)])
+        w_mine = lax.dynamic_index_in_dim(halves, core, 2, keepdims=False)
+        w_other = lax.dynamic_index_in_dim(halves, 1 - core, 2, keepdims=False)
+        w_mine, w_other = lax.optimization_barrier((w_mine, w_other))
+        other = jnp.einsum("ktc,cqo->kqto", tokens, w_other, preferred_element_type=jnp.float32)
+        sent = lax.ppermute(other, "core", [(0, 1), (1, 0)])
+        mine = jnp.einsum("ktc,cqo->kqto", tokens, w_mine, preferred_element_type=jnp.float32)
+        mine = lax.optimization_barrier(mine) + sent
         mine = mine.reshape((n_lo * n_x,) + mine.shape[2:])
         pieces = lax.all_to_all(mine, ("clo", "x"), 0, 0, tiled=True)
         pieces = pieces.reshape((n_lo, n_x) + pieces.shape[1:])

time: 166 us -> 163 us (0.982)
  other arithmetic: 9.11 us -> 6.37 us
  transfers between devices with their start and end apart: 7 -> 7, of which waited for: 4 -> 4; matrix products, arithmetic and copies ran while one was open for 3% -> 5% of each run, Pallas kernels for 0% -> 0%
where the time goes in v10:
time: 163 us; the launch traced here: 162 us
  waiting for transfers between devices  72.3 us (44%)
  starting transfers between devices  37.5 us (23%)
  blocking collectives  18.5 us (11%)
  between operations  13.8 us (8%)
  local copies, waits for them, and re-layouts  11.3 us (7%)
  other arithmetic  6.37 us (4%)
  matrix products  2.37 us (1%)
    all_gather x1, waiting for transfers between devices, per_device(): weight = lax.all_gather(out_weight, 'chi', axis=1, tiled=True)  59.3 us
    all_to_all x1, starting transfers between devices, per_device(): totals = lax.all_to_all(spread, 'clo', 0, 0, tiled=True)[:n_tp]  18.7 us
    all_to_all x1, blocking collectives, per_device(): pieces = lax.all_to_all(mine, ('clo', 'x'), 0, 0, tiled=True)  18.5 us
    all_to_all x1, waiting for transfers between devices, per_device(): got = lax.all_to_all(spread, 'clo', 0, 0, tiled=True)  7.16 us
    all_to_all x1, starting transfers between devices, per_device(): got = lax.all_to_all(spread, 'clo', 0, 0, tiled=True)  5.37 us
    ppermute x1, starting transfers between devices, per_device(): sent = lax.ppermute(other, 'core', [(0, 1), (1, 0)])  5.02 us
    ppermute x1, starting transfers between devices, shifted(): return lax.ppermute(value, axis, pairs)  4.02 us
    all_to_all x1, waiting for transfers between devices, per_device(): totals = lax.all_to_all(spread, 'clo', 0, 0, tiled=True)[:n_tp]  3.64 us
  transfers between devices with their start and end apart: 7, of which 4 were waited for; matrix products, arithmetic and copies ran while one was open for 5% of the time, Pallas kernels for 0%

profile of v10, /device:TPU:1, one launch (start us, length us, event | category | flops | bytes accessed | tf_op | source)
XLA Modules:
  0.0 162.1 jit_solution(18278218353670277228)
XLA Ops:
  6.5 0.9 slice.29
  7.4 4.0 %collective-permute-start = (bf16[3,2,1024]{2,1,0:T(2,128)(2,1)S(1)}, bf16[3,2,1024]{2,1,0:T(2,128)(2,1)S(1)}, u32[]{:S(2)}, u32[]{:S(2)}) collective-permute-start(bf16[3,2,1024]{2,1,0:T(2,128)(2,1)S(1)} %slice.29), channel_id=1, source_target_pairs={{0,8},{8,16},{16,24},{24,32},{32,40},{40,48},{48,56},{56,64},{64,7... | collective-permute-start | bytes 36872 | tf_op jit(solution)/shard_map/ppermute | solution.py:15
  11.5 0.9 fusion.12
  12.4 0.7 negate_bitcast_fusion
  14.0 0.7 multiply_reduce_fusion.1
  14.8 0.8 broadcast_in_dim.34
  15.6 5.4 %all-to-all-start = ((f32[8,16,1024]{2,1,0:T(8,128)}), f32[8,16,1024]{2,1,0:T(8,128)S(1)}, u32[]{:S(2)}, u32[]{:S(2)}) async-start(f32[8,16,1024]{2,1,0:T(8,128)} %broadcast_in_dim.34), calls=%async_computation | async-start | bytes 1048576 | tf_op jit(solution)/shard_map/all_to_all | solution.py:75
  21.0 7.2 %all-to-all-done = f32[8,16,1024]{2,1,0:T(8,128)S(1)} async-done(((f32[8,16,1024]{2,1,0:T(8,128)}), f32[8,16,1024]{2,1,0:T(8,128)S(1)}, u32[]{:S(2)}, u32[]{:S(2)}) %all-to-all-start) | async-done | bytes 524320 | tf_op jit(solution)/shard_map/all_to_all | solution.py:75
  28.1 0.3 multiply_reduce_fusion.3
  28.5 0.8 collective-permute-start.1
  29.3 0.8 broadcast_in_dim.36
  30.2 18.7 %all-to-all-start.1 = ((f32[8,16,1024]{2,1,0:T(8,128)}), f32[8,16,1024]{2,1,0:T(8,128)S(1)}, u32[]{:S(2)}, u32[]{:S(2)}) async-start(f32[8,16,1024]{2,1,0:T(8,128)} %broadcast_in_dim.36), calls=%async_computation.1 | async-start | bytes 1048576 | tf_op jit(solution)/shard_map/all_to_all | solution.py:87
  49.0 0.4 multiply_reduce_fusion.5
  49.7 1.1 reshape.129
  51.5 0.6 fusion.13
  52.3 3.6 %all-to-all-done.1 = f32[8,16,1024]{2,1,0:T(8,128)S(1)} async-done(((f32[8,16,1024]{2,1,0:T(8,128)}), f32[8,16,1024]{2,1,0:T(8,128)S(1)}, u32[]{:S(2)}, u32[]{:S(2)}) %all-to-all-start.1) | async-done | bytes 524320 | tf_op jit(solution)/shard_map/all_to_all | solution.py:87
  56.2 1.4 multiply_reduce_fusion
  57.7 1.1 broadcast_in_dim.68
  58.8 3.6 %all-to-all-start.2 = ((bf16[8,64,1024]{2,1,0:T(8,128)(2,1)}), bf16[8,64,1024]{2,1,0:T(8,128)(2,1)S(1)}, u32[]{:S(2)}, u32[]{:S(2)}) async-start(bf16[8,64,1024]{2,1,0:T(8,128)(2,1)} %broadcast_in_dim.68), calls=%async_computation.2 | async-start | bytes 2097152 | tf_op jit(solution)/shard_map/all_to_all | solution.py:99
  62.4 0.7 all-gather.2.cloned.1.call-update
  63.1 59.3 %all-gather.2.cloned.1.call-done = bf16[1024,512]{0,1:T(8,128)(2,1)} async-done(((bf16[1024,64]{0,1:T(8,128)(2,1)}), bf16[1024,512]{0,1:T(8,128)(2,1)}) %all-gather.2.cloned.1.call-update) | async-done | bytes 1048592 | tf_op jit(solution)/shard_map/all_gather | solution.py:31
  122.4 1.3 dynamic-slice_bitcast_fusion
  123.8 0.7 convolution_bitcast_fusion
  124.5 5.0 %collective-permute-start.2 = (f32[8,4,64,64]{2,3,0,1:T(8,128)S(1)}, f32[8,4,64,64]{2,3,0,1:T(8,128)S(1)}, u32[]{:S(2)}, u32[]{:S(2)}) collective-permute-start(f32[8,4,64,64]{2,3,0,1:T(8,128)S(1)} %convolution_bitcast_fusion), channel_id=1, source_target_pairs={{0,1},{1,0},{2,3},{3,2},{4,5},{5,4},{6,7},{7,6},{8,9},{9,8},{10,11... | collective-permute-start | bytes 1572872 | tf_op jit(solution)/shard_map/ppermute | solution.py:106
  129.5 0.7 convolution_bitcast_fusion.1
  130.3 1.5 collective-permute-done.2
  132.3 0.7 reshape.138
  133.0 18.5 %all_to_all.20 = f32[32,1,4096]{2,1,0:T(1,128)S(1)} all-to-all(f32[32,1,4096]{2,1,0:T(1,128)S(1)} %reshape.138), channel_id=1, replica_groups=mesh['chi'=8,'clo'=8,'x'=4,'core'=2] {'clo','x'}, dimensions={0} | all-to-all | bytes 1048576 | tf_op jit(solution)/shard_map/all_to_all | solution.py:110
  151.4 0.5 broadcast.109
  152.0 1.9 %reduce = f32[32,4096]{1,0:T(8,128)S(1)} reduce(f32[32,1,4096]{2,1,0:T(1,128)S(1)} %all_to_all.20, f32[]{:T(128)} %broadcast.109), dimensions={1}, to_apply=%all_to_all.15.reduce_sub_computation | reduce | bytes 1048580 | tf_op jit(solution)/shard_map/all_to_all | solution.py:110
  153.9 0.4 reshape.139
  154.5 0.8 reshape.133
  (37 shorter events, 3.1 us)
Async XLA Ops:
  6.5 7.1 %copy-start.1 = (bf16[3,64,1024]{2,1,0:T(8,128)(2,1)S(1)}, bf16[3,64,1024]{2,1,0:T(8,128)(2,1)}, u32[]{:S(2)}) copy-start(bf16[3,64,1024]{2,1,0:T(8,128)(2,1)} %param.7) | copy-start | bytes 1179652
  7.4 6.2 %collective-permute-start = (bf16[3,2,1024]{2,1,0:T(2,128)(2,1)S(1)}, bf16[3,2,1024]{2,1,0:T(2,128)(2,1)S(1)}, u32[]{:S(2)}, u32[]{:S(2)}) collective-permute-start(bf16[3,2,1024]{2,1,0:T(2,128)(2,1)S(1)} %slice.29), channel_id=1, source_target_pairs={{0,8},{8,16},{16,24},{24,32},{32,40},{40,48},{48,56},{56,64},{64,7... | collective-permute-start | bytes 36872 | tf_op jit(solution)/shard_map/ppermute | solution.py:15
  15.6 12.5 %all-to-all-start = ((f32[8,16,1024]{2,1,0:T(8,128)}), f32[8,16,1024]{2,1,0:T(8,128)S(1)}, u32[]{:S(2)}, u32[]{:S(2)}) async-start(f32[8,16,1024]{2,1,0:T(8,128)} %broadcast_in_dim.34), calls=%async_computation | async-start | bytes 1048576 | tf_op jit(solution)/shard_map/all_to_all | solution.py:75
  28.5 20.9 %copy-start = (bf16[64,4096]{1,0:T(8,128)(2,1)S(1)}, bf16[64,4096]{1,0:T(8,128)(2,1)}, u32[]{:S(2)}) copy-start(bf16[64,4096]{1,0:T(8,128)(2,1)} %constant.47.clone) | copy-start | bytes 1572868
  28.5 0.8 collective-permute-start.1
  30.2 25.8 %all-to-all-start.1 = ((f32[8,16,1024]{2,1,0:T(8,128)}), f32[8,16,1024]{2,1,0:T(8,128)S(1)}, u32[]{:S(2)}, u32[]{:S(2)}) async-start(f32[8,16,1024]{2,1,0:T(8,128)} %broadcast_in_dim.36), calls=%async_computation.1 | async-start | bytes 1048576 | tf_op jit(solution)/shard_map/all_to_all | solution.py:87
  56.2 1.4 copy-start.2
  58.8 64.9 %all-to-all-start.2 = ((bf16[8,64,1024]{2,1,0:T(8,128)(2,1)}), bf16[8,64,1024]{2,1,0:T(8,128)(2,1)S(1)}, u32[]{:S(2)}, u32[]{:S(2)}) async-start(bf16[8,64,1024]{2,1,0:T(8,128)(2,1)} %broadcast_in_dim.68), calls=%async_computation.2 | async-start | bytes 2097152 | tf_op jit(solution)/shard_map/all_to_all | solution.py:99
  62.4 60.1 %all-gather.2.cloned.1.call-start = ((), (), s32[]{:S(2)}) async-start(), calls=%async_computation.4 | async-start | bytes 1179648 | tf_op jit(solution)/shard_map/all_gather | solution.py:31
  124.5 7.3 %collective-permute-start.2 = (f32[8,4,64,64]{2,3,0,1:T(8,128)S(1)}, f32[8,4,64,64]{2,3,0,1:T(8,128)S(1)}, u32[]{:S(2)}, u32[]{:S(2)}) collective-permute-start(f32[8,4,64,64]{2,3,0,1:T(8,128)S(1)} %convolution_bitcast_fusion), channel_id=1, source_target_pairs={{0,1},{1,0},{2,3},{3,2},{4,5},{5,4},{6,7},{7,6},{8,9},{9,8},{10,11... | collective-permute-start | bytes 1572872 | tf_op jit(solution)/shard_map/ppermute | solution.py:106
Sparse Core Ops, SparseCore 0:
  65.3 57.1 all-gather.1

commit v11 on v10

--- a/solution.py
+++ b/solution.py
@@ -76,8 +76,14 @@
         src = jnp.arange(n_lo)
         gap = jnp.maximum(clo - src - 1, 0)[:, None, None]
         inside = jnp.where((src < clo)[:, None, None], decay(gap), 0.0)
+        to_end = decay((n_lo - 1 - src)[:, None, None])
+        rows_before = jnp.arange(n_tp)
+        lag = jnp.maximum(chi - rows_before - 1, 0)[:, None, None]
+        outside = jnp.where((rows_before < chi)[:, None, None], decay(n_lo * lag), 0.0)
+        outside = outside * decay(clo)
+        inside, to_end, outside = lax.optimization_barrier((inside, to_end, outside))
         before = jnp.sum(inside * got, axis=0)
-        group_total = jnp.sum(decay((n_lo - 1 - src)[:, None, None]) * got, axis=0)
+        group_total = jnp.sum(to_end * got, axis=0)
         flip = [
             (c * n_lo + m, m * n_lo + c) for c in range(n_tp) for m in range(n_tp) if c != m
         ]
@@ -85,10 +91,7 @@
         turned = jnp.where(chi == clo, group_total, turned)
         spread = jnp.broadcast_to(turned[None], (n_lo,) + turned.shape)
         totals = lax.all_to_all(spread, "clo", 0, 0, tiled=True)[:n_tp]
-        rows_before = jnp.arange(n_tp)
-        lag = jnp.maximum(chi - rows_before - 1, 0)[:, None, None]
-        outside = jnp.where((rows_before < chi)[:, None, None], decay(n_lo * lag), 0.0)
-        before = before + decay(clo) * jnp.sum(outside * totals, axis=0)
+        before = before + jnp.sum(outside * totals, axis=0)
 
         far_basis = coef_c[None] * jnp.exp(-rate_c[None] * (lags + 1.0)[:, None, None])
         far = jnp.sum(far_basis * before[None], axis=1)

time: 163 us -> 163 us (level)
  waiting for transfers between devices: 72.3 us -> 69.2 us
    all_to_all x1, waiting for transfers between devices: 3.64 us -> 1.43 us  [per_device(): totals = lax.all_to_all(spread, 'clo', 0, 0, tiled=True)[:n_tp]]
  transfers between devices with their start and end apart: 7 -> 7, of which waited for: 4 -> 4; matrix products, arithmetic and copies ran while one was open for 5% -> 6% of each run, Pallas kernels for 0% -> 0%
where the time goes in v11:
time: 163 us
  waiting for transfers between devices  69.2 us (42%)
  starting transfers between devices  38 us (23%)
  blocking collectives  19 us (12%)
  between operations  13.8 us (8%)
  local copies, waits for them, and re-layouts  12.6 us (8%)
  other arithmetic  7.04 us (4%)
  matrix products  3.32 us (2%)
    all_gather x1, waiting for transfers between devices, per_device(): weight = lax.all_gather(out_weight, 'chi', axis=1, tiled=True)  58.8 us
    all_to_all x1, blocking collectives, per_device(): pieces = lax.all_to_all(mine, ('clo', 'x'), 0, 0, tiled=True)  19 us
    all_to_all x1, starting transfers between devices, per_device(): totals = lax.all_to_all(spread, 'clo', 0, 0, tiled=True)[:n_tp]  18.8 us
    all_to_all x1, waiting for transfers between devices, per_device(): got = lax.all_to_all(spread, 'clo', 0, 0, tiled=True)  6.72 us
    all_to_all x1, starting transfers between devices, per_device(): got = lax.all_to_all(spread, 'clo', 0, 0, tiled=True)  5.37 us
    ppermute x1, starting transfers between devices, per_device(): sent = lax.ppermute(other, 'core', [(0, 1), (1, 0)])  4.8 us
    all_to_all x1, starting transfers between devices, per_device(): tokens = lax.all_to_all(spread, 'clo', 0, 0, tiled=True)  4.3 us
    ppermute x1, starting transfers between devices, shifted(): return lax.ppermute(value, axis, pairs)  4.02 us
  transfers between devices with their start and end apart: 7, of which 4 were waited for; matrix products, arithmetic and copies ran while one was open for 6% of the time, Pallas kernels for 0%

profile of v11, /device:TPU:1, one launch (start us, length us, event | category | flops | bytes accessed | tf_op | source)
XLA Modules:
  0.0 162.8 jit_solution(7907064927806707126)
XLA Ops:
  6.5 0.9 slice.29
  7.4 4.0 %collective-permute-start = (bf16[3,2,1024]{2,1,0:T(2,128)(2,1)S(1)}, bf16[3,2,1024]{2,1,0:T(2,128)(2,1)S(1)}, u32[]{:S(2)}, u32[]{:S(2)}) collective-permute-start(bf16[3,2,1024]{2,1,0:T(2,128)(2,1)S(1)} %slice.29), channel_id=1, source_target_pairs={{0,8},{8,16},{16,24},{24,32},{32,40},{40,48},{48,56},{56,64},{64,7... | collective-permute-start | bytes 36872 | tf_op jit(solution)/shard_map/ppermute | solution.py:15
  11.5 0.9 fusion.12
  12.4 0.7 negate_bitcast_fusion
  14.0 0.7 multiply_reduce_fusion.1
  14.8 0.8 broadcast_in_dim.35
  15.6 5.4 %all-to-all-start = ((f32[8,16,1024]{2,1,0:T(8,128)}), f32[8,16,1024]{2,1,0:T(8,128)S(1)}, u32[]{:S(2)}, u32[]{:S(2)}) async-start(f32[8,16,1024]{2,1,0:T(8,128)} %broadcast_in_dim.35), calls=%async_computation | async-start | bytes 1048576 | tf_op jit(solution)/shard_map/all_to_all | solution.py:75
  21.4 6.7 %all-to-all-done = f32[8,16,1024]{2,1,0:T(8,128)S(1)} async-done(((f32[8,16,1024]{2,1,0:T(8,128)}), f32[8,16,1024]{2,1,0:T(8,128)S(1)}, u32[]{:S(2)}, u32[]{:S(2)}) %all-to-all-start) | async-done | bytes 524320 | tf_op jit(solution)/shard_map/all_to_all | solution.py:75
  28.2 0.7 multiply_reduce_fusion.3
  28.9 0.7 collective-permute-start.1
  29.6 0.9 broadcast_in_dim.36
  30.4 18.8 %all-to-all-start.1 = ((f32[8,16,1024]{2,1,0:T(8,128)}), f32[8,16,1024]{2,1,0:T(8,128)S(1)}, u32[]{:S(2)}, u32[]{:S(2)}) async-start(f32[8,16,1024]{2,1,0:T(8,128)} %broadcast_in_dim.36), calls=%async_computation.1 | async-start | bytes 1048576 | tf_op jit(solution)/shard_map/all_to_all | solution.py:93
  49.5 0.9 mul.249
  51.2 1.1 reshape.128
  52.3 0.8 copy.37
  53.1 1.6 fusion.13
  54.9 1.4 all-to-all-done.1
  56.5 1.4 multiply_reduce_fusion
  58.0 1.1 broadcast_in_dim.38
  59.1 4.3 %all-to-all-start.2 = ((bf16[8,64,1024]{2,1,0:T(8,128)(2,1)}), bf16[8,64,1024]{2,1,0:T(8,128)(2,1)S(1)}, u32[]{:S(2)}, u32[]{:S(2)}) async-start(bf16[8,64,1024]{2,1,0:T(8,128)(2,1)} %broadcast_in_dim.38), calls=%async_computation.2 | async-start | bytes 2097152 | tf_op jit(solution)/shard_map/all_to_all | solution.py:102
  63.4 0.7 all-gather.2.cloned.1.call-update
  64.1 58.8 %all-gather.2.cloned.1.call-done = bf16[1024,512]{0,1:T(8,128)(2,1)} async-done(((bf16[1024,64]{0,1:T(8,128)(2,1)}), bf16[1024,512]{0,1:T(8,128)(2,1)}) %all-gather.2.cloned.1.call-update) | async-done | bytes 1048592 | tf_op jit(solution)/shard_map/all_gather | solution.py:31
  122.9 1.3 dynamic-slice_bitcast_fusion
  124.2 0.7 convolution_bitcast_fusion
  125.0 4.8 %collective-permute-start.2 = (f32[8,4,64,64]{2,3,0,1:T(8,128)S(1)}, f32[8,4,64,64]{2,3,0,1:T(8,128)S(1)}, u32[]{:S(2)}, u32[]{:S(2)}) collective-permute-start(f32[8,4,64,64]{2,3,0,1:T(8,128)S(1)} %convolution_bitcast_fusion), channel_id=1, source_target_pairs={{0,1},{1,0},{2,3},{3,2},{4,5},{5,4},{6,7},{7,6},{8,9},{9,8},{10,11... | collective-permute-start | bytes 1572872 | tf_op jit(solution)/shard_map/ppermute | solution.py:109
  129.8 0.7 convolution_bitcast_fusion.1
  130.5 1.5 collective-permute-done.2
  132.6 0.7 reshape.137
  133.2 19.0 %all_to_all.20 = f32[32,1,4096]{2,1,0:T(1,128)S(1)} all-to-all(f32[32,1,4096]{2,1,0:T(1,128)S(1)} %reshape.137), channel_id=1, replica_groups=mesh['chi'=8,'clo'=8,'x'=4,'core'=2] {'clo','x'}, dimensions={0} | all-to-all | bytes 1048576 | tf_op jit(solution)/shard_map/all_to_all | solution.py:113
  152.2 0.5 broadcast.109
  152.7 1.9 %reduce = f32[32,4096]{1,0:T(8,128)S(1)} reduce(f32[32,1,4096]{2,1,0:T(1,128)S(1)} %all_to_all.20, f32[]{:T(128)} %broadcast.109), dimensions={1}, to_apply=%all_to_all.15.reduce_sub_computation | reduce | bytes 1048580 | tf_op jit(solution)/shard_map/all_to_all | solution.py:113
  155.2 0.8 reshape.132
  (46 shorter events, 3.7 us)
Async XLA Ops:
  6.5 7.1 %copy-start.3 = (bf16[3,64,1024]{2,1,0:T(8,128)(2,1)S(1)}, bf16[3,64,1024]{2,1,0:T(8,128)(2,1)}, u32[]{:S(2)}) copy-start(bf16[3,64,1024]{2,1,0:T(8,128)(2,1)} %param.7) | copy-start | bytes 1179652
  7.4 6.2 %collective-permute-start = (bf16[3,2,1024]{2,1,0:T(2,128)(2,1)S(1)}, bf16[3,2,1024]{2,1,0:T(2,128)(2,1)S(1)}, u32[]{:S(2)}, u32[]{:S(2)}) collective-permute-start(bf16[3,2,1024]{2,1,0:T(2,128)(2,1)S(1)} %slice.29), channel_id=1, source_target_pairs={{0,8},{8,16},{16,24},{24,32},{32,40},{40,48},{48,56},{56,64},{64,7... | collective-permute-start | bytes 36872 | tf_op jit(solution)/shard_map/ppermute | solution.py:15
  13.6 7.4 %copy-start = (f32[16,1024]{1,0:T(8,128)}, f32[16,1024]{1,0:T(8,128)S(1)}, u32[]{:S(2)}) copy-start(f32[16,1024]{1,0:T(8,128)S(1)} %neg.32) | copy-start | bytes 196612
  15.6 12.5 %all-to-all-start = ((f32[8,16,1024]{2,1,0:T(8,128)}), f32[8,16,1024]{2,1,0:T(8,128)S(1)}, u32[]{:S(2)}, u32[]{:S(2)}) async-start(f32[8,16,1024]{2,1,0:T(8,128)} %broadcast_in_dim.35), calls=%async_computation | async-start | bytes 1048576 | tf_op jit(solution)/shard_map/all_to_all | solution.py:75
  28.9 0.7 collective-permute-start.1
  30.4 20.4 %copy-start.2 = (bf16[64,4096]{1,0:T(8,128)(2,1)S(1)}, bf16[64,4096]{1,0:T(8,128)(2,1)}, u32[]{:S(2)}) copy-start(bf16[64,4096]{1,0:T(8,128)(2,1)} %constant.47.clone) | copy-start | bytes 1572868
  30.4 25.9 %all-to-all-start.1 = ((f32[8,16,1024]{2,1,0:T(8,128)}), f32[8,16,1024]{2,1,0:T(8,128)S(1)}, u32[]{:S(2)}, u32[]{:S(2)}) async-start(f32[8,16,1024]{2,1,0:T(8,128)} %broadcast_in_dim.36), calls=%async_computation.1 | async-start | bytes 1048576 | tf_op jit(solution)/shard_map/all_to_all | solution.py:93
  54.7 1.7 %copy-start.4 = (f32[16,1024]{1,0:T(8,128)S(1)}, f32[16,1024]{1,0:T(8,128)}, u32[]{:S(2)}) copy-start(f32[16,1024]{1,0:T(8,128)} %get-tuple-element.16) | copy-start | bytes 196612
  54.7 1.7 %copy-start.1 = (f32[16,1024]{1,0:T(8,128)S(1)}, f32[16,1024]{1,0:T(8,128)}, u32[]{:S(2)}) copy-start(f32[16,1024]{1,0:T(8,128)} %copy-done) | copy-start | bytes 196612
  54.7 1.7 %copy-start.5 = (f32[16,1024]{1,0:T(8,128)S(1)}, f32[16,1024]{1,0:T(8,128)}, u32[]{:S(2)}) copy-start(f32[16,1024]{1,0:T(8,128)} %mul.249) | copy-start | bytes 196612
  56.4 1.5 copy-start.6
  59.1 65.1 %all-to-all-start.2 = ((bf16[8,64,1024]{2,1,0:T(8,128)(2,1)}), bf16[8,64,1024]{2,1,0:T(8,128)(2,1)S(1)}, u32[]{:S(2)}, u32[]{:S(2)}) async-start(bf16[8,64,1024]{2,1,0:T(8,128)(2,1)} %broadcast_in_dim.38), calls=%async_computation.2 | async-start | bytes 2097152 | tf_op jit(solution)/shard_map/all_to_all | solution.py:102
  63.4 59.5 %all-gather.2.cloned.1.call-start = ((), (), s32[]{:S(2)}) async-start(), calls=%async_computation.4 | async-start | bytes 1179648 | tf_op jit(solution)/shard_map/all_gather | solution.py:31
  125.0 7.1 %collective-permute-start.2 = (f32[8,4,64,64]{2,3,0,1:T(8,128)S(1)}, f32[8,4,64,64]{2,3,0,1:T(8,128)S(1)}, u32[]{:S(2)}, u32[]{:S(2)}) collective-permute-start(f32[8,4,64,64]{2,3,0,1:T(8,128)S(1)} %convolution_bitcast_fusion), channel_id=1, source_target_pairs={{0,1},{1,0},{2,3},{3,2},{4,5},{5,4},{6,7},{7,6},{8,9},{9,8},{10,11... | collective-permute-start | bytes 1572872 | tf_op jit(solution)/shard_map/ppermute | solution.py:109
Sparse Core Ops, SparseCore 0:
  66.3 56.5 all-gather.1
